TPU v7x, 32 devices: a whole 2x2x4 slice. The times are simulated.
32 devices in a mesh: grp: 2 (over x), seq: 16 (over z, y, core).
Axes of the slice: x: 2, y: 2, z: 4, core: 2. Of those that a mesh axis runs over, the one named last changes fastest.
Arguments:
- tile_embeds: bfloat16 [16384, 1536], P(('grp', 'seq')), parts along dimension 0, may hold values from -6 to 6
- tile_pos: int32 [16384], P(('grp', 'seq')), parts along dimension 0, may hold values from 0 to 4095, as said below
- tile_count: int32 [32], P(('grp', 'seq')), parts along dimension 0, may hold values from 0 to 512, as said below
- slide_weight: bfloat16 [1536, 1536], replicated, may hold values from -0.15625 to 0.15625
- slide_bias: float32 [1536], replicated, may hold values from -3 to 3
- norm_gain: float32 [1536], replicated, may hold values from 0.5 to 1.5
- in_weight: bfloat16 [1536, 3328], replicated, may hold values from -0.15625 to 0.15625
- dt_weight: bfloat16 [1536, 24], replicated, may hold values from -0.15625 to 0.15625
- conv_weight: float32 [2, 4, 1792], replicated, may hold values from -0.6 to 0.6
- conv_bias: float32 [2, 1792], replicated, may hold values from -0.5 to 0.1
- dt_bias: float32 [2, 24], replicated, may hold values from -10.5 to -4
- a_log: float32 [2, 24], replicated, may hold values from 0 to 1.5
- out_gain: float32 [1536], replicated, may hold values from 0.5 to 1.5
- out_weight: bfloat16 [1536, 1536], replicated, may hold values from -0.15625 to 0.15625
Outputs:
- hidden: bfloat16 [8192, 1536], P(('grp', 'seq')), parts along dimension 0
There are 2 independent parts, one for each index of `grp`. A program takes and returns all parts, laid end to end along the dimension named above; an argument that names none is the same for every part. Nothing has to cross between parts.
Inputs may be any that keep to these rules, and one draw needn't show every extreme that they name: The live slots of all readers together hold every slide position exactly once; the position's owner is tile_pos // 256. A reader with live slots holds the same number for every owner, at most 32, and 32 is reached in every draw. Slots beyond a reader's count hold arbitrary positions. `tile_count`: A quarter of the readers hold 512 live tiles, half of them 256, the rest none; which readers is drawn.
All inputs are finite; a program needn't handle non-finite values.
Results may differ from a plain program's by a relative error of at most 0.009.
Values may be sent and summed in bfloat16 or wider, within the bound.
No kernel may reach another device: no remote copies, remote signals or barrier semaphores. Data moves between devices by JAX's collectives and lax.ppermute only.
A program may use at most 192 MiB of HBM per device.

v0:
```python
import jax
import jax.numpy as jnp
from jax import lax
from jax.sharding import PartitionSpec as P

E = 1536
HEAD_DIM = 64
NS = 128
KERNEL = 4
HEADS = 24


precise = lax.Precision.HIGHEST
epsilon = 1e-05


def rms_scale(values, scale_gain):
    mean_sq = jnp.mean(values * values, axis=-1, keepdims=True)
    return values * lax.rsqrt(mean_sq + epsilon) * scale_gain


def route_tiles(tile_embeds, tile_pos, tile_count, devices, rows):
    slots, width = tile_embeds.shape
    capacity = slots // devices
    is_live = jnp.arange(slots, dtype=jnp.int32) < tile_count[0]
    owners = jnp.where(is_live, tile_pos // rows, devices)
    one_hot = (owners[:, None] == jnp.arange(devices, dtype=jnp.int32)[None, :]).astype(jnp.int32)
    ranking = jnp.sum(jnp.cumsum(one_hot, axis=0) * one_hot, axis=1) - 1
    target = jnp.where(is_live, owners * capacity + ranking, -1)
    match = target[None, :] == jnp.arange(devices * capacity, dtype=jnp.int32)[:, None]
    send = jnp.dot(match.astype(jnp.bfloat16), tile_embeds, preferred_element_type=jnp.float32)
    send = send.astype(jnp.bfloat16).reshape(devices, capacity, width)
    send_rows = jnp.sum(jnp.where(match, (tile_pos % rows + 1)[None, :], 0), axis=1) - 1
    arrived = lax.all_to_all(send, "seq", 0, 0, tiled=True).reshape(devices * capacity, width)
    arrived_rows = lax.all_to_all(
        send_rows.reshape(devices, capacity), "seq", 0, 0, tiled=True
    ).reshape(devices * capacity)
    place = arrived_rows[None, :] == jnp.arange(rows, dtype=jnp.int32)[:, None]
    tiles = jnp.dot(place.astype(jnp.bfloat16), arrived, preferred_element_type=jnp.float32)
    return tiles.astype(jnp.bfloat16)


def halo(shard, width):
    size = lax.axis_size("seq")
    up = [(i, i + 1) for i in range(size - 1)]
    down = [(i + 1, i) for i in range(size - 1)]
    before = lax.ppermute(shard[-width:], "seq", up)
    after = lax.ppermute(shard[:width], "seq", down)
    return jnp.concatenate([before, shard, after], axis=0)


def local_terms(activated, step_size, decay_rate, backward):
    rows = activated.shape[0]
    signal = activated[:, :E].reshape(rows, HEADS, HEAD_DIM)
    write_map = activated[:, E : E + NS]
    read_map = activated[:, E + NS :]
    log_step = step_size * decay_rate
    log_decay = lax.cumsum(log_step, axis=0, reverse=backward)
    positions = jnp.arange(rows)
    if backward:
        mask = positions[:, None] <= positions[None, :]
        edge = log_decay[0]
    else:
        mask = positions[:, None] >= positions[None, :]
        edge = log_decay[-1]
    turned = log_decay.T
    gaps = turned[:, :, None] - turned[:, None, :]
    weights = jnp.exp(jnp.where(mask[None], gaps, -1e30))
    scores = jnp.dot(read_map, write_map.T, precision=precise)
    mixing = scores[None] * weights * step_size.T[:, None, :]
    within = jnp.einsum("hts,shp->thp", mixing, signal, precision=precise)
    tail_weight = jnp.exp(edge[None, :] - log_decay) * step_size
    own_state = jnp.einsum(
        "shp,sn->hpn", tail_weight[:, :, None] * signal, write_map, precision=precise
    )
    return within, own_state, jnp.exp(edge), jnp.exp(log_decay), read_map


def exchange(decay, state, backward):
    size, me = lax.axis_size("seq"), lax.axis_index("seq")
    done_decay = jnp.ones_like(decay)
    done_state = jnp.zeros_like(state)
    run_decay, run_state = decay, state
    shift = 1
    while shift < size:
        if backward:
            pairs = [(i + shift, i) for i in range(size - shift)]
            valid = me + shift < size
        else:
            pairs = [(i, i + shift) for i in range(size - shift)]
            valid = me >= shift
        got_state = lax.ppermute(run_state.astype(jnp.bfloat16), "seq", pairs).astype(jnp.float32)
        got_decay = jnp.where(valid, lax.ppermute(run_decay, "seq", pairs), 1.0)
        done_state = done_decay[:, None, None] * got_state + done_state
        done_decay = got_decay * done_decay
        if 2 * shift < size:
            run_state = run_decay[:, None, None] * got_state + run_state
            run_decay = got_decay * run_decay
        shift *= 2
    return done_state


def per_device(
    tile_embeds,
    tile_pos,
    tile_count,
    slide_weight,
    slide_bias,
    norm_gain,
    in_weight,
    dt_weight,
    conv_weight,
    conv_bias,
    dt_bias,
    a_log,
    out_gain,
    out_weight,
):
    devices = lax.axis_size("seq")
    rows = tile_embeds.shape[0] // 2
    tiles = route_tiles(tile_embeds, tile_pos, tile_count, devices, rows)
    embedded = (
        jnp.dot(tiles, slide_weight, preferred_element_type=jnp.float32) + slide_bias
    ).astype(jnp.bfloat16)
    normed = rms_scale(embedded.astype(jnp.float32), norm_gain).astype(jnp.bfloat16)
    projected = jnp.dot(normed, in_weight, preferred_element_type=jnp.float32).astype(jnp.bfloat16)
    dt_raw = jnp.dot(normed, dt_weight, preferred_element_type=jnp.float32)
    gate_part = projected[:, :E].astype(jnp.float32)
    conv_input = projected[:, E:]
    padded = halo(conv_input, KERNEL - 1).astype(jnp.float32)
    parts = []
    for direction in range(2):
        summed = conv_bias[direction] + jnp.zeros((rows, conv_input.shape[1]), jnp.float32)
        for offset in range(KERNEL):
            first = offset if direction == 0 else 2 * (KERNEL - 1) - offset
            summed = summed + conv_weight[direction, offset] * padded[first : first + rows]
        activated = jax.nn.silu(summed)
        step_size = jax.nn.softplus(dt_raw + dt_bias[direction])
        decay_rate = -jnp.exp(a_log[direction])
        parts.append(local_terms(activated, step_size, decay_rate, direction == 1))
    total = jnp.zeros((rows, E), jnp.float32)
    for direction in range(2):
        within, own_state, device_decay, decay_to, read_map = parts[direction]
        incoming = exchange(device_decay, own_state, direction == 1)
        carried = (
            jnp.einsum("tn,hpn->thp", read_map, incoming, precision=precise)
            * decay_to[:, :, None]
        )
        total = total + (within + carried).reshape(rows, E)
    gated = total * jax.nn.silu(gate_part)
    mixed = rms_scale(gated, out_gain).astype(jnp.bfloat16)
    hidden = embedded.astype(jnp.float32) + jnp.dot(
        mixed, out_weight, preferred_element_type=jnp.float32
    )
    return hidden.astype(jnp.bfloat16)


def solution(mesh):
    return jax.shard_map(
        per_device,
        mesh=mesh,
        in_specs=(
            P(("grp", "seq"), None),
            P(("grp", "seq")),
            P(("grp", "seq")),
            P(),
            P(),
            P(),
            P(),
            P(),
            P(),
            P(),
            P(),
            P(),
            P(),
            P(),
        ),
        out_specs=P(("grp", "seq"), None),
        check_vma=False,
    )
```

profile of v0, /device:TPU:0, one launch (start us, length us, event | category | flops | bytes accessed | tf_op | source)
XLA Modules:
  0.0 204.2 jit_solution(17389208350641054142)
XLA Ops:
  3.9 7.4 %all-to-all-start = ((s32[16,1,32]{2,1,0:T(1,128)}), s32[16,1,32]{2,1,0:T(1,128)S(1)}, u32[]{:S(2)}, u32[]{:S(2)}) async-start(s32[16,1,32]{2,1,0:T(1,128)} %sub.59), calls=%async_computation | async-start | bytes 16384 | tf_op jit(solution)/shard_map/all_to_all | solution.py:35
  13.5 4.2 %all-to-all-done = s32[16,1,32]{2,1,0:T(1,128)S(1)} async-done(((s32[16,1,32]{2,1,0:T(1,128)}), s32[16,1,32]{2,1,0:T(1,128)S(1)}, u32[]{:S(2)}, u32[]{:S(2)}) %all-to-all-start) | async-done | bytes 2080 | tf_op jit(solution)/shard_map/all_to_all | solution.py:35
  17.7 3.7 %all-to-all-start.1 = ((bf16[16,32,1536]{2,1,0:T(8,128)(2,1)}), bf16[16,32,1536]{2,1,0:T(8,128)(2,1)S(1)}, u32[]{:S(2)}, u32[]{:S(2)}) async-start(bf16[16,32,1536]{2,1,0:T(8,128)(2,1)} %bitcast.144), calls=%async_computation.1 | async-start | bytes 3145728 | tf_op jit(solution)/shard_map/all_to_all | solution.py:34
  23.0 30.1 %all-to-all-done.1 = bf16[16,32,1536]{2,1,0:T(8,128)(2,1)S(1)} async-done(((bf16[16,32,1536]{2,1,0:T(8,128)(2,1)}), bf16[16,32,1536]{2,1,0:T(8,128)(2,1)S(1)}, u32[]{:S(2)}, u32[]{:S(2)}) %all-to-all-start.1) | async-done | bytes 1572896 | tf_op jit(solution)/shard_map/all_to_all | solution.py:34
  54.3 4.7 %multiply_reduce_fusion.1 = (f32[256]{0:T(256)S(1)}, f32[256,1536]{1,0:T(8,128)S(1)}) fusion(f32[1536]{0:T(1024)S(1)} %copy-done.38, bf16[1536,1536]{1,0:T(8,128)(2,1)} %param.17, bf16[512,1536]{1,0:T(8,128)(2,1)} %bitcast.143, s32[512]{0:T(512)S(1)} %eq.63), kind=kOutput, calls=%fused_computation.64 | convolution fusion | flops 1613102848 | bytes 7873536 | tf_op jit(solution)/shard_map/dot_general | solution.py:123
  65.6 6.8 %convolution_convert_fusion = bf16[256,3328]{1,0:T(8,128)(2,1)S(1)} fusion(bf16[1536,3328]{1,0:T(8,128)(2,1)} %param.20, f32[256,1536]{1,0:T(8,128)S(1)} %get-tuple-element.48, f32[1536]{0:T(1024)} %param.19, f32[256]{0:T(256)} %copy-done.27), kind=kOutput, calls=%fused_computation.12 | convolution fusion | flops 2619277312 | bytes 13507584 | tf_op jit(solution)/shard_map/dot_general | solution.py:126
  72.6 2.9 %collective-permute-start.2 = (f32[24]{0:T(128)S(1)}, f32[24]{0:T(128)S(1)}, u32[]{:S(2)}, u32[]{:S(2)}) collective-permute-start(f32[24]{0:T(128)S(1)} %exp.70), channel_id=1, source_target_pairs={{0,1},{1,2},{2,3},{3,4},{4,5},{5,6},{6,7},{7,8},{8,9},{9,10},{10,1... | collective-permute-start | bytes 296 | tf_op jit(solution)/shard_map/ppermute | solution.py:93
  76.7 4.4 %collective-permute-start = (bf16[3,1792]{1,0:T(4,128)(2,1)S(1)}, bf16[3,1792]{1,0:T(4,128)(2,1)S(1)}, u32[]{:S(2)}, u32[]{:S(2)}) collective-permute-start(bf16[3,1792]{1,0:T(4,128)(2,1)S(1)} %get-tuple-element.29), channel_id=1, source_target_pairs={{0,1},{1,2},{2,3},{3,4},{4,5},{5,6},{6,7},{7,8},{8,9},{9,10},{10,1... | collective-permute-start | bytes 32264 | tf_op jit(solution)/shard_map/ppermute | solution.py:47
  82.4 6.1 %collective-permute-start.3 = (f32[24]{0:T(128)S(1)}, f32[24]{0:T(128)S(1)}, u32[]{:S(2)}, u32[]{:S(2)}) collective-permute-start(f32[24]{0:T(128)S(1)} %get-tuple-element.21), channel_id=1, source_target_pairs={{0,2},{1,3},{2,4},{3,5},{4,6},{5,7},{6,8},{7,9},{8,10},{9,11},{10,... | collective-permute-start | bytes 296 | tf_op jit(solution)/shard_map/ppermute | solution.py:93
  89.9 9.1 %collective-permute-start.4 = (f32[24]{0:T(128)S(1)}, f32[24]{0:T(128)S(1)}, u32[]{:S(2)}, u32[]{:S(2)}) collective-permute-start(f32[24]{0:T(128)S(1)} %fusion.111), channel_id=1, source_target_pairs={{0,4},{1,5},{2,6},{3,7},{4,8},{5,9},{6,10},{7,11},{8,12},{9,13},{1... | collective-permute-start | bytes 296 | tf_op jit(solution)/shard_map/ppermute | solution.py:93
  101.0 4.7 %collective-permute-done.11 = f32[24]{0:T(128)S(1)} collective-permute-done((f32[24]{0:T(128)S(1)}, f32[24]{0:T(128)S(1)}, u32[]{:S(2)}, u32[]{:S(2)}) %collective-permute-start.11) | collective-permute-done | bytes 128 | tf_op jit(solution)/shard_map/ppermute | solution.py:93
  106.5 3.3 %divide_multiply_fusion.1 = (f32[256,1792]{1,0:T(8,128)S(1)}, f32[256,1792]{1,0:T(8,128)}) fusion(f32[262,1792]{1,0:T(8,128)S(1)} %maximum_convert_fusion, f32[1792]{0:T(1024)S(1)} %get-tuple-element.8, f32[1792]{0:T(1024)S(1)} %get-tuple-element.9, f32[1792]{0:T(1024)S(1)} %get-tuple-element.10, f32[1792]{0:T(1024)S(1)} %get-tuple-element.5, ...), kind=kLoop, calls=%fused_computation.49 | loop fusion | flops 11010048 | bytes 16586752 | tf_op jit(solution)/shard_map/jit(silu)/mul | solution.py:137
  112.9 2.9 %fusion.125 = (bf16[24,64,128]{2,1,0:T(8,128)(2,1)S(1)}, f32[24,64,128]{2,1,0:T(8,128)S(1)}) fusion(f32[256,1792]{1,0:T(8,128)} %copy-done.2, f32[256,24,64]{0,2,1:T(8,128)} %bitcast.140, f32[256,24]{0,1:T(8,128)S(1)} %get-tuple-element.32), kind=kOutput, calls=%fused_computation.219 | convolution fusion | flops 604569600 | bytes 2908160 | tf_op jit(solution)/shard_map/shp,sn->hpn/dot_general | solution.py:73
  118.7 3.1 %copy.36 = f32[256,1536]{0,1:T(8,128)} copy(f32[256,1536]{1,0:T(8,128)} %slice.175) | data formatting | bytes 3145728 | tf_op jit(solution)/shard_map/slice | solution.py:54
  121.7 2.8 %fusion.126 = (bf16[24,64,128]{2,1,0:T(8,128)(2,1)S(1)}, f32[24,64,128]{2,1,0:T(8,128)S(1)}) fusion(f32[256,1792]{1,0:T(8,128)} %get-tuple-element.28, f32[256,24,64]{0,2,1:T(8,128)} %bitcast.138, f32[256,24]{0,1:T(8,128)S(1)} %get-tuple-element.33), kind=kOutput, calls=%fused_computation.220 | convolution fusion | flops 604569600 | bytes 2908160 | tf_op jit(solution)/shard_map/shp,sn->hpn/dot_general | solution.py:73
  127.6 5.9 %collective-permute-start.6 = (bf16[24,64,128]{2,1,0:T(8,128)(2,1)S(1)}, bf16[24,64,128]{2,1,0:T(8,128)(2,1)S(1)}, u32[]{:S(2)}, u32[]{:S(2)}) collective-permute-start(bf16[24,64,128]{2,1,0:T(8,128)(2,1)S(1)} %fusion.119), channel_id=1, source_target_pairs={{0,2},{1,3},{2,4},{3,5},{4,6},{5,7},{6,8},{7,9},{8,10},{9,11},{10,... | collective-permute-start | bytes 1179656 | tf_op jit(solution)/shard_map/ppermute | solution.py:92
  135.0 7.1 %fusion.6 = f32[24,64,256]{2,1,0:T(8,128)S(1)} fusion(f32[256,24,64]{0,2,1:T(8,128)S(1)} %bitcast.141, f32[24,256]{1,0:T(8,128)S(1)} %copy-done.13, f32[24,256]{1,0:T(8,128)S(1)} %copy-done.11, f32[256,256]{1,0:T(8,128)S(1)} %fusion.88, pred[256,256]{1,0:T(8,128)(4,1)S(1)} %iota_compare_fusion.6), kind=kOutput, calls=%fused_computation.6 | convolution fusion | flops 1214251008 | bytes 3522560 | tf_op jit(solution)/shard_map/hts,shp->thp/dot_general | solution.py:71
  142.1 11.4 %collective-permute-done.6 = bf16[24,64,128]{2,1,0:T(8,128)(2,1)S(1)} collective-permute-done((bf16[24,64,128]{2,1,0:T(8,128)(2,1)S(1)}, bf16[24,64,128]{2,1,0:T(8,128)(2,1)S(1)}, u32[]{:S(2)}, u32[]{:S(2)}) %collective-permute-start.6) | collective-permute-done | bytes 393248 | tf_op jit(solution)/shard_map/ppermute | solution.py:92
  158.0 5.1 %collective-permute-done.7 = bf16[24,64,128]{2,1,0:T(8,128)(2,1)S(1)} collective-permute-done((bf16[24,64,128]{2,1,0:T(8,128)(2,1)S(1)}, bf16[24,64,128]{2,1,0:T(8,128)(2,1)S(1)}, u32[]{:S(2)}, u32[]{:S(2)}) %collective-permute-start.7) | collective-permute-done | bytes 393248 | tf_op jit(solution)/shard_map/ppermute | solution.py:92
  163.5 6.9 %collective-permute-start.8 = (bf16[24,64,128]{2,1,0:T(8,128)(2,1)S(1)}, bf16[24,64,128]{2,1,0:T(8,128)(2,1)S(1)}, u32[]{:S(2)}, u32[]{:S(2)}) collective-permute-start(bf16[24,64,128]{2,1,0:T(8,128)(2,1)S(1)} %fusion.51), channel_id=1, source_target_pairs={{0,8},{1,9},{2,10},{3,11},{4,12},{5,13},{6,14},{7,15},{16,24},{17,... | collective-permute-start | bytes 1179656 | tf_op jit(solution)/shard_map/ppermute | solution.py:92
  172.4 7.1 %fusion = f32[24,64,256]{2,1,0:T(8,128)S(1)} fusion(f32[256,24,64]{0,2,1:T(8,128)S(1)} %bitcast.139, f32[24,256]{1,0:T(8,128)S(1)} %copy-done.12, f32[24,256]{1,0:T(8,128)S(1)} %get-tuple-element.36, f32[256,256]{1,0:T(8,128)S(1)} %fusion.83, pred[256,256]{1,0:T(8,128)(4,1)S(1)} %iota_compare_fusion.5), kind=kOutput, calls=%fused_computation | convolution fusion | flops 1214251008 | bytes 3522560 | tf_op jit(solution)/shard_map/hts,shp->thp/dot_general | solution.py:71
  181.9 9.7 %collective-permute-done.15 = bf16[24,64,128]{2,1,0:T(8,128)(2,1)S(1)} collective-permute-done((bf16[24,64,128]{2,1,0:T(8,128)(2,1)S(1)}, bf16[24,64,128]{2,1,0:T(8,128)(2,1)S(1)}, u32[]{:S(2)}, u32[]{:S(2)}) %collective-permute-start.15) | collective-permute-done | bytes 393248 | tf_op jit(solution)/shard_map/ppermute | solution.py:92
  191.7 3.7 %fusion.39 = f32[256,24,64]{0,2,1:T(8,128)} fusion(f32[24,64,256]{2,1,0:T(8,128)S(1)} %fusion, f32[24,64,256]{2,1,0:T(8,128)S(1)} %fusion.6, f32[256,24,64]{0,2,1:T(8,128)S(1)} %fusion.47, bf16[24,64,128]{2,1,0:T(8,128)(2,1)S(1)} %collective-permute-done.12, bf16[24,64,128]{2,1,0:T(8,128)(2,1)S(1)} %collective-permute-done.13, ...), kind=kOutput, calls=%fused_computation.55 | convolution fusion | flops 607911936 | bytes 8044832 | tf_op jit(solution)/shard_map/tn,hpn->thp/dot_general | solution.py:146
  199.1 5.1 %fusion.26 = bf16[256,1536]{1,0:T(8,128)(2,1)} fusion(f32[256,1536]{1,0:T(8,128)S(1)} %copy-done.7, bf16[1536,1536]{1,0:T(8,128)(2,1)} %param.27, f32[1536]{0:T(1024)S(1)} %copy-done.39, f32[256]{0:T(256)S(1)} %add_rsqrt_fusion, f32[256,1536]{1,0:T(8,128)S(1)} %copy.39, bf16[256,3328]{1,0:T(8,128)(2,1)} %copy-done.5), kind=kOutput, calls=%fused_computation.30 | convolution fusion | flops 1212284928 | bytes 9444352 | tf_op jit(solution)/shard_map/dot_general | solution.py:152
  (166 shorter events, 44.2 us)
Async XLA Ops:
  3.9 13.8 %all-to-all-start = ((s32[16,1,32]{2,1,0:T(1,128)}), s32[16,1,32]{2,1,0:T(1,128)S(1)}, u32[]{:S(2)}, u32[]{:S(2)}) async-start(s32[16,1,32]{2,1,0:T(1,128)} %sub.59), calls=%async_computation | async-start | bytes 16384 | tf_op jit(solution)/shard_map/all_to_all | solution.py:35
  13.5 40.9 %copy-start.38 = (f32[1536]{0:T(1024)S(1)}, f32[1536]{0:T(1024)}, u32[]{:S(2)}) copy-start(f32[1536]{0:T(1024)} %param.18) | copy-start | bytes 18436
  17.7 35.5 %all-to-all-start.1 = ((bf16[16,32,1536]{2,1,0:T(8,128)(2,1)}), bf16[16,32,1536]{2,1,0:T(8,128)(2,1)S(1)}, u32[]{:S(2)}, u32[]{:S(2)}) async-start(bf16[16,32,1536]{2,1,0:T(8,128)(2,1)} %bitcast.144), calls=%async_computation.1 | async-start | bytes 3145728 | tf_op jit(solution)/shard_map/all_to_all | solution.py:34
  21.7 37.8 %copy-start.21 = (f32[24]{0:T(128)}, f32[24]{0:T(128)S(1)}, u32[]{:S(2)}) copy-start(f32[24]{0:T(128)S(1)} %get-tuple-element.43) | copy-start | bytes 292
  21.7 37.8 %copy-start.22 = (f32[24]{0:T(128)}, f32[24]{0:T(128)S(1)}, u32[]{:S(2)}) copy-start(f32[24]{0:T(128)S(1)} %get-tuple-element.44) | copy-start | bytes 292
  72.4 34.0 %copy-start.5 = (bf16[256,3328]{1,0:T(8,128)(2,1)}, bf16[256,3328]{1,0:T(8,128)(2,1)S(1)}, u32[]{:S(2)}) copy-start(bf16[256,3328]{1,0:T(8,128)(2,1)S(1)} %convolution_convert_fusion) | copy-start | bytes 5111812
  72.6 9.9 %collective-permute-start.2 = (f32[24]{0:T(128)S(1)}, f32[24]{0:T(128)S(1)}, u32[]{:S(2)}, u32[]{:S(2)}) collective-permute-start(f32[24]{0:T(128)S(1)} %exp.70), channel_id=1, source_target_pairs={{0,1},{1,2},{2,3},{3,4},{4,5},{5,6},{6,7},{7,8},{8,9},{9,10},{10,1... | collective-permute-start | bytes 296 | tf_op jit(solution)/shard_map/ppermute | solution.py:93
  75.4 13.1 %collective-permute-start.9 = (f32[24]{0:T(128)S(1)}, f32[24]{0:T(128)S(1)}, u32[]{:S(2)}, u32[]{:S(2)}) collective-permute-start(f32[24]{0:T(128)S(1)} %exp.78), channel_id=1, source_target_pairs={{1,0},{2,1},{3,2},{4,3},{5,4},{6,5},{7,6},{8,7},{9,8},{10,9},{11,1... | collective-permute-start | bytes 296 | tf_op jit(solution)/shard_map/ppermute | solution.py:93
  76.7 29.5 %collective-permute-start = (bf16[3,1792]{1,0:T(4,128)(2,1)S(1)}, bf16[3,1792]{1,0:T(4,128)(2,1)S(1)}, u32[]{:S(2)}, u32[]{:S(2)}) collective-permute-start(bf16[3,1792]{1,0:T(4,128)(2,1)S(1)} %get-tuple-element.29), channel_id=1, source_target_pairs={{0,1},{1,2},{2,3},{3,4},{4,5},{5,6},{6,7},{7,8},{8,9},{9,10},{10,1... | collective-permute-start | bytes 32264 | tf_op jit(solution)/shard_map/ppermute | solution.py:47
  81.1 25.2 %collective-permute-start.1 = (bf16[3,1792]{1,0:T(4,128)(2,1)S(1)}, bf16[3,1792]{1,0:T(4,128)(2,1)S(1)}, u32[]{:S(2)}, u32[]{:S(2)}) collective-permute-start(bf16[3,1792]{1,0:T(4,128)(2,1)S(1)} %get-tuple-element.30), channel_id=1, source_target_pairs={{1,0},{2,1},{3,2},{4,3},{5,4},{6,5},{7,6},{8,7},{9,8},{10,9},{11,1... | collective-permute-start | bytes 32264 | tf_op jit(solution)/shard_map/ppermute | solution.py:48
  82.4 23.8 %copy-start.25 = (f32[24]{0:T(128)}, f32[24]{0:T(128)S(1)}, u32[]{:S(2)}) copy-start(f32[24]{0:T(128)S(1)} %get-tuple-element.22) | copy-start | bytes 292
  82.4 7.5 %collective-permute-start.3 = (f32[24]{0:T(128)S(1)}, f32[24]{0:T(128)S(1)}, u32[]{:S(2)}, u32[]{:S(2)}) collective-permute-start(f32[24]{0:T(128)S(1)} %get-tuple-element.21), channel_id=1, source_target_pairs={{0,2},{1,3},{2,4},{3,5},{4,6},{5,7},{6,8},{7,9},{8,10},{9,11},{10,... | collective-permute-start | bytes 296 | tf_op jit(solution)/shard_map/ppermute | solution.py:93
  88.6 10.5 %collective-permute-start.10 = (f32[24]{0:T(128)S(1)}, f32[24]{0:T(128)S(1)}, u32[]{:S(2)}, u32[]{:S(2)}) collective-permute-start(f32[24]{0:T(128)S(1)} %get-tuple-element.17), channel_id=1, source_target_pairs={{2,0},{3,1},{4,2},{5,3},{6,4},{7,5},{8,6},{9,7},{10,8},{11,9},{12,... | collective-permute-start | bytes 296 | tf_op jit(solution)/shard_map/ppermute | solution.py:93
  89.9 10.5 %collective-permute-start.4 = (f32[24]{0:T(128)S(1)}, f32[24]{0:T(128)S(1)}, u32[]{:S(2)}, u32[]{:S(2)}) collective-permute-start(f32[24]{0:T(128)S(1)} %fusion.111), channel_id=1, source_target_pairs={{0,4},{1,5},{2,6},{3,7},{4,8},{5,9},{6,10},{7,11},{8,12},{9,13},{1... | collective-permute-start | bytes 296 | tf_op jit(solution)/shard_map/ppermute | solution.py:93
  99.1 6.6 %collective-permute-start.11 = (f32[24]{0:T(128)S(1)}, f32[24]{0:T(128)S(1)}, u32[]{:S(2)}, u32[]{:S(2)}) collective-permute-start(f32[24]{0:T(128)S(1)} %fusion.113), channel_id=1, source_target_pairs={{4,0},{5,1},{6,2},{7,3},{8,4},{9,5},{10,6},{11,7},{12,8},{13,9},{1... | collective-permute-start | bytes 296 | tf_op jit(solution)/shard_map/ppermute | solution.py:93
  115.8 11.6 %collective-permute-start.5 = (bf16[24,64,128]{2,1,0:T(8,128)(2,1)S(1)}, bf16[24,64,128]{2,1,0:T(8,128)(2,1)S(1)}, u32[]{:S(2)}, u32[]{:S(2)}) collective-permute-start(bf16[24,64,128]{2,1,0:T(8,128)(2,1)S(1)} %get-tuple-element.49), channel_id=1, source_target_pairs={{0,1},{1,2},{2,3},{3,4},{4,5},{5,6},{6,7},{7,8},{8,9},{9,10},{10,1... | collective-permute-start | bytes 1179656 | tf_op jit(solution)/shard_map/ppermute | solution.py:92
  124.6 8.9 %collective-permute-start.12 = (bf16[24,64,128]{2,1,0:T(8,128)(2,1)S(1)}, bf16[24,64,128]{2,1,0:T(8,128)(2,1)S(1)}, u32[]{:S(2)}, u32[]{:S(2)}) collective-permute-start(bf16[24,64,128]{2,1,0:T(8,128)(2,1)S(1)} %get-tuple-element.51), channel_id=1, source_target_pairs={{1,0},{2,1},{3,2},{4,3},{5,4},{6,5},{7,6},{8,7},{9,8},{10,9},{11,1... | collective-permute-start | bytes 1179656 | tf_op jit(solution)/shard_map/ppermute | solution.py:92
  127.6 25.9 %collective-permute-start.6 = (bf16[24,64,128]{2,1,0:T(8,128)(2,1)S(1)}, bf16[24,64,128]{2,1,0:T(8,128)(2,1)S(1)}, u32[]{:S(2)}, u32[]{:S(2)}) collective-permute-start(bf16[24,64,128]{2,1,0:T(8,128)(2,1)S(1)} %fusion.119), channel_id=1, source_target_pairs={{0,2},{1,3},{2,4},{3,5},{4,6},{5,7},{6,8},{7,9},{8,10},{9,11},{10,... | collective-permute-start | bytes 1179656 | tf_op jit(solution)/shard_map/ppermute | solution.py:92
  133.7 21.4 %collective-permute-start.13 = (bf16[24,64,128]{2,1,0:T(8,128)(2,1)S(1)}, bf16[24,64,128]{2,1,0:T(8,128)(2,1)S(1)}, u32[]{:S(2)}, u32[]{:S(2)}) collective-permute-start(bf16[24,64,128]{2,1,0:T(8,128)(2,1)S(1)} %fusion.118), channel_id=1, source_target_pairs={{2,0},{3,1},{4,2},{5,3},{6,4},{7,5},{8,6},{9,7},{10,8},{11,9},{12,... | collective-permute-start | bytes 1179656 | tf_op jit(solution)/shard_map/ppermute | solution.py:92
  142.1 21.1 %copy-start.35 = (f32[24]{0:T(128)S(1)}, f32[24]{0:T(128)}, u32[]{:S(2)}) copy-start(f32[24]{0:T(128)} %copy-done.34) | copy-start | bytes 292
  153.7 9.4 %collective-permute-start.7 = (bf16[24,64,128]{2,1,0:T(8,128)(2,1)S(1)}, bf16[24,64,128]{2,1,0:T(8,128)(2,1)S(1)}, u32[]{:S(2)}, u32[]{:S(2)}) collective-permute-start(bf16[24,64,128]{2,1,0:T(8,128)(2,1)S(1)} %fusion.69), channel_id=1, source_target_pairs={{0,4},{1,5},{2,6},{3,7},{4,8},{5,9},{6,10},{7,11},{8,12},{9,13},{1... | collective-permute-start | bytes 1179656 | tf_op jit(solution)/shard_map/ppermute | solution.py:92
  155.4 15.1 %collective-permute-start.14 = (bf16[24,64,128]{2,1,0:T(8,128)(2,1)S(1)}, bf16[24,64,128]{2,1,0:T(8,128)(2,1)S(1)}, u32[]{:S(2)}, u32[]{:S(2)}) collective-permute-start(bf16[24,64,128]{2,1,0:T(8,128)(2,1)S(1)} %fusion.68), channel_id=1, source_target_pairs={{4,0},{5,1},{6,2},{7,3},{8,4},{9,5},{10,6},{11,7},{12,8},{13,9},{1... | collective-permute-start | bytes 1179656 | tf_op jit(solution)/shard_map/ppermute | solution.py:92
  163.5 16.0 %collective-permute-start.8 = (bf16[24,64,128]{2,1,0:T(8,128)(2,1)S(1)}, bf16[24,64,128]{2,1,0:T(8,128)(2,1)S(1)}, u32[]{:S(2)}, u32[]{:S(2)}) collective-permute-start(bf16[24,64,128]{2,1,0:T(8,128)(2,1)S(1)} %fusion.51), channel_id=1, source_target_pairs={{0,8},{1,9},{2,10},{3,11},{4,12},{5,13},{6,14},{7,15},{16,24},{17,... | collective-permute-start | bytes 1179656 | tf_op jit(solution)/shard_map/ppermute | solution.py:92
  170.9 20.8 %collective-permute-start.15 = (bf16[24,64,128]{2,1,0:T(8,128)(2,1)S(1)}, bf16[24,64,128]{2,1,0:T(8,128)(2,1)S(1)}, u32[]{:S(2)}, u32[]{:S(2)}) collective-permute-start(bf16[24,64,128]{2,1,0:T(8,128)(2,1)S(1)} %fusion.58), channel_id=1, source_target_pairs={{8,0},{9,1},{10,2},{11,3},{12,4},{13,5},{14,6},{15,7},{24,16},{25,... | collective-permute-start | bytes 1179656 | tf_op jit(solution)/shard_map/ppermute | solution.py:92
  (34 other events, 294.9 us)
where the time goes:
time: 205 us; the launch traced here: 204 us
  waiting for transfers between devices  65.3 us (32%)
  starting transfers between devices  59.9 us (29%)
  matrix products  47.8 us (23%)
  other arithmetic  16.5 us (8%)
  local copies, waits for them, and re-layouts  13 us (6%)
    all_to_all x1, waiting for transfers between devices, route_tiles(): lax.all_to_all(send, 'seq', 0, 0, tiled=True)  30.1 us
    ppermute x8, waiting for transfers between devices, exchange(): lax.ppermute(run_state.astype(jnp.bfloat16), 'seq', pairs)  26.2 us
    ppermute x6, starting transfers between devices, exchange(): got_decay = jnp.where(valid, lax.ppermute(run_decay, 'seq', pairs), 1.0)  22 us
    ppermute x8, starting transfers between devices, exchange(): lax.ppermute(run_state.astype(jnp.bfloat16), 'seq', pairs)  21.1 us
    dot_general x2, matrix products, local_terms(): within = jnp.einsum('hts,shp->thp', mixing, signal, precision=precise)  14.2 us
    all_to_all x1, starting transfers between devices, route_tiles(): lax.all_to_all(send_rows.reshape(devices, capacity), 'seq', 0, 0, tiled=T...  7.41 us
    dot_general x1, matrix products, per_device(): jnp.dot(normed, in_weight, preferred_element_type=jnp.float32)  6.79 us
    slice x4, local copies, waits for them, and re-layouts, local_terms(): signal = activated[:, :E].reshape(rows, HEADS, HEAD_DIM)  6.27 us
  transfers between devices with their start and end apart: 18, of which 6 were waited for; matrix products, arithmetic and copies ran while one was open for 16% of the time, Pallas kernels for 0%

commit v1 on v0

--- a/solution.py
+++ b/solution.py
@@ -28,15 +28,18 @@
     ranking = jnp.sum(jnp.cumsum(one_hot, axis=0) * one_hot, axis=1) - 1
     target = jnp.where(is_live, owners * capacity + ranking, -1)
     match = target[None, :] == jnp.arange(devices * capacity, dtype=jnp.int32)[:, None]
-    send = jnp.dot(match.astype(jnp.bfloat16), tile_embeds, preferred_element_type=jnp.float32)
-    send = send.astype(jnp.bfloat16).reshape(devices, capacity, width)
-    send_rows = jnp.sum(jnp.where(match, (tile_pos % rows + 1)[None, :], 0), axis=1) - 1
-    arrived = lax.all_to_all(send, "seq", 0, 0, tiled=True).reshape(devices * capacity, width)
-    arrived_rows = lax.all_to_all(
-        send_rows.reshape(devices, capacity), "seq", 0, 0, tiled=True
-    ).reshape(devices * capacity)
+    row_column = (tile_pos % rows + 1).astype(jnp.bfloat16)[:, None]
+    source = jnp.concatenate(
+        [tile_embeds, jnp.pad(row_column, ((0, 0), (0, 127)))], axis=1
+    )
+    send = jnp.dot(match.astype(jnp.bfloat16), source, preferred_element_type=jnp.float32)
+    send = send.astype(jnp.bfloat16).reshape(devices, capacity, width + 128)
+    arrived = lax.all_to_all(send, "seq", 0, 0, tiled=True).reshape(devices * capacity, width + 128)
+    arrived_rows = arrived[:, width].astype(jnp.float32).astype(jnp.int32) - 1
     place = arrived_rows[None, :] == jnp.arange(rows, dtype=jnp.int32)[:, None]
-    tiles = jnp.dot(place.astype(jnp.bfloat16), arrived, preferred_element_type=jnp.float32)
+    tiles = jnp.dot(
+        place.astype(jnp.bfloat16), arrived[:, :width], preferred_element_type=jnp.float32
+    )
     return tiles.astype(jnp.bfloat16)
 
 
@@ -76,28 +79,46 @@
     return within, own_state, jnp.exp(edge), jnp.exp(log_decay), read_map
 
 
-def exchange(decay, state, backward):
+def combine(earlier, later):
+    return (earlier[0] * later[0], later[0][:, None, None] * earlier[1] + later[1])
+
+
+def transfer(pair, pairs):
+    decay, state = pair
+    high = decay.astype(jnp.bfloat16)
+    low = (decay - high.astype(jnp.float32)).astype(jnp.bfloat16)
+    extra = jnp.stack([high, low])
+    extra = jnp.pad(extra, ((0, state.shape[1] - 2), (0, state.shape[2] - decay.shape[0])))
+    payload = jnp.concatenate([state.astype(jnp.bfloat16), extra[None]], axis=0)
+    got = lax.ppermute(payload, "seq", pairs)
+    heads = decay.shape[0]
+    got_decay = got[heads, 0, :heads].astype(jnp.float32) + got[heads, 1, :heads].astype(jnp.float32)
+    return got_decay, got[:heads].astype(jnp.float32)
+
+
+def exchange(forward, backward):
     size, me = lax.axis_size("seq"), lax.axis_index("seq")
-    done_decay = jnp.ones_like(decay)
-    done_state = jnp.zeros_like(state)
-    run_decay, run_state = decay, state
+    chips, chip, is_one = size // 2, me // 2, me % 2 == 1
+    swap = [(2 * k + d, 2 * k + 1 - d) for k in range(chips) for d in range(2)]
+    pick = lambda a, b: jax.tree.map(lambda x, y: jnp.where(is_one, x, y), a, b)
+    mine = pick(forward, backward)
+    first = transfer(pick(backward, forward), swap)
+    run = combine(first, mine)
+    done = (jnp.ones_like(mine[0]), jnp.zeros_like(mine[1]))
     shift = 1
-    while shift < size:
-        if backward:
-            pairs = [(i + shift, i) for i in range(size - shift)]
-            valid = me + shift < size
-        else:
-            pairs = [(i, i + shift) for i in range(size - shift)]
-            valid = me >= shift
-        got_state = lax.ppermute(run_state.astype(jnp.bfloat16), "seq", pairs).astype(jnp.float32)
-        got_decay = jnp.where(valid, lax.ppermute(run_decay, "seq", pairs), 1.0)
-        done_state = done_decay[:, None, None] * got_state + done_state
-        done_decay = got_decay * done_decay
-        if 2 * shift < size:
-            run_state = run_decay[:, None, None] * got_state + run_state
-            run_decay = got_decay * run_decay
+    while shift < chips:
+        pairs = [(2 * k + 1, 2 * (k + shift) + 1) for k in range(chips - shift)]
+        pairs += [(2 * (k + shift), 2 * k) for k in range(chips - shift)]
+        valid = jnp.where(is_one, chip >= shift, chip + shift < chips)
+        got_decay, got_state = transfer(run, pairs)
+        got = (jnp.where(valid, got_decay, 1.0), got_state)
+        done = combine(got, done)
+        if 2 * shift < chips:
+            run = combine(got, run)
         shift *= 2
-    return done_state
+    other = lax.ppermute(done[1].astype(jnp.bfloat16), "seq", swap).astype(jnp.float32)
+    mine_in = first[0][:, None, None] * done[1] + first[1]
+    return jnp.where(is_one, mine_in, other), jnp.where(is_one, other, mine_in)
 
 
 def per_device(
@@ -138,10 +159,13 @@
         step_size = jax.nn.softplus(dt_raw + dt_bias[direction])
         decay_rate = -jnp.exp(a_log[direction])
         parts.append(local_terms(activated, step_size, decay_rate, direction == 1))
+    incomings = exchange(
+        (parts[0][2], parts[0][1]), (parts[1][2], parts[1][1])
+    )
     total = jnp.zeros((rows, E), jnp.float32)
     for direction in range(2):
         within, own_state, device_decay, decay_to, read_map = parts[direction]
-        incoming = exchange(device_decay, own_state, direction == 1)
+        incoming = incomings[direction]
         carried = (
             jnp.einsum("tn,hpn->thp", read_map, incoming, precision=precise)
             * decay_to[:, :, None]

time: 205 us -> 159 us (0.78)
  starting transfers between devices: 59.9 us -> 18.7 us
  local copies, waits for them, and re-layouts: 13 us -> 22.3 us
  waiting for transfers between devices: 65.3 us -> 56.1 us
  other arithmetic: 16.5 us -> 14.2 us
    ppermute x14 -> x5, starting transfers between devices: 43.1 us -> 6.82 us  [the longest x4 6.75 us: transfer(): got = lax.ppermute(payload, 'seq', pairs)]
    ppermute x14 -> x5, waiting for transfers between devices: 31 us -> 20.3 us  [the longest x4 20.3 us: transfer(): got = lax.ppermute(payload, 'seq', pairs)]
    all_to_all x1 -> x0, starting transfers between devices: 7.41 us -> none  [route_tiles(): lax.all_to_all(send_rows.reshape(devices, capacity), 'seq', 0, 0, tiled=T...]
    all_to_all x1 -> x0, waiting for transfers between devices: 4.18 us -> none  [route_tiles(): lax.all_to_all(send_rows.reshape(devices, capacity), 'seq', 0, 0, tiled=T...]
    all_to_all x1, starting transfers between devices: 3.71 us -> 7.56 us  [route_tiles(): lax.all_to_all(send, 'seq', 0, 0, tiled=True)]
    all_to_all x1, waiting for transfers between devices: 30.1 us -> 33.9 us  [route_tiles(): lax.all_to_all(send, 'seq', 0, 0, tiled=True)]
    another operation x6 -> x11, local copies, waits for them, and re-layouts: 0.27 us -> 3.75 us  [the longest x4 3.35 us: local_terms(): log_decay = lax.cumsum(log_step, axis=0, reverse=backward)]
    select_n x0 -> x2, local copies, waits for them, and re-layouts: none -> 3.15 us  [per_device(): step_size = jax.nn.softplus(dt_raw + dt_bias[direction])]
  transfers between devices with their start and end apart: 18 -> 8, of which waited for: 6 -> 6; matrix products, arithmetic and copies ran while one was open for 16% -> 18% of each run, Pallas kernels for 0% -> 0%
where the time goes in v1:
time: 159 us
  waiting for transfers between devices  56.1 us (35%)
  matrix products  45.9 us (29%)
  local copies, waits for them, and re-layouts  22.3 us (14%)
  starting transfers between devices  18.7 us (12%)
  other arithmetic  14.2 us (9%)
    all_to_all x1, waiting for transfers between devices, route_tiles(): lax.all_to_all(send, 'seq', 0, 0, tiled=True)  33.9 us
    ppermute x4, waiting for transfers between devices, transfer(): got = lax.ppermute(payload, 'seq', pairs)  20.3 us
    dot_general x2, matrix products, local_terms(): within = jnp.einsum('hts,shp->thp', mixing, signal, precision=precise)  14.1 us
    slice x4, local copies, waits for them, and re-layouts, local_terms(): signal = activated[:, :E].reshape(rows, HEADS, HEAD_DIM)  7.91 us
    all_to_all x1, starting transfers between devices, route_tiles(): lax.all_to_all(send, 'seq', 0, 0, tiled=True)  7.56 us
    dot_general x1, matrix products, per_device(): jnp.dot(normed, in_weight, preferred_element_type=jnp.float32)  6.83 us
    ppermute x4, starting transfers between devices, transfer(): got = lax.ppermute(payload, 'seq', pairs)  6.75 us
    dot_general x2, matrix products, per_device(): jnp.einsum('tn,hpn->thp', read_map, incoming, precision=precise)  5.33 us
  transfers between devices with their start and end apart: 8, of which 6 were waited for; matrix products, arithmetic and copies ran while one was open for 18% of the time, Pallas kernels for 0%

profile of v1, /device:TPU:0, one launch (start us, length us, event | category | flops | bytes accessed | tf_op | source)
XLA Modules:
  0.0 158.6 jit_solution(1717761081222617738)
XLA Ops:
  3.1 3.7 %convolution_convert_fusion.1 = bf16[512,1664]{1,0:T(8,128)(2,1)} fusion(bf16[512,1]{1,0:T(8,128)(2,1)S(1)} %broadcast_in_dim.48, bf16[512,1536]{1,0:T(8,128)(2,1)} %param.14, s32[512]{0:T(512)S(1)} %add_select_fusion.2), kind=kOutput, calls=%fused_computation.27 | convolution fusion | flops 878641152 | bytes 3279872 | tf_op jit(solution)/shard_map/dot_general | solution.py:35
  6.8 7.6 %all-to-all-start = ((bf16[16,32,1664]{2,1,0:T(8,128)(2,1)}), bf16[16,32,1664]{2,1,0:T(8,128)(2,1)S(1)}, u32[]{:S(2)}, u32[]{:S(2)}) async-start(bf16[16,32,1664]{2,1,0:T(8,128)(2,1)} %bitcast.3), calls=%async_computation | async-start | bytes 3407872 | tf_op jit(solution)/shard_map/all_to_all | solution.py:37
  14.7 33.9 %all-to-all-done = bf16[16,32,1664]{2,1,0:T(8,128)(2,1)S(1)} async-done(((bf16[16,32,1664]{2,1,0:T(8,128)(2,1)}), bf16[16,32,1664]{2,1,0:T(8,128)(2,1)S(1)}, u32[]{:S(2)}, u32[]{:S(2)}) %all-to-all-start) | async-done | bytes 1703968 | tf_op jit(solution)/shard_map/all_to_all | solution.py:37
  48.7 4.2 %multiply_reduce_fusion.1 = (f32[256]{0:T(256)S(1)}, f32[256,1536]{1,0:T(8,128)S(1)}) fusion(f32[1536]{0:T(1024)S(1)} %copy-done.24, bf16[1536,1536]{1,0:T(8,128)(2,1)} %param.17, bf16[512,1664]{1,0:T(8,128)(2,1)S(1)} %bitcast.151, s32[512]{0:T(512)S(1)} %add_reduce_fusion), kind=kOutput, calls=%fused_computation.71 | convolution fusion | flops 1613102848 | bytes 7875584 | tf_op jit(solution)/shard_map/dot_general | solution.py:144
  55.2 2.5 %reduce-window.26 = f32[24,2,128]{2,0,1:T(8,128)S(1)} reduce-window(f32[24,2,128]{2,0,1:T(8,128)S(1)} %copy.95, f32[]{:T(128)} %constant.87.clone.1), window={size=1x1x128 pad=0_0x0_0x0_127}, to_apply=%region_6.7 | reduce-window | flops 780288 | bytes 49156 | tf_op jit(solution)/shard_map/reduce-window.4
  58.1 6.8 %convolution_convert_fusion = bf16[256,3328]{1,0:T(8,128)(2,1)S(1)} fusion(bf16[1536,3328]{1,0:T(8,128)(2,1)} %param.20, f32[256,1536]{1,0:T(8,128)S(1)} %get-tuple-element.53, f32[1536]{0:T(1024)S(1)} %copy-done.21, f32[256]{0:T(256)S(1)} %add_rsqrt_fusion.1), kind=kOutput, calls=%fused_computation.12 | convolution fusion | flops 2619277312 | bytes 13507584 | tf_op jit(solution)/shard_map/dot_general | solution.py:147
  65.0 2.9 %collective-permute-start = (bf16[3,1792]{1,0:T(4,128)(2,1)S(1)}, bf16[3,1792]{1,0:T(4,128)(2,1)S(1)}, u32[]{:S(2)}, u32[]{:S(2)}) collective-permute-start(bf16[3,1792]{1,0:T(4,128)(2,1)S(1)} %get-tuple-element.34), channel_id=1, source_target_pairs={{0,1},{1,2},{2,3},{3,4},{4,5},{5,6},{6,7},{7,8},{8,9},{9,10},{10,1... | collective-permute-start | bytes 32264 | tf_op jit(solution)/shard_map/ppermute | solution.py:50
  70.5 1.9 %collective-permute-done.1 = bf16[3,1792]{1,0:T(4,128)(2,1)S(1)} collective-permute-done((bf16[3,1792]{1,0:T(4,128)(2,1)S(1)}, bf16[3,1792]{1,0:T(4,128)(2,1)S(1)}, u32[]{:S(2)}, u32[]{:S(2)}) %collective-permute-start.1) | collective-permute-done | bytes 10784 | tf_op jit(solution)/shard_map/ppermute | solution.py:51
  72.7 2.3 %divide_multiply_fusion.1 = (f32[256,1792]{1,0:T(8,128)S(1)}, f32[256,1792]{1,0:T(8,128)S(1)}) fusion(f32[262,1792]{1,0:T(8,128)S(1)} %maximum_convert_fusion, f32[1792]{0:T(1024)S(1)} %get-tuple-element.8, f32[1792]{0:T(1024)S(1)} %get-tuple-element.9, f32[1792]{0:T(1024)S(1)} %get-tuple-element.10, f32[1792]{0:T(1024)S(1)} %get-tuple-element.5, ...), kind=kLoop, calls=%fused_computation.51 | loop fusion | flops 11010048 | bytes 16586752 | tf_op jit(solution)/shard_map/jit(silu)/mul | solution.py:158
  77.7 1.9 %copy.87 = f32[256,1536]{0,1:T(8,128)S(1)} copy(f32[256,1536]{1,0:T(8,128)} %slice.217) | data formatting | bytes 3145728 | tf_op jit(solution)/shard_map/slice | solution.py:57
  79.5 1.6 slice.226
  81.1 3.1 %copy.98 = f32[256,1536]{0,1:T(8,128)} copy(f32[256,1536]{1,0:T(8,128)} %slice.226) | data formatting | bytes 3145728 | tf_op jit(solution)/shard_map/slice | solution.py:57
  84.2 2.4 %fusion.47 = f32[24,64,128]{2,1,0:T(8,128)S(1)} fusion(f32[256,24,64]{0,2,1:T(8,128)S(1)} %bitcast.145, f32[256,24]{0,1:T(8,128)S(1)} %copy.99, f32[256,1792]{1,0:T(8,128)} %copy-done.1), kind=kOutput, calls=%fused_computation.66 | convolution fusion | flops 604372992 | bytes 2514944 | tf_op jit(solution)/shard_map/shp,sn->hpn/dot_general | solution.py:76
  88.1 2.5 %collective-permute-start.2 = (bf16[25,64,128]{2,1,0:T(8,128)(2,1)S(1)}, bf16[25,64,128]{2,1,0:T(8,128)(2,1)S(1)}, u32[]{:S(2)}, u32[]{:S(2)}) collective-permute-start(bf16[25,64,128]{2,1,0:T(8,128)(2,1)S(1)} %pad_maximum_fusion), channel_id=1, source_target_pairs={{0,1},{1,0},{2,3},{3,2},{4,5},{5,4},{6,7},{7,6},{8,9},{9,8},{10,11... | collective-permute-start | bytes 1228808 | tf_op jit(solution)/shard_map/ppermute | solution.py:93
  103.7 1.6 %copy.104 = f32[256,24]{0,1:T(8,128)} copy(f32[256,24]{1,0:T(8,128)} %get-tuple-element.39) | data formatting | bytes 49152 | tf_op jit(solution)/shard_map/exp | solution.py:79
  109.9 11.8 %collective-permute-done.4 = bf16[25,64,128]{2,1,0:T(8,128)(2,1)S(1)} collective-permute-done((bf16[25,64,128]{2,1,0:T(8,128)(2,1)S(1)}, bf16[25,64,128]{2,1,0:T(8,128)(2,1)S(1)}, u32[]{:S(2)}, u32[]{:S(2)}) %collective-permute-start.4) | collective-permute-done | bytes 409632 | tf_op jit(solution)/shard_map/ppermute | solution.py:93
  122.1 1.6 %collective-permute-start.5 = (bf16[25,64,128]{2,1,0:T(8,128)(2,1)S(1)}, bf16[25,64,128]{2,1,0:T(8,128)(2,1)S(1)}, u32[]{:S(2)}, u32[]{:S(2)}) collective-permute-start(bf16[25,64,128]{2,1,0:T(8,128)(2,1)S(1)} %pad_maximum_fusion.3), channel_id=1, source_target_pairs={{1,9},{3,11},{5,13},{7,15},{8,0},{10,2},{12,4},{14,6},{17,25},{19,... | collective-permute-start | bytes 1228808 | tf_op jit(solution)/shard_map/ppermute | solution.py:93
  123.8 7.1 %fusion.6 = f32[24,64,256]{2,1,0:T(8,128)S(1)} fusion(f32[256,24,64]{0,2,1:T(8,128)S(1)} %bitcast.146, f32[24,256]{1,0:T(8,128)S(1)} %copy-done.18, f32[24,256]{1,0:T(8,128)S(1)} %copy-done.19, f32[256,256]{1,0:T(8,128)S(1)} %fusion.94, pred[256,256]{1,0:T(8,128)(4,1)S(1)} %copy-done.14), kind=kOutput, calls=%fused_computation.6 | convolution fusion | flops 1214251008 | bytes 3522560 | tf_op jit(solution)/shard_map/hts,shp->thp/dot_general | solution.py:74
  130.9 6.5 %collective-permute-done.5 = bf16[25,64,128]{2,1,0:T(8,128)(2,1)S(1)} collective-permute-done((bf16[25,64,128]{2,1,0:T(8,128)(2,1)S(1)}, bf16[25,64,128]{2,1,0:T(8,128)(2,1)S(1)}, u32[]{:S(2)}, u32[]{:S(2)}) %collective-permute-start.5) | collective-permute-done | bytes 409632 | tf_op jit(solution)/shard_map/ppermute | solution.py:93
  137.9 7.1 %fusion = f32[24,64,256]{2,1,0:T(8,128)S(1)} fusion(f32[256,24,64]{0,2,1:T(8,128)S(1)} %bitcast.149, f32[24,256]{1,0:T(8,128)S(1)} %copy-done.16, f32[24,256]{1,0:T(8,128)S(1)} %copy-done.17, f32[256,256]{1,0:T(8,128)S(1)} %fusion.89, pred[256,256]{1,0:T(8,128)(4,1)S(1)} %copy-done.13), kind=kOutput, calls=%fused_computation | convolution fusion | flops 1214251008 | bytes 3522560 | tf_op jit(solution)/shard_map/hts,shp->thp/dot_general | solution.py:74
  145.0 2.6 %fusion.59 = f32[256,24,64]{0,2,1:T(8,128)S(1)} fusion(bf16[24,64,128]{2,1,0:T(8,128)(2,1)S(1)} %collective-permute-done.6, f32[24]{0:T(128)S(1)} %fusion.140, pred[]{:T(512)S(6)} %eq.69, bf16[25,64,128]{2,1,0:T(8,128)(2,1)S(1)} %collective-permute-done.2, f32[256,1792]{1,0:T(8,128)} %copy-done.1, bf16[25,64,128]{2,1,0:T(8,128)(2,1)S(1)} %collective-permute-done.5, ...), kind=kOutput, calls=%fused_computation.88 | convolution fusion | flops 606339072 | bytes 3671553 | tf_op jit(solution)/shard_map/tn,hpn->thp/dot_general | solution.py:170
  147.6 2.7 %fusion.46 = f32[256,24,64]{0,2,1:T(8,128)} fusion(f32[24,64,256]{2,1,0:T(8,128)S(1)} %fusion, f32[24,64,256]{2,1,0:T(8,128)S(1)} %fusion.6, f32[256,24,64]{0,2,1:T(8,128)S(1)} %fusion.59, bf16[24,64,128]{2,1,0:T(8,128)(2,1)S(1)} %collective-permute-done.6, f32[256,24]{0,1:T(8,128)S(1)} %copy-done.12, f32[256,24]{0,1:T(8,128)S(1)} %copy.100, ...), kind=kOutput, calls=%fused_computation.62 | convolution fusion | flops 608305152 | bytes 8439297 | tf_op jit(solution)/shard_map/tn,hpn->thp/dot_general | solution.py:170
  150.3 2.0 %copy.105 = f32[256,1536]{1,0:T(8,128)S(1)} copy(f32[256,1536]{0,1:T(8,128)} %bitcast.147) | data formatting | bytes 3145728 | tf_op jit(solution)/shard_map/add | solution.py:173
  153.7 4.9 %fusion.27 = bf16[256,1536]{1,0:T(8,128)(2,1)} fusion(f32[256,1536]{1,0:T(8,128)S(1)} %copy-done.9, bf16[1536,1536]{1,0:T(8,128)(2,1)} %param.27, f32[1536]{0:T(1024)S(1)} %copy-done.25, f32[256]{0:T(256)S(1)} %add_rsqrt_fusion, f32[256,1536]{1,0:T(8,128)S(1)} %copy.105, bf16[256,3328]{1,0:T(8,128)(2,1)S(1)} %copy-done.7), kind=kOutput, calls=%fused_computation.32 | convolution fusion | flops 1212284928 | bytes 9446400 | tf_op jit(solution)/shard_map/dot_general | solution.py:176
  (130 shorter events, 32.0 us)
Async XLA Ops:
  0.0 52.9 %copy-start = (bf16[1536,24]{0,1:T(8,128)(2,1)S(1)}, bf16[1536,24]{0,1:T(8,128)(2,1)}, u32[]{:S(2)}) copy-start(bf16[1536,24]{0,1:T(8,128)(2,1)} %param.21) | copy-start | bytes 221188
  6.8 7.7 %copy-start.15 = (f32[2,4,1792]{2,1,0:T(4,128)S(1)}, f32[2,4,1792]{2,1,0:T(4,128)}, u32[]{:S(2)}) copy-start(f32[2,4,1792]{2,1,0:T(4,128)} %param.22) | copy-start | bytes 172036
  6.8 7.8 %copy-start.22 = (f32[2,24]{1,0:T(2,128)S(1)}, f32[2,24]{1,0:T(2,128)}, u32[]{:S(2)}) copy-start(f32[2,24]{1,0:T(2,128)} %param.25) | copy-start | bytes 580
  6.8 7.8 %copy-start.23 = (f32[2,24]{1,0:T(2,128)S(1)}, f32[2,24]{1,0:T(2,128)}, u32[]{:S(2)}) copy-start(f32[2,24]{1,0:T(2,128)} %param.24) | copy-start | bytes 580
  6.8 41.9 %copy-start.24 = (f32[1536]{0:T(1024)S(1)}, f32[1536]{0:T(1024)}, u32[]{:S(2)}) copy-start(f32[1536]{0:T(1024)} %param.18) | copy-start | bytes 18436
  6.8 41.7 %all-to-all-start = ((bf16[16,32,1664]{2,1,0:T(8,128)(2,1)}), bf16[16,32,1664]{2,1,0:T(8,128)(2,1)S(1)}, u32[]{:S(2)}, u32[]{:S(2)}) async-start(bf16[16,32,1664]{2,1,0:T(8,128)(2,1)} %bitcast.3), calls=%async_computation | async-start | bytes 3407872 | tf_op jit(solution)/shard_map/all_to_all | solution.py:37
  52.9 12.1 %copy-start.8 = (f32[256,1536]{1,0:T(8,128)}, f32[256,1536]{1,0:T(8,128)S(1)}, u32[]{:S(2)}) copy-start(f32[256,1536]{1,0:T(8,128)S(1)} %get-tuple-element.53) | copy-start | bytes 4718596
  58.0 11.4 %copy-start.10 = (f32[24,2,128]{0,2,1:T(8,128)}, f32[24,2,128]{0,2,1:T(8,128)S(1)}, u32[]{:S(2)}) copy-start(f32[24,2,128]{0,2,1:T(8,128)S(1)} %copy.96) | copy-start | bytes 73732
  58.1 11.3 %copy-start.11 = (f32[24,2,128]{0,2,1:T(8,128)}, f32[24,2,128]{0,2,1:T(8,128)S(1)}, u32[]{:S(2)}) copy-start(f32[24,2,128]{0,2,1:T(8,128)S(1)} %copy.90) | copy-start | bytes 73732
  65.0 5.5 %collective-permute-start = (bf16[3,1792]{1,0:T(4,128)(2,1)S(1)}, bf16[3,1792]{1,0:T(4,128)(2,1)S(1)}, u32[]{:S(2)}, u32[]{:S(2)}) collective-permute-start(bf16[3,1792]{1,0:T(4,128)(2,1)S(1)} %get-tuple-element.34), channel_id=1, source_target_pairs={{0,1},{1,2},{2,3},{3,4},{4,5},{5,6},{6,7},{7,8},{8,9},{9,10},{10,1... | collective-permute-start | bytes 32264 | tf_op jit(solution)/shard_map/ppermute | solution.py:50
  67.9 4.6 %collective-permute-start.1 = (bf16[3,1792]{1,0:T(4,128)(2,1)S(1)}, bf16[3,1792]{1,0:T(4,128)(2,1)S(1)}, u32[]{:S(2)}, u32[]{:S(2)}) collective-permute-start(bf16[3,1792]{1,0:T(4,128)(2,1)S(1)} %get-tuple-element.35), channel_id=1, source_target_pairs={{1,0},{2,1},{3,2},{4,3},{5,4},{6,5},{7,6},{8,7},{9,8},{10,9},{11,1... | collective-permute-start | bytes 32264 | tf_op jit(solution)/shard_map/ppermute | solution.py:51
  88.1 3.9 %collective-permute-start.2 = (bf16[25,64,128]{2,1,0:T(8,128)(2,1)S(1)}, bf16[25,64,128]{2,1,0:T(8,128)(2,1)S(1)}, u32[]{:S(2)}, u32[]{:S(2)}) collective-permute-start(bf16[25,64,128]{2,1,0:T(8,128)(2,1)S(1)} %pad_maximum_fusion), channel_id=1, source_target_pairs={{0,1},{1,0},{2,3},{3,2},{4,5},{5,4},{6,7},{7,6},{8,9},{9,8},{10,11... | collective-permute-start | bytes 1228808 | tf_op jit(solution)/shard_map/ppermute | solution.py:93
  93.8 12.8 %collective-permute-start.3 = (bf16[25,64,128]{2,1,0:T(8,128)(2,1)}, bf16[25,64,128]{2,1,0:T(8,128)(2,1)S(1)}, u32[]{:S(2)}, u32[]{:S(2)}) collective-permute-start(bf16[25,64,128]{2,1,0:T(8,128)(2,1)} %pad_maximum_fusion.1), channel_id=1, source_target_pairs={{1,3},{3,5},{5,7},{7,9},{9,11},{11,13},{13,15},{2,0},{4,2},{6,4},{... | collective-permute-start | bytes 1228808 | tf_op jit(solution)/shard_map/ppermute | solution.py:93
  106.8 14.9 %collective-permute-start.4 = (bf16[25,64,128]{2,1,0:T(8,128)(2,1)S(1)}, bf16[25,64,128]{2,1,0:T(8,128)(2,1)S(1)}, u32[]{:S(2)}, u32[]{:S(2)}) collective-permute-start(bf16[25,64,128]{2,1,0:T(8,128)(2,1)S(1)} %pad_maximum_fusion.2), channel_id=1, source_target_pairs={{1,5},{3,7},{5,9},{7,11},{9,13},{11,15},{4,0},{6,2},{8,4},{10,6},{... | collective-permute-start | bytes 1228808 | tf_op jit(solution)/shard_map/ppermute | solution.py:93
  109.5 14.3 %copy-start.3 = (f32[256,1536]{0,1:T(8,128)S(1)}, f32[256,1536]{0,1:T(8,128)}, u32[]{:S(2)}) copy-start(f32[256,1536]{0,1:T(8,128)} %copy-done.2) | copy-start | bytes 4718596
  109.5 14.3 %copy-start.14 = (pred[256,256]{1,0:T(8,128)(4,1)S(1)}, pred[256,256]{1,0:T(8,128)(4,1)}, u32[]{:S(2)}) copy-start(pred[256,256]{1,0:T(8,128)(4,1)} %iota_compare_fusion.7) | copy-start | bytes 196612
  109.5 14.3 %copy-start.18 = (f32[24,256]{1,0:T(8,128)S(1)}, f32[24,256]{1,0:T(8,128)}, u32[]{:S(2)}) copy-start(f32[24,256]{1,0:T(8,128)} %copy.93) | copy-start | bytes 73732
  109.5 14.3 %copy-start.19 = (f32[24,256]{1,0:T(8,128)S(1)}, f32[24,256]{1,0:T(8,128)}, u32[]{:S(2)}) copy-start(f32[24,256]{1,0:T(8,128)} %copy.91) | copy-start | bytes 73732
  122.1 15.7 %copy-start.5 = (f32[256,1536]{0,1:T(8,128)S(1)}, f32[256,1536]{0,1:T(8,128)}, u32[]{:S(2)}) copy-start(f32[256,1536]{0,1:T(8,128)} %copy.98) | copy-start | bytes 4718596
  122.1 15.7 %copy-start.13 = (pred[256,256]{1,0:T(8,128)(4,1)S(1)}, pred[256,256]{1,0:T(8,128)(4,1)}, u32[]{:S(2)}) copy-start(pred[256,256]{1,0:T(8,128)(4,1)} %iota_compare_fusion.6) | copy-start | bytes 196612
  122.1 15.7 %copy-start.16 = (f32[24,256]{1,0:T(8,128)S(1)}, f32[24,256]{1,0:T(8,128)}, u32[]{:S(2)}) copy-start(f32[24,256]{1,0:T(8,128)} %copy.103) | copy-start | bytes 73732
  122.1 15.7 %copy-start.17 = (f32[24,256]{1,0:T(8,128)S(1)}, f32[24,256]{1,0:T(8,128)}, u32[]{:S(2)}) copy-start(f32[24,256]{1,0:T(8,128)} %copy.101) | copy-start | bytes 73732
  122.1 15.3 %collective-permute-start.5 = (bf16[25,64,128]{2,1,0:T(8,128)(2,1)S(1)}, bf16[25,64,128]{2,1,0:T(8,128)(2,1)S(1)}, u32[]{:S(2)}, u32[]{:S(2)}) collective-permute-start(bf16[25,64,128]{2,1,0:T(8,128)(2,1)S(1)} %pad_maximum_fusion.3), channel_id=1, source_target_pairs={{1,9},{3,11},{5,13},{7,15},{8,0},{10,2},{12,4},{14,6},{17,25},{19,... | collective-permute-start | bytes 1228808 | tf_op jit(solution)/shard_map/ppermute | solution.py:93
  137.8 7.2 %collective-permute-start.6 = (bf16[24,64,128]{2,1,0:T(8,128)(2,1)S(1)}, bf16[24,64,128]{2,1,0:T(8,128)(2,1)S(1)}, u32[]{:S(2)}, u32[]{:S(2)}) collective-permute-start(bf16[24,64,128]{2,1,0:T(8,128)(2,1)S(1)} %fusion.144), channel_id=1, source_target_pairs={{0,1},{1,0},{2,3},{3,2},{4,5},{5,4},{6,7},{7,6},{8,9},{9,8},{10,11... | collective-permute-start | bytes 1179656 | tf_op jit(solution)/shard_map/ppermute | solution.py:119
  (10 other events, 33.1 us)

commit v2 on v1

--- a/solution.py
+++ b/solution.py
@@ -10,7 +10,7 @@
 HEADS = 24
 
 
-precise = lax.Precision.HIGHEST
+fast = lax.Precision.HIGH
 epsilon = 1e-05
 
 
@@ -47,36 +47,35 @@
     size = lax.axis_size("seq")
     up = [(i, i + 1) for i in range(size - 1)]
     down = [(i + 1, i) for i in range(size - 1)]
-    before = lax.ppermute(shard[-width:], "seq", up)
-    after = lax.ppermute(shard[:width], "seq", down)
-    return jnp.concatenate([before, shard, after], axis=0)
+    before = lax.ppermute(shard[:, -width:].T, "seq", up).T
+    after = lax.ppermute(shard[:, :width].T, "seq", down).T
+    return jnp.concatenate([before, shard, after], axis=1)
 
 
 def local_terms(activated, step_size, decay_rate, backward):
-    rows = activated.shape[0]
-    signal = activated[:, :E].reshape(rows, HEADS, HEAD_DIM)
-    write_map = activated[:, E : E + NS]
-    read_map = activated[:, E + NS :]
-    log_step = step_size * decay_rate
-    log_decay = lax.cumsum(log_step, axis=0, reverse=backward)
+    rows = activated.shape[1]
+    signal = activated[:E].reshape(HEADS, HEAD_DIM, rows)
+    write_map = activated[E : E + NS]
+    read_map = activated[E + NS :]
+    log_step = step_size * decay_rate[:, None]
+    log_decay = lax.cumsum(log_step, axis=1, reverse=backward)
     positions = jnp.arange(rows)
     if backward:
         mask = positions[:, None] <= positions[None, :]
-        edge = log_decay[0]
+        edge = log_decay[:, :1]
     else:
         mask = positions[:, None] >= positions[None, :]
-        edge = log_decay[-1]
-    turned = log_decay.T
-    gaps = turned[:, :, None] - turned[:, None, :]
+        edge = log_decay[:, -1:]
+    gaps = log_decay[:, :, None] - log_decay[:, None, :]
     weights = jnp.exp(jnp.where(mask[None], gaps, -1e30))
-    scores = jnp.dot(read_map, write_map.T, precision=precise)
-    mixing = scores[None] * weights * step_size.T[:, None, :]
-    within = jnp.einsum("hts,shp->thp", mixing, signal, precision=precise)
-    tail_weight = jnp.exp(edge[None, :] - log_decay) * step_size
-    own_state = jnp.einsum(
-        "shp,sn->hpn", tail_weight[:, :, None] * signal, write_map, precision=precise
-    )
-    return within, own_state, jnp.exp(edge), jnp.exp(log_decay), read_map
+    scores = lax.dot_general(read_map, write_map, (((0,), (0,)), ((), ())), precision=fast)
+    mixing = scores[None] * weights * step_size[:, None, :]
+    within = lax.dot_general(signal, mixing, (((2,), (2,)), ((0,), (0,))), precision=fast)
+    tail_weight = jnp.exp(edge - log_decay) * step_size
+    own_state = lax.dot_general(
+        signal * tail_weight[:, None, :], write_map, (((2,), (1,)), ((), ())), precision=fast
+    )
+    return within, own_state, jnp.exp(edge[:, 0]), jnp.exp(log_decay), read_map
 
 
 def combine(earlier, later):
@@ -144,37 +143,40 @@
         jnp.dot(tiles, slide_weight, preferred_element_type=jnp.float32) + slide_bias
     ).astype(jnp.bfloat16)
     normed = rms_scale(embedded.astype(jnp.float32), norm_gain).astype(jnp.bfloat16)
-    projected = jnp.dot(normed, in_weight, preferred_element_type=jnp.float32).astype(jnp.bfloat16)
-    dt_raw = jnp.dot(normed, dt_weight, preferred_element_type=jnp.float32)
-    gate_part = projected[:, :E].astype(jnp.float32)
-    conv_input = projected[:, E:]
+    turned = (((0,), (1,)), ((), ()))
+    projected = lax.dot_general(
+        in_weight, normed, turned, preferred_element_type=jnp.float32
+    ).astype(jnp.bfloat16)
+    dt_raw = lax.dot_general(dt_weight, normed, turned, preferred_element_type=jnp.float32)
+    gate_part = projected[:E].astype(jnp.float32)
+    conv_input = projected[E:]
     padded = halo(conv_input, KERNEL - 1).astype(jnp.float32)
     parts = []
     for direction in range(2):
-        summed = conv_bias[direction] + jnp.zeros((rows, conv_input.shape[1]), jnp.float32)
+        summed = conv_bias[direction][:, None] + jnp.zeros((conv_input.shape[0], rows), jnp.float32)
         for offset in range(KERNEL):
             first = offset if direction == 0 else 2 * (KERNEL - 1) - offset
-            summed = summed + conv_weight[direction, offset] * padded[first : first + rows]
+            summed = summed + conv_weight[direction, offset][:, None] * padded[:, first : first + rows]
         activated = jax.nn.silu(summed)
-        step_size = jax.nn.softplus(dt_raw + dt_bias[direction])
+        step_size = jax.nn.softplus(dt_raw + dt_bias[direction][:, None])
         decay_rate = -jnp.exp(a_log[direction])
         parts.append(local_terms(activated, step_size, decay_rate, direction == 1))
     incomings = exchange(
         (parts[0][2], parts[0][1]), (parts[1][2], parts[1][1])
     )
-    total = jnp.zeros((rows, E), jnp.float32)
+    total = jnp.zeros((HEADS, HEAD_DIM, rows), jnp.float32)
     for direction in range(2):
         within, own_state, device_decay, decay_to, read_map = parts[direction]
         incoming = incomings[direction]
-        carried = (
-            jnp.einsum("tn,hpn->thp", read_map, incoming, precision=precise)
-            * decay_to[:, :, None]
-        )
-        total = total + (within + carried).reshape(rows, E)
-    gated = total * jax.nn.silu(gate_part)
-    mixed = rms_scale(gated, out_gain).astype(jnp.bfloat16)
-    hidden = embedded.astype(jnp.float32) + jnp.dot(
-        mixed, out_weight, preferred_element_type=jnp.float32
+        carried = lax.dot_general(
+            incoming, read_map, (((2,), (0,)), ((), ())), precision=fast
+        ) * decay_to[:, None, :]
+        total = total + within + carried
+    gated = total.reshape(E, rows) * jax.nn.silu(gate_part)
+    mean_sq = jnp.mean(gated * gated, axis=0, keepdims=True)
+    mixed = (gated * lax.rsqrt(mean_sq + epsilon) * out_gain[:, None]).astype(jnp.bfloat16)
+    hidden = embedded.astype(jnp.float32) + lax.dot_general(
+        mixed, out_weight, (((0,), (0,)), ((), ())), preferred_element_type=jnp.float32
     )
     return hidden.astype(jnp.bfloat16)
 

time: 159 us -> 153 us (0.962)
  waiting for transfers between devices: 56.1 us -> 70.5 us
  matrix products: 45.9 us -> 36 us
  local copies, waits for them, and re-layouts: 22.3 us -> 13 us
  other arithmetic: 14.2 us -> 12.2 us
    ppermute x4, waiting for transfers between devices: 20.3 us -> 34.5 us  [transfer(): got = lax.ppermute(payload, 'seq', pairs)]
    dot_general x11, matrix products: 37.9 us -> 28 us  [the longest x2 7.78 us: local_terms(): lax.dot_general(signal, mixing, (((2,), (2,)), ((0,), (0,))), precision=f...]
    another operation x11 -> x6, local copies, waits for them, and re-layouts: 3.75 us -> 0.27 us  [the longest x4 3.35 us: local_terms(): log_decay = lax.cumsum(log_step, axis=0, reverse=backward)]
    select_n x2 -> x0, local copies, waits for them, and re-layouts: 3.15 us -> none  [per_device(): step_size = jax.nn.softplus(dt_raw + dt_bias[direction])]
    exp x2 -> x0, local copies, waits for them, and re-layouts: 2.55 us -> none  [local_terms(): return (within, own_state, jnp.exp(edge), jnp.exp(log_decay), read_map)]
    reshape x0 -> x1, local copies, waits for them, and re-layouts: none -> 2 us  [per_device(): gated = total.reshape(E, rows) * jax.nn.silu(gate_part)]
    add x1, local copies, waits for them, and re-layouts: 2 us -> 0.01 us  [per_device(): step_size = jax.nn.softplus(dt_raw + dt_bias[direction][:, None])]
    slice x9 -> x8, local copies, waits for them, and re-layouts: 8.39 us -> 8.37 us  [the longest x4 7.91 us: local_terms(): signal = activated[:E].reshape(HEADS, HEAD_DIM, rows)]
  transfers between devices with their start and end apart: 8 -> 8, of which waited for: 6 -> 6; matrix products, arithmetic and copies ran while one was open for 18% -> 7% of each run, Pallas kernels for 0% -> 0%
where the time goes in v2:
time: 153 us; the launch traced here: 152 us
  waiting for transfers between devices  70.5 us (46%)
  matrix products  36 us (24%)
  starting transfers between devices  18.7 us (12%)
  local copies, waits for them, and re-layouts  13 us (8%)
  other arithmetic  12.2 us (8%)
    ppermute x4, waiting for transfers between devices, transfer(): got = lax.ppermute(payload, 'seq', pairs)  34.5 us
    all_to_all x1, waiting for transfers between devices, route_tiles(): lax.all_to_all(send, 'seq', 0, 0, tiled=True)  33.8 us
    slice x4, local copies, waits for them, and re-layouts, local_terms(): signal = activated[:E].reshape(HEADS, HEAD_DIM, rows)  7.91 us
    dot_general x2, matrix products, local_terms(): lax.dot_general(signal, mixing, (((2,), (2,)), ((0,), (0,))), precision=f...  7.78 us
    all_to_all x1, starting transfers between devices, route_tiles(): lax.all_to_all(send, 'seq', 0, 0, tiled=True)  7.56 us
    dot_general x1, matrix products, per_device(): lax.dot_general(in_weight, normed, turned, preferred_element_type=jnp.flo...  6.79 us
    ppermute x4, starting transfers between devices, transfer(): got = lax.ppermute(payload, 'seq', pairs)  6.75 us
    dot_general x1, matrix products, per_device(): lax.dot_general(mixed, out_weight, (((0,), (0,)), ((), ())), preferred_el...  4.86 us
  transfers between devices with their start and end apart: 8, of which 6 were waited for; matrix products, arithmetic and copies ran while one was open for 7% of the time, Pallas kernels for 0%

profile of v2, /device:TPU:0, one launch (start us, length us, event | category | flops | bytes accessed | tf_op | source)
XLA Modules:
  0.0 151.9 jit_solution(7267690538385868487)
XLA Ops:
  3.1 3.7 %convolution_convert_fusion.1 = bf16[512,1664]{1,0:T(8,128)(2,1)} fusion(bf16[512,1]{1,0:T(8,128)(2,1)S(1)} %broadcast_in_dim.48, bf16[512,1536]{1,0:T(8,128)(2,1)} %param.14, s32[512]{0:T(512)S(1)} %add_select_fusion.2), kind=kOutput, calls=%fused_computation.28 | convolution fusion | flops 878641152 | bytes 3279872 | tf_op jit(solution)/shard_map/dot_general | solution.py:35
  6.8 7.6 %all-to-all-start = ((bf16[16,32,1664]{2,1,0:T(8,128)(2,1)}), bf16[16,32,1664]{2,1,0:T(8,128)(2,1)S(1)}, u32[]{:S(2)}, u32[]{:S(2)}) async-start(bf16[16,32,1664]{2,1,0:T(8,128)(2,1)} %bitcast.3), calls=%async_computation | async-start | bytes 3407872 | tf_op jit(solution)/shard_map/all_to_all | solution.py:37
  14.7 33.8 %all-to-all-done = bf16[16,32,1664]{2,1,0:T(8,128)(2,1)S(1)} async-done(((bf16[16,32,1664]{2,1,0:T(8,128)(2,1)}), bf16[16,32,1664]{2,1,0:T(8,128)(2,1)S(1)}, u32[]{:S(2)}, u32[]{:S(2)}) %all-to-all-start) | async-done | bytes 1703968 | tf_op jit(solution)/shard_map/all_to_all | solution.py:37
  48.7 4.2 %multiply_reduce_fusion.1 = (f32[256]{0:T(256)S(1)}, f32[256,1536]{1,0:T(8,128)S(1)}) fusion(f32[1536]{0:T(1024)S(1)} %copy-done.31, bf16[1536,1536]{1,0:T(8,128)(2,1)} %param.17, bf16[512,1664]{1,0:T(8,128)(2,1)S(1)} %bitcast.180, s32[512]{0:T(512)S(1)} %add_reduce_fusion), kind=kOutput, calls=%fused_computation.70 | convolution fusion | flops 1613102848 | bytes 7875584 | tf_op jit(solution)/shard_map/dot_general | solution.py:143
  53.4 2.5 %reduce-window.26 = f32[24,2,128]{2,0,1:T(8,128)S(1)} reduce-window(f32[24,2,128]{2,0,1:T(8,128)S(1)} %get-tuple-element.56, f32[]{:T(128)} %constant.89.clone.1), window={size=1x1x128 pad=0_0x0_0x0_127}, to_apply=%region_6.7 | reduce-window | flops 780288 | bytes 49156 | tf_op jit(solution)/shard_map/reduce-window.4
  57.8 6.8 %fusion.12 = bf16[3328,256]{0,1:T(8,128)(2,1)S(1)} fusion(bf16[1536,3328]{1,0:T(8,128)(2,1)} %param.20, f32[256,1536]{1,0:T(8,128)S(1)} %get-tuple-element.53, f32[1536]{0:T(1024)S(1)} %copy-done.22, f32[256]{0:T(256)S(1)} %add_rsqrt_fusion.1), kind=kOutput, calls=%fused_computation.13 | convolution fusion | flops 2619277312 | bytes 13507584 | tf_op jit(solution)/shard_map/dot_general | solution.py:147
  64.7 2.9 %collective-permute-start = (bf16[3,1792]{1,0:T(4,128)(2,1)S(1)}, bf16[3,1792]{1,0:T(4,128)(2,1)S(1)}, u32[]{:S(2)}, u32[]{:S(2)}) collective-permute-start(bf16[3,1792]{1,0:T(4,128)(2,1)S(1)} %get-tuple-element.36), channel_id=1, source_target_pairs={{0,1},{1,2},{2,3},{3,4},{4,5},{5,6},{6,7},{7,8},{8,9},{9,10},{10,1... | collective-permute-start | bytes 32264 | tf_op jit(solution)/shard_map/ppermute | solution.py:50
  70.0 2.2 %collective-permute-done.1 = bf16[3,1792]{1,0:T(4,128)(2,1)S(1)} collective-permute-done((bf16[3,1792]{1,0:T(4,128)(2,1)S(1)}, bf16[3,1792]{1,0:T(4,128)(2,1)S(1)}, u32[]{:S(2)}, u32[]{:S(2)}) %collective-permute-start.1) | collective-permute-done | bytes 10784 | tf_op jit(solution)/shard_map/ppermute | solution.py:51
  72.4 2.3 %divide_multiply_fusion.1 = (f32[1792,256]{0,1:T(8,128)S(1)}, f32[1792,256]{0,1:T(8,128)S(1)}) fusion(f32[1792,262]{0,1:T(8,128)S(1)} %maximum_convert_fusion, f32[1792]{0:T(1024)S(1)} %get-tuple-element.8, f32[1792]{0:T(1024)S(1)} %get-tuple-element.9, f32[1792]{0:T(1024)S(1)} %get-tuple-element.10, f32[1792]{0:T(1024)S(1)} %get-tuple-element.5, ...), kind=kLoop, calls=%fused_computation.52 | loop fusion | flops 11010048 | bytes 16586752 | tf_op jit(solution)/shard_map/jit(silu)/mul | solution.py:160
  77.3 1.9 %copy.44 = f32[1536,256]{1,0:T(8,128)S(1)} copy(f32[1536,256]{0,1:T(8,128)} %slice.217) | data formatting | bytes 3145728 | tf_op jit(solution)/shard_map/slice | solution.py:57
  79.2 1.6 %slice.224 = f32[1536,256]{0,1:T(8,128)} slice(f32[1792,256]{0,1:T(8,128)S(1)} %get-tuple-element.35), slice={[0:1536], [0:256]} | slice | bytes 3145728 | tf_op jit(solution)/shard_map/slice | solution.py:57
  80.8 3.1 %copy.47 = f32[1536,256]{1,0:T(8,128)} copy(f32[1536,256]{0,1:T(8,128)} %slice.224) | data formatting | bytes 3145728 | tf_op jit(solution)/shard_map/slice | solution.py:57
  83.9 1.8 %fusion.47 = f32[24,64,128]{2,1,0:T(8,128)S(1)} fusion(f32[24,64,256]{2,1,0:T(8,128)S(1)} %bitcast.174, f32[24,256]{1,0:T(8,128)S(1)} %get-tuple-element.39, f32[1792,256]{0,1:T(8,128)} %copy-done.1), kind=kOutput, calls=%fused_computation.65 | convolution fusion | flops 302383104 | bytes 2514944 | tf_op jit(solution)/shard_map/dot_general | solution.py:75
  86.6 2.5 %collective-permute-start.2 = (bf16[25,64,128]{2,1,0:T(8,128)(2,1)S(1)}, bf16[25,64,128]{2,1,0:T(8,128)(2,1)S(1)}, u32[]{:S(2)}, u32[]{:S(2)}) collective-permute-start(bf16[25,64,128]{2,1,0:T(8,128)(2,1)S(1)} %pad_maximum_fusion), channel_id=1, source_target_pairs={{0,1},{1,0},{2,3},{3,2},{4,5},{5,4},{6,7},{7,6},{8,9},{9,8},{10,11... | collective-permute-start | bytes 1228808 | tf_op jit(solution)/shard_map/ppermute | solution.py:92
  92.9 11.4 %collective-permute-done.3 = bf16[25,64,128]{2,1,0:T(8,128)(2,1)S(1)} collective-permute-done((bf16[25,64,128]{2,1,0:T(8,128)(2,1)}, bf16[25,64,128]{2,1,0:T(8,128)(2,1)S(1)}, u32[]{:S(2)}, u32[]{:S(2)}) %collective-permute-start.3) | collective-permute-done | bytes 409632 | tf_op jit(solution)/shard_map/ppermute | solution.py:92
  107.5 12.1 %collective-permute-done.4 = bf16[25,64,128]{2,1,0:T(8,128)(2,1)S(1)} collective-permute-done((bf16[25,64,128]{2,1,0:T(8,128)(2,1)S(1)}, bf16[25,64,128]{2,1,0:T(8,128)(2,1)S(1)}, u32[]{:S(2)}, u32[]{:S(2)}) %collective-permute-start.4) | collective-permute-done | bytes 409632 | tf_op jit(solution)/shard_map/ppermute | solution.py:92
  119.9 1.6 %collective-permute-start.5 = (bf16[25,64,128]{2,1,0:T(8,128)(2,1)S(1)}, bf16[25,64,128]{2,1,0:T(8,128)(2,1)S(1)}, u32[]{:S(2)}, u32[]{:S(2)}) collective-permute-start(bf16[25,64,128]{2,1,0:T(8,128)(2,1)S(1)} %pad_maximum_fusion.3), channel_id=1, source_target_pairs={{1,9},{3,11},{5,13},{7,15},{8,0},{10,2},{12,4},{14,6},{17,25},{19,... | collective-permute-start | bytes 1228808 | tf_op jit(solution)/shard_map/ppermute | solution.py:92
  121.6 3.9 %fusion.6 = f32[24,64,256]{2,1,0:T(8,128)S(1)} fusion(f32[24,64,256]{2,1,0:T(8,128)S(1)} %bitcast.175, f32[24,256]{1,0:T(8,128)S(1)} %copy-done.15, f32[24,256]{1,0:T(8,128)S(1)} %copy-done.20, f32[256,256]{1,0:T(8,128)S(1)} %fusion.84, pred[256,256]{1,0:T(8,128)(4,1)S(1)} %iota_compare_fusion.7), kind=kOutput, calls=%fused_computation.6 | convolution fusion | flops 610271232 | bytes 3522560 | tf_op jit(solution)/shard_map/dot_general | solution.py:73
  125.5 9.7 %collective-permute-done.5 = bf16[25,64,128]{2,1,0:T(8,128)(2,1)S(1)} collective-permute-done((bf16[25,64,128]{2,1,0:T(8,128)(2,1)S(1)}, bf16[25,64,128]{2,1,0:T(8,128)(2,1)S(1)}, u32[]{:S(2)}, u32[]{:S(2)}) %collective-permute-start.5) | collective-permute-done | bytes 409632 | tf_op jit(solution)/shard_map/ppermute | solution.py:92
  135.7 3.9 %fusion = f32[24,64,256]{2,1,0:T(8,128)S(1)} fusion(f32[24,64,256]{2,1,0:T(8,128)S(1)} %bitcast.178, f32[24,256]{1,0:T(8,128)S(1)} %copy-done.13, f32[24,256]{1,0:T(8,128)S(1)} %copy-done.18, f32[256,256]{1,0:T(8,128)S(1)} %fusion.79, pred[256,256]{1,0:T(8,128)(4,1)S(1)} %iota_compare_fusion.6), kind=kOutput, calls=%fused_computation | convolution fusion | flops 610271232 | bytes 3522560 | tf_op jit(solution)/shard_map/dot_general | solution.py:73
  139.6 1.9 %fusion.59 = f32[24,64,256]{2,1,0:T(8,128)S(1)} fusion(bf16[24,64,128]{2,1,0:T(8,128)(2,1)S(1)} %collective-permute-done.6, f32[24]{0:T(128)S(1)} %bitcast.187, pred[]{:T(512)S(6)} %eq.69, bf16[25,64,128]{2,1,0:T(8,128)(2,1)S(1)} %collective-permute-done.2, f32[1792,256]{0,1:T(8,128)} %copy-done.1, bf16[25,64,128]{2,1,0:T(8,128)(2,1)S(1)} %collective-permute-done.5, ...), kind=kOutput, calls=%fused_computation.87 | convolution fusion | flops 304349184 | bytes 3671553 | tf_op jit(solution)/shard_map/dot_general | solution.py:171
  141.5 2.2 %multiply_add_fusion = f32[24,64,256]{2,1,0:T(8,128)} fusion(f32[24,64,256]{2,1,0:T(8,128)S(1)} %fusion, f32[24,64,256]{2,1,0:T(8,128)S(1)} %fusion.6, f32[24,64,256]{2,1,0:T(8,128)S(1)} %fusion.59, bf16[24,64,128]{2,1,0:T(8,128)(2,1)S(1)} %collective-permute-done.6, f32[24,256]{1,0:T(8,128)S(1)} %copy-done.10, f32[24,256]{1,0:T(8,128)S(1)} %get-tuple-element.38, ...), kind=kOutput, calls=%fused_computation.64 | convolution fusion | flops 306315264 | bytes 8439297 | tf_op jit(solution)/shard_map/dot_general | solution.py:171
  143.6 2.0 %copy.54 = f32[1536,256]{0,1:T(8,128)S(1)} copy(f32[1536,256]{1,0:T(8,128)} %bitcast.176) | data formatting | bytes 3145728 | tf_op jit(solution)/shard_map/reshape | solution.py:175
  147.0 4.9 %fusion.28 = bf16[256,1536]{1,0:T(8,128)(2,1)} fusion(f32[256,1536]{1,0:T(8,128)S(1)} %copy-done.9, bf16[1536,1536]{1,0:T(8,128)(2,1)} %param.27, f32[1536]{0:T(1024)S(1)} %copy-done.32, f32[256]{0:T(256)S(1)} %add_rsqrt_fusion, f32[1536,256]{0,1:T(8,128)S(1)} %copy.54, bf16[3328,256]{0,1:T(8,128)(2,1)S(1)} %copy-done.7), kind=kOutput, calls=%fused_computation.33 | convolution fusion | flops 1212284928 | bytes 9446400 | tf_op jit(solution)/shard_map/dot_general | solution.py:178
  (135 shorter events, 20.1 us)
Async XLA Ops:
  0.0 52.9 %copy-start = (bf16[1536,24]{0,1:T(8,128)(2,1)S(1)}, bf16[1536,24]{0,1:T(8,128)(2,1)}, u32[]{:S(2)}) copy-start(bf16[1536,24]{0,1:T(8,128)(2,1)} %param.21) | copy-start | bytes 221188
  6.8 7.8 %copy-start.29 = (f32[2,24]{1,0:T(2,128)S(1)}, f32[2,24]{1,0:T(2,128)}, u32[]{:S(2)}) copy-start(f32[2,24]{1,0:T(2,128)} %param.24) | copy-start | bytes 580
  6.8 7.8 %copy-start.30 = (f32[2,24]{1,0:T(2,128)S(1)}, f32[2,24]{1,0:T(2,128)}, u32[]{:S(2)}) copy-start(f32[2,24]{1,0:T(2,128)} %param.25) | copy-start | bytes 580
  6.8 41.9 %copy-start.31 = (f32[1536]{0:T(1024)S(1)}, f32[1536]{0:T(1024)}, u32[]{:S(2)}) copy-start(f32[1536]{0:T(1024)} %param.18) | copy-start | bytes 18436
  6.8 41.7 %all-to-all-start = ((bf16[16,32,1664]{2,1,0:T(8,128)(2,1)}), bf16[16,32,1664]{2,1,0:T(8,128)(2,1)S(1)}, u32[]{:S(2)}, u32[]{:S(2)}) async-start(bf16[16,32,1664]{2,1,0:T(8,128)(2,1)} %bitcast.3), calls=%async_computation | async-start | bytes 3407872 | tf_op jit(solution)/shard_map/all_to_all | solution.py:37
  52.9 11.7 %copy-start.8 = (f32[256,1536]{1,0:T(8,128)}, f32[256,1536]{1,0:T(8,128)S(1)}, u32[]{:S(2)}) copy-start(f32[256,1536]{1,0:T(8,128)S(1)} %get-tuple-element.53) | copy-start | bytes 4718596
  53.4 15.6 %copy-start.14 = (f32[24,256]{1,0:T(8,128)}, f32[24,256]{1,0:T(8,128)S(1)}, u32[]{:S(2)}) copy-start(f32[24,256]{1,0:T(8,128)S(1)} %get-tuple-element.31) | copy-start | bytes 73732
  53.4 15.8 %copy-start.12 = (f32[24,256]{1,0:T(8,128)}, f32[24,256]{1,0:T(8,128)S(1)}, u32[]{:S(2)}) copy-start(f32[24,256]{1,0:T(8,128)S(1)} %get-tuple-element.43) | copy-start | bytes 73732
  57.8 11.3 %copy-start.23 = (f32[24]{0:T(128)}, f32[24]{0:T(128)S(1)}, u32[]{:S(2)}) copy-start(f32[24]{0:T(128)S(1)} %get-tuple-element.15) | copy-start | bytes 292
  57.8 11.4 %copy-start.25 = (f32[24]{0:T(128)}, f32[24]{0:T(128)S(1)}, u32[]{:S(2)}) copy-start(f32[24]{0:T(128)S(1)} %get-tuple-element.16) | copy-start | bytes 292
  64.7 5.3 %collective-permute-start = (bf16[3,1792]{1,0:T(4,128)(2,1)S(1)}, bf16[3,1792]{1,0:T(4,128)(2,1)S(1)}, u32[]{:S(2)}, u32[]{:S(2)}) collective-permute-start(bf16[3,1792]{1,0:T(4,128)(2,1)S(1)} %get-tuple-element.36), channel_id=1, source_target_pairs={{0,1},{1,2},{2,3},{3,4},{4,5},{5,6},{6,7},{7,8},{8,9},{9,10},{10,1... | collective-permute-start | bytes 32264 | tf_op jit(solution)/shard_map/ppermute | solution.py:50
  67.6 4.6 %collective-permute-start.1 = (bf16[3,1792]{1,0:T(4,128)(2,1)S(1)}, bf16[3,1792]{1,0:T(4,128)(2,1)S(1)}, u32[]{:S(2)}, u32[]{:S(2)}) collective-permute-start(bf16[3,1792]{1,0:T(4,128)(2,1)S(1)} %get-tuple-element.37), channel_id=1, source_target_pairs={{1,0},{2,1},{3,2},{4,3},{5,4},{6,5},{7,6},{8,7},{9,8},{10,9},{11,1... | collective-permute-start | bytes 32264 | tf_op jit(solution)/shard_map/ppermute | solution.py:51
  86.6 3.9 %collective-permute-start.2 = (bf16[25,64,128]{2,1,0:T(8,128)(2,1)S(1)}, bf16[25,64,128]{2,1,0:T(8,128)(2,1)S(1)}, u32[]{:S(2)}, u32[]{:S(2)}) collective-permute-start(bf16[25,64,128]{2,1,0:T(8,128)(2,1)S(1)} %pad_maximum_fusion), channel_id=1, source_target_pairs={{0,1},{1,0},{2,3},{3,2},{4,5},{5,4},{6,7},{7,6},{8,9},{9,8},{10,11... | collective-permute-start | bytes 1228808 | tf_op jit(solution)/shard_map/ppermute | solution.py:92
  90.5 13.8 %copy-start.28 = (f32[24]{0:T(128)S(1)}, f32[24]{0:T(128)}, u32[]{:S(2)}) copy-start(f32[24]{0:T(128)} %get-tuple-element.14) | copy-start | bytes 292
  91.6 12.8 %collective-permute-start.3 = (bf16[25,64,128]{2,1,0:T(8,128)(2,1)}, bf16[25,64,128]{2,1,0:T(8,128)(2,1)S(1)}, u32[]{:S(2)}, u32[]{:S(2)}) collective-permute-start(bf16[25,64,128]{2,1,0:T(8,128)(2,1)} %pad_maximum_fusion.1), channel_id=1, source_target_pairs={{1,3},{3,5},{5,7},{7,9},{9,11},{11,13},{13,15},{2,0},{4,2},{6,4},{... | collective-permute-start | bytes 1228808 | tf_op jit(solution)/shard_map/ppermute | solution.py:92
  104.6 14.9 %collective-permute-start.4 = (bf16[25,64,128]{2,1,0:T(8,128)(2,1)S(1)}, bf16[25,64,128]{2,1,0:T(8,128)(2,1)S(1)}, u32[]{:S(2)}, u32[]{:S(2)}) collective-permute-start(bf16[25,64,128]{2,1,0:T(8,128)(2,1)S(1)} %pad_maximum_fusion.2), channel_id=1, source_target_pairs={{1,5},{3,7},{5,9},{7,11},{9,13},{11,15},{4,0},{6,2},{8,4},{10,6},{... | collective-permute-start | bytes 1228808 | tf_op jit(solution)/shard_map/ppermute | solution.py:92
  107.1 14.4 %copy-start.3 = (f32[1536,256]{1,0:T(8,128)S(1)}, f32[1536,256]{1,0:T(8,128)}, u32[]{:S(2)}) copy-start(f32[1536,256]{1,0:T(8,128)} %copy-done.2) | copy-start | bytes 4718596
  107.2 14.4 %copy-start.15 = (f32[24,256]{1,0:T(8,128)S(1)}, f32[24,256]{1,0:T(8,128)}, u32[]{:S(2)}) copy-start(f32[24,256]{1,0:T(8,128)} %copy-done.14) | copy-start | bytes 73732
  107.2 14.4 %copy-start.20 = (f32[24,256]{1,0:T(8,128)S(1)}, f32[24,256]{1,0:T(8,128)}, u32[]{:S(2)}) copy-start(f32[24,256]{1,0:T(8,128)} %copy-done.19) | copy-start | bytes 73732
  119.9 15.7 %copy-start.5 = (f32[1536,256]{1,0:T(8,128)S(1)}, f32[1536,256]{1,0:T(8,128)}, u32[]{:S(2)}) copy-start(f32[1536,256]{1,0:T(8,128)} %copy.47) | copy-start | bytes 4718596
  119.9 15.7 %copy-start.13 = (f32[24,256]{1,0:T(8,128)S(1)}, f32[24,256]{1,0:T(8,128)}, u32[]{:S(2)}) copy-start(f32[24,256]{1,0:T(8,128)} %copy-done.12) | copy-start | bytes 73732
  119.9 15.7 %copy-start.18 = (f32[24,256]{1,0:T(8,128)S(1)}, f32[24,256]{1,0:T(8,128)}, u32[]{:S(2)}) copy-start(f32[24,256]{1,0:T(8,128)} %copy-done.17) | copy-start | bytes 73732
  119.9 15.3 %collective-permute-start.5 = (bf16[25,64,128]{2,1,0:T(8,128)(2,1)S(1)}, bf16[25,64,128]{2,1,0:T(8,128)(2,1)S(1)}, u32[]{:S(2)}, u32[]{:S(2)}) collective-permute-start(bf16[25,64,128]{2,1,0:T(8,128)(2,1)S(1)} %pad_maximum_fusion.3), channel_id=1, source_target_pairs={{1,9},{3,11},{5,13},{7,15},{8,0},{10,2},{12,4},{14,6},{17,25},{19,... | collective-permute-start | bytes 1228808 | tf_op jit(solution)/shard_map/ppermute | solution.py:92
  135.6 4.0 %collective-permute-start.6 = (bf16[24,64,128]{2,1,0:T(8,128)(2,1)S(1)}, bf16[24,64,128]{2,1,0:T(8,128)(2,1)S(1)}, u32[]{:S(2)}, u32[]{:S(2)}) collective-permute-start(bf16[24,64,128]{2,1,0:T(8,128)(2,1)S(1)} %fusion.144), channel_id=1, source_target_pairs={{0,1},{1,0},{2,3},{3,2},{4,5},{5,4},{6,7},{7,6},{8,9},{9,8},{10,11... | collective-permute-start | bytes 1179656 | tf_op jit(solution)/shard_map/ppermute | solution.py:118
  (17 other events, 70.4 us)

commit v3 on v2

--- a/solution.py
+++ b/solution.py
@@ -43,13 +43,16 @@
     return tiles.astype(jnp.bfloat16)
 
 
-def halo(shard, width):
+def halo(normed, in_weight, width):
     size = lax.axis_size("seq")
     up = [(i, i + 1) for i in range(size - 1)]
     down = [(i + 1, i) for i in range(size - 1)]
-    before = lax.ppermute(shard[:, -width:].T, "seq", up).T
-    after = lax.ppermute(shard[:, :width].T, "seq", down).T
-    return jnp.concatenate([before, shard, after], axis=1)
+    before = lax.ppermute(normed[-width:], "seq", up)
+    after = lax.ppermute(normed[:width], "seq", down)
+    rows = jnp.concatenate([before, after], axis=0)
+    return lax.dot_general(
+        in_weight[:, E:], rows, (((0,), (1,)), ((), ())), preferred_element_type=jnp.float32
+    ).astype(jnp.bfloat16)
 
 
 def local_terms(activated, step_size, decay_rate, backward):
@@ -58,8 +61,12 @@
     write_map = activated[E : E + NS]
     read_map = activated[E + NS :]
     log_step = step_size * decay_rate[:, None]
-    log_decay = lax.cumsum(log_step, axis=1, reverse=backward)
     positions = jnp.arange(rows)
+    if backward:
+        upper = positions[:, None] >= positions[None, :]
+    else:
+        upper = positions[:, None] <= positions[None, :]
+    log_decay = jnp.dot(log_step, upper.astype(jnp.float32), precision=lax.Precision.HIGHEST)
     if backward:
         mask = positions[:, None] <= positions[None, :]
         edge = log_decay[:, :1]
@@ -150,7 +157,10 @@
     dt_raw = lax.dot_general(dt_weight, normed, turned, preferred_element_type=jnp.float32)
     gate_part = projected[:E].astype(jnp.float32)
     conv_input = projected[E:]
-    padded = halo(conv_input, KERNEL - 1).astype(jnp.float32)
+    sides = halo(normed, in_weight, KERNEL - 1)
+    padded = jnp.concatenate(
+        [sides[:, : KERNEL - 1], conv_input, sides[:, KERNEL - 1 :]], axis=1
+    ).astype(jnp.float32)
     parts = []
     for direction in range(2):
         summed = conv_bias[direction][:, None] + jnp.zeros((conv_input.shape[0], rows), jnp.float32)

time: 153 us -> 150 us (0.980)
  other arithmetic: 12.2 us -> 9.13 us
  waiting for transfers between devices: 70.5 us -> 68.2 us
  matrix products: 36 us -> 37.8 us
    another operation x8 -> x2, other arithmetic: 4.51 us -> 1.19 us
    ppermute x2, waiting for transfers between devices: 2.17 us -> 0.01 us  [the longest x1 0.01 us: halo(): before = lax.ppermute(normed[-width:], 'seq', up)]
  transfers between devices with their start and end apart: 8 -> 8, of which waited for: 6 -> 5; matrix products, arithmetic and copies ran while one was open for 7% -> 12% of each run, Pallas kernels for 0% -> 0%
where the time goes in v3:
time: 150 us
  waiting for transfers between devices  68.2 us (45%)
  matrix products  37.8 us (25%)
  starting transfers between devices  19.1 us (13%)
  local copies, waits for them, and re-layouts  13.9 us (9%)
  other arithmetic  9.13 us (6%)
  between operations  1.55 us (1%)
    ppermute x4, waiting for transfers between devices, transfer(): got = lax.ppermute(payload, 'seq', pairs)  34.9 us
    all_to_all x1, waiting for transfers between devices, route_tiles(): lax.all_to_all(send, 'seq', 0, 0, tiled=True)  33.3 us
    slice x4, local copies, waits for them, and re-layouts, local_terms(): signal = activated[:E].reshape(HEADS, HEAD_DIM, rows)  7.94 us
    dot_general x2, matrix products, local_terms(): lax.dot_general(signal, mixing, (((2,), (2,)), ((0,), (0,))), precision=f...  7.78 us
    all_to_all x1, starting transfers between devices, route_tiles(): lax.all_to_all(send, 'seq', 0, 0, tiled=True)  7.56 us
    dot_general x1, matrix products, per_device(): lax.dot_general(in_weight, normed, turned, preferred_element_type=jnp.flo...  7.47 us
    ppermute x4, starting transfers between devices, transfer(): got = lax.ppermute(payload, 'seq', pairs)  6.84 us
    dot_general x1, matrix products, per_device(): lax.dot_general(mixed, out_weight, (((0,), (0,)), ((), ())), preferred_el...  4.86 us
  transfers between devices with their start and end apart: 8, of which 5 were waited for; matrix products, arithmetic and copies ran while one was open for 12% of the time, Pallas kernels for 0%

profile of v3, /device:TPU:0, one launch (start us, length us, event | category | flops | bytes accessed | tf_op | source)
XLA Modules:
  0.0 149.7 jit_solution(12474882511443123707)
XLA Ops:
  3.1 3.8 %convolution_convert_fusion.1 = bf16[512,1664]{1,0:T(8,128)(2,1)} fusion(bf16[512,1]{1,0:T(8,128)(2,1)S(1)} %broadcast_in_dim.48, bf16[512,1536]{1,0:T(8,128)(2,1)} %param.14, s32[512]{0:T(512)S(1)} %add_select_fusion.2), kind=kOutput, calls=%fused_computation.30 | convolution fusion | flops 878641152 | bytes 3279872 | tf_op jit(solution)/shard_map/dot_general | solution.py:35
  6.8 7.6 %all-to-all-start = ((bf16[16,32,1664]{2,1,0:T(8,128)(2,1)}), bf16[16,32,1664]{2,1,0:T(8,128)(2,1)S(1)}, u32[]{:S(2)}, u32[]{:S(2)}) async-start(bf16[16,32,1664]{2,1,0:T(8,128)(2,1)} %bitcast.3), calls=%async_computation | async-start | bytes 3407872 | tf_op jit(solution)/shard_map/all_to_all | solution.py:37
  15.3 33.3 %all-to-all-done = bf16[16,32,1664]{2,1,0:T(8,128)(2,1)S(1)} async-done(((bf16[16,32,1664]{2,1,0:T(8,128)(2,1)}), bf16[16,32,1664]{2,1,0:T(8,128)(2,1)S(1)}, u32[]{:S(2)}, u32[]{:S(2)}) %all-to-all-start) | async-done | bytes 1703968 | tf_op jit(solution)/shard_map/all_to_all | solution.py:37
  48.7 4.2 %multiply_reduce_fusion.1 = (f32[256]{0:T(256)S(1)}, f32[256,1536]{1,0:T(8,128)S(1)}) fusion(f32[1536]{0:T(1024)S(1)} %copy-done.35, bf16[1536,1536]{1,0:T(8,128)(2,1)} %param.17, bf16[512,1664]{1,0:T(8,128)(2,1)S(1)} %bitcast.150, s32[512]{0:T(512)S(1)} %add_reduce_fusion), kind=kOutput, calls=%fused_computation.74 | convolution fusion | flops 1613102848 | bytes 7875584 | tf_op jit(solution)/shard_map/dot_general | solution.py:150
  54.8 2.9 %collective-permute-start = (bf16[3,1536]{1,0:T(4,128)(2,1)S(1)}, bf16[3,1536]{1,0:T(4,128)(2,1)S(1)}, u32[]{:S(2)}, u32[]{:S(2)}) collective-permute-start(bf16[3,1536]{1,0:T(4,128)(2,1)S(1)} %get-tuple-element.32), channel_id=1, source_target_pairs={{0,1},{1,2},{2,3},{3,4},{4,5},{5,6},{6,7},{7,8},{8,9},{9,10},{10,1... | collective-permute-start | bytes 27656 | tf_op jit(solution)/shard_map/ppermute | solution.py:50
  57.7 1.7 %collective-permute-start.1 = (bf16[3,1536]{1,0:T(4,128)(2,1)S(1)}, bf16[3,1536]{1,0:T(4,128)(2,1)S(1)}, u32[]{:S(2)}, u32[]{:S(2)}) collective-permute-start(bf16[3,1536]{1,0:T(4,128)(2,1)S(1)} %get-tuple-element.33), channel_id=1, source_target_pairs={{1,0},{2,1},{3,2},{4,3},{5,4},{6,5},{7,6},{8,7},{9,8},{10,9},{11,1... | collective-permute-start | bytes 27656 | tf_op jit(solution)/shard_map/ppermute | solution.py:51
  59.5 7.5 %fusion.14 = bf16[3328,256]{0,1:T(8,128)(2,1)S(1)} fusion(bf16[256,1536]{1,0:T(8,128)(2,1)S(1)} %multiply_convert_fusion.1, bf16[1536,3328]{1,0:T(8,128)(2,1)} %param.20), kind=kOutput, calls=%fused_computation.15 | convolution fusion | flops 2618097664 | bytes 12713984 | tf_op jit(solution)/shard_map/dot_general | solution.py:154
  69.6 2.3 %divide_multiply_fusion.1 = (f32[1792,256]{0,1:T(8,128)S(1)}, f32[1792,256]{0,1:T(8,128)S(1)}) fusion(f32[1792,262]{0,1:T(8,128)S(1)} %maximum_convert_fusion, f32[1792]{0:T(1024)S(1)} %copy-done.20, f32[1792]{0:T(1024)S(1)} %copy-done.21, f32[1792]{0:T(1024)S(1)} %copy-done.22, f32[1792]{0:T(1024)S(1)} %get-tuple-element.5, f32[1792]{0:T(1024)S(1)} %get-tuple-element.17, ...), kind=kLoop, calls=%fused_computation.56 | loop fusion | flops 11010048 | bytes 16586752 | tf_op jit(solution)/shard_map/jit(silu)/mul | solution.py:170
  74.6 1.9 %copy.36 = f32[1536,256]{1,0:T(8,128)S(1)} copy(f32[1536,256]{0,1:T(8,128)} %slice.213) | data formatting | bytes 3145728 | tf_op jit(solution)/shard_map/slice | solution.py:60
  76.5 1.6 %slice.219 = f32[1536,256]{0,1:T(8,128)} slice(f32[1792,256]{0,1:T(8,128)S(1)} %get-tuple-element.31), slice={[0:1536], [0:256]} | slice | bytes 3145728 | tf_op jit(solution)/shard_map/slice | solution.py:60
  78.0 3.1 %copy.37 = f32[1536,256]{1,0:T(8,128)} copy(f32[1536,256]{0,1:T(8,128)} %slice.219) | data formatting | bytes 3145728 | tf_op jit(solution)/shard_map/slice | solution.py:60
  81.1 1.8 %fusion.55 = f32[24,64,128]{2,1,0:T(8,128)S(1)} fusion(f32[24,64,256]{2,1,0:T(8,128)S(1)} %bitcast.142, f32[24,256]{1,0:T(8,128)} %get-tuple-element.37, f32[1792,256]{0,1:T(8,128)} %copy-done.1), kind=kOutput, calls=%fused_computation.69 | convolution fusion | flops 302383104 | bytes 2514944 | tf_op jit(solution)/shard_map/dot_general | solution.py:82
  83.9 2.5 %collective-permute-start.2 = (bf16[25,64,128]{2,1,0:T(8,128)(2,1)S(1)}, bf16[25,64,128]{2,1,0:T(8,128)(2,1)S(1)}, u32[]{:S(2)}, u32[]{:S(2)}) collective-permute-start(bf16[25,64,128]{2,1,0:T(8,128)(2,1)S(1)} %pad_maximum_fusion), channel_id=1, source_target_pairs={{0,1},{1,0},{2,3},{3,2},{4,5},{5,4},{6,7},{7,6},{8,9},{9,8},{10,11... | collective-permute-start | bytes 1228808 | tf_op jit(solution)/shard_map/ppermute | solution.py:99
  90.2 10.5 %collective-permute-done.3 = bf16[25,64,128]{2,1,0:T(8,128)(2,1)S(1)} collective-permute-done((bf16[25,64,128]{2,1,0:T(8,128)(2,1)}, bf16[25,64,128]{2,1,0:T(8,128)(2,1)S(1)}, u32[]{:S(2)}, u32[]{:S(2)}) %collective-permute-start.3) | collective-permute-done | bytes 409632 | tf_op jit(solution)/shard_map/ppermute | solution.py:99
  101.0 1.4 collective-permute-start.4
  103.9 12.7 %collective-permute-done.4 = bf16[25,64,128]{2,1,0:T(8,128)(2,1)S(1)} collective-permute-done((bf16[25,64,128]{2,1,0:T(8,128)(2,1)S(1)}, bf16[25,64,128]{2,1,0:T(8,128)(2,1)S(1)}, u32[]{:S(2)}, u32[]{:S(2)}) %collective-permute-start.4) | collective-permute-done | bytes 409632 | tf_op jit(solution)/shard_map/ppermute | solution.py:99
  117.0 1.6 %collective-permute-start.5 = (bf16[25,64,128]{2,1,0:T(8,128)(2,1)S(1)}, bf16[25,64,128]{2,1,0:T(8,128)(2,1)S(1)}, u32[]{:S(2)}, u32[]{:S(2)}) collective-permute-start(bf16[25,64,128]{2,1,0:T(8,128)(2,1)S(1)} %pad_maximum_fusion.3), channel_id=1, source_target_pairs={{1,9},{3,11},{5,13},{7,15},{8,0},{10,2},{12,4},{14,6},{17,25},{19,... | collective-permute-start | bytes 1228808 | tf_op jit(solution)/shard_map/ppermute | solution.py:99
  118.7 3.9 %fusion.6 = f32[24,64,256]{2,1,0:T(8,128)S(1)} fusion(f32[24,64,256]{2,1,0:T(8,128)S(1)} %bitcast.143, f32[24,256]{1,0:T(8,128)S(1)} %copy-done.14, f32[24,256]{1,0:T(8,128)S(1)} %copy-done.19, f32[256,256]{1,0:T(8,128)S(1)} %fusion.92, pred[256,256]{1,0:T(8,128)(4,1)S(1)} %iota_compare_fusion.7), kind=kOutput, calls=%fused_computation.6 | convolution fusion | flops 610271232 | bytes 3522560 | tf_op jit(solution)/shard_map/dot_general | solution.py:80
  122.6 10.4 %collective-permute-done.5 = bf16[25,64,128]{2,1,0:T(8,128)(2,1)S(1)} collective-permute-done((bf16[25,64,128]{2,1,0:T(8,128)(2,1)S(1)}, bf16[25,64,128]{2,1,0:T(8,128)(2,1)S(1)}, u32[]{:S(2)}, u32[]{:S(2)}) %collective-permute-start.5) | collective-permute-done | bytes 409632 | tf_op jit(solution)/shard_map/ppermute | solution.py:99
  133.5 3.9 %fusion = f32[24,64,256]{2,1,0:T(8,128)S(1)} fusion(f32[24,64,256]{2,1,0:T(8,128)S(1)} %bitcast.146, f32[24,256]{1,0:T(8,128)S(1)} %copy-done.12, f32[24,256]{1,0:T(8,128)S(1)} %copy-done.17, f32[256,256]{1,0:T(8,128)S(1)} %fusion.87, pred[256,256]{1,0:T(8,128)(4,1)S(1)} %iota_compare_fusion.6), kind=kOutput, calls=%fused_computation | convolution fusion | flops 610271232 | bytes 3522560 | tf_op jit(solution)/shard_map/dot_general | solution.py:80
  137.4 1.9 %fusion.67 = f32[24,64,256]{2,1,0:T(8,128)S(1)} fusion(bf16[24,64,128]{2,1,0:T(8,128)(2,1)S(1)} %collective-permute-done.6, f32[24]{0:T(128)S(1)} %bitcast.155, pred[]{:T(512)S(6)} %eq.69, bf16[25,64,128]{2,1,0:T(8,128)(2,1)S(1)} %collective-permute-done.2, f32[1792,256]{0,1:T(8,128)} %copy-done.1, bf16[25,64,128]{2,1,0:T(8,128)(2,1)S(1)} %collective-permute-done.5, ...), kind=kOutput, calls=%fused_computation.91 | convolution fusion | flops 304349184 | bytes 3671553 | tf_op jit(solution)/shard_map/dot_general | solution.py:181
  139.3 2.1 %multiply_add_fusion = f32[24,64,256]{2,1,0:T(8,128)} fusion(f32[24,64,256]{2,1,0:T(8,128)S(1)} %fusion, f32[24,64,256]{2,1,0:T(8,128)S(1)} %fusion.6, f32[24,64,256]{2,1,0:T(8,128)S(1)} %fusion.67, bf16[24,64,128]{2,1,0:T(8,128)(2,1)S(1)} %collective-permute-done.6, f32[24,256]{1,0:T(8,128)S(1)} %copy-done.10, f32[24,256]{1,0:T(8,128)S(1)} %get-tuple-element.36, ...), kind=kOutput, calls=%fused_computation.68 | convolution fusion | flops 306315264 | bytes 8439297 | tf_op jit(solution)/shard_map/dot_general | solution.py:181
  141.4 2.0 %copy.42 = f32[1536,256]{0,1:T(8,128)S(1)} copy(f32[1536,256]{1,0:T(8,128)} %bitcast.144) | data formatting | bytes 3145728 | tf_op jit(solution)/shard_map/reshape | solution.py:185
  144.9 4.9 %fusion.30 = bf16[256,1536]{1,0:T(8,128)(2,1)} fusion(f32[256,1536]{1,0:T(8,128)S(1)} %copy-done.9, bf16[1536,1536]{1,0:T(8,128)(2,1)} %param.27, f32[1536]{0:T(1024)S(1)} %copy-done.36, f32[256]{0:T(256)S(1)} %add_rsqrt_fusion, f32[1536,256]{0,1:T(8,128)S(1)} %copy.42, bf16[3328,256]{0,1:T(8,128)(2,1)S(1)} %copy-done.7), kind=kOutput, calls=%fused_computation.35 | convolution fusion | flops 1212284928 | bytes 9446400 | tf_op jit(solution)/shard_map/dot_general | solution.py:188
  (143 shorter events, 18.8 us)
Async XLA Ops:
  0.0 53.2 %copy-start = (bf16[1536,24]{0,1:T(8,128)(2,1)S(1)}, bf16[1536,24]{0,1:T(8,128)(2,1)}, u32[]{:S(2)}) copy-start(bf16[1536,24]{0,1:T(8,128)(2,1)} %param.21) | copy-start | bytes 221188
  6.8 41.9 %copy-start.35 = (f32[1536]{0:T(1024)S(1)}, f32[1536]{0:T(1024)}, u32[]{:S(2)}) copy-start(f32[1536]{0:T(1024)} %param.18) | copy-start | bytes 18436
  6.8 41.7 %all-to-all-start = ((bf16[16,32,1664]{2,1,0:T(8,128)(2,1)}), bf16[16,32,1664]{2,1,0:T(8,128)(2,1)S(1)}, u32[]{:S(2)}, u32[]{:S(2)}) async-start(bf16[16,32,1664]{2,1,0:T(8,128)(2,1)} %bitcast.3), calls=%async_computation | async-start | bytes 3407872 | tf_op jit(solution)/shard_map/all_to_all | solution.py:37
  53.0 14.0 %copy-start.8 = (f32[256,1536]{1,0:T(8,128)}, f32[256,1536]{1,0:T(8,128)S(1)}, u32[]{:S(2)}) copy-start(f32[256,1536]{1,0:T(8,128)S(1)} %get-tuple-element.51) | copy-start | bytes 4718596
  53.6 13.4 %copy-start.11 = (f32[24,256]{1,0:T(8,128)}, f32[24,256]{1,0:T(8,128)S(1)}, u32[]{:S(2)}) copy-start(f32[24,256]{1,0:T(8,128)S(1)} %get-tuple-element.41) | copy-start | bytes 73732
  53.6 13.4 %copy-start.13 = (f32[24,256]{1,0:T(8,128)}, f32[24,256]{1,0:T(8,128)S(1)}, u32[]{:S(2)}) copy-start(f32[24,256]{1,0:T(8,128)S(1)} %get-tuple-element.40) | copy-start | bytes 73732
  53.8 13.2 %copy-start.18 = (f32[24,256]{1,0:T(8,128)}, f32[24,256]{1,0:T(8,128)S(1)}, u32[]{:S(2)}) copy-start(f32[24,256]{1,0:T(8,128)S(1)} %fusion.97) | copy-start | bytes 73732
  54.0 13.0 %copy-start.16 = (f32[24,256]{1,0:T(8,128)}, f32[24,256]{1,0:T(8,128)S(1)}, u32[]{:S(2)}) copy-start(f32[24,256]{1,0:T(8,128)S(1)} %fusion.96) | copy-start | bytes 73732
  54.8 12.2 %copy-start.27 = (f32[24]{0:T(128)}, f32[24]{0:T(128)S(1)}, u32[]{:S(2)}) copy-start(f32[24]{0:T(128)S(1)} %get-tuple-element.15) | copy-start | bytes 292
  54.8 12.2 %copy-start.29 = (f32[24]{0:T(128)}, f32[24]{0:T(128)S(1)}, u32[]{:S(2)}) copy-start(f32[24]{0:T(128)S(1)} %get-tuple-element.16) | copy-start | bytes 292
  54.8 13.2 %collective-permute-start = (bf16[3,1536]{1,0:T(4,128)(2,1)S(1)}, bf16[3,1536]{1,0:T(4,128)(2,1)S(1)}, u32[]{:S(2)}, u32[]{:S(2)}) collective-permute-start(bf16[3,1536]{1,0:T(4,128)(2,1)S(1)} %get-tuple-element.32), channel_id=1, source_target_pairs={{0,1},{1,2},{2,3},{3,4},{4,5},{5,6},{6,7},{7,8},{8,9},{9,10},{10,1... | collective-permute-start | bytes 27656 | tf_op jit(solution)/shard_map/ppermute | solution.py:50
  57.7 10.3 %collective-permute-start.1 = (bf16[3,1536]{1,0:T(4,128)(2,1)S(1)}, bf16[3,1536]{1,0:T(4,128)(2,1)S(1)}, u32[]{:S(2)}, u32[]{:S(2)}) collective-permute-start(bf16[3,1536]{1,0:T(4,128)(2,1)S(1)} %get-tuple-element.33), channel_id=1, source_target_pairs={{1,0},{2,1},{3,2},{4,3},{5,4},{6,5},{7,6},{8,7},{9,8},{10,9},{11,1... | collective-permute-start | bytes 27656 | tf_op jit(solution)/shard_map/ppermute | solution.py:51
  83.9 3.9 %collective-permute-start.2 = (bf16[25,64,128]{2,1,0:T(8,128)(2,1)S(1)}, bf16[25,64,128]{2,1,0:T(8,128)(2,1)S(1)}, u32[]{:S(2)}, u32[]{:S(2)}) collective-permute-start(bf16[25,64,128]{2,1,0:T(8,128)(2,1)S(1)} %pad_maximum_fusion), channel_id=1, source_target_pairs={{0,1},{1,0},{2,3},{3,2},{4,5},{5,4},{6,7},{7,6},{8,9},{9,8},{10,11... | collective-permute-start | bytes 1228808 | tf_op jit(solution)/shard_map/ppermute | solution.py:99
  87.8 12.9 %copy-start.32 = (f32[24]{0:T(128)S(1)}, f32[24]{0:T(128)}, u32[]{:S(2)}) copy-start(f32[24]{0:T(128)} %get-tuple-element.14) | copy-start | bytes 292
  88.8 11.9 %collective-permute-start.3 = (bf16[25,64,128]{2,1,0:T(8,128)(2,1)}, bf16[25,64,128]{2,1,0:T(8,128)(2,1)S(1)}, u32[]{:S(2)}, u32[]{:S(2)}) collective-permute-start(bf16[25,64,128]{2,1,0:T(8,128)(2,1)} %pad_maximum_fusion.1), channel_id=1, source_target_pairs={{1,3},{3,5},{5,7},{7,9},{9,11},{11,13},{13,15},{2,0},{4,2},{6,4},{... | collective-permute-start | bytes 1228808 | tf_op jit(solution)/shard_map/ppermute | solution.py:99
  100.9 17.7 %copy-start.3 = (f32[1536,256]{1,0:T(8,128)S(1)}, f32[1536,256]{1,0:T(8,128)}, u32[]{:S(2)}) copy-start(f32[1536,256]{1,0:T(8,128)} %copy-done.2) | copy-start | bytes 4718596
  101.0 17.7 %copy-start.14 = (f32[24,256]{1,0:T(8,128)S(1)}, f32[24,256]{1,0:T(8,128)}, u32[]{:S(2)}) copy-start(f32[24,256]{1,0:T(8,128)} %copy-done.13) | copy-start | bytes 73732
  101.0 17.7 %copy-start.19 = (f32[24,256]{1,0:T(8,128)S(1)}, f32[24,256]{1,0:T(8,128)}, u32[]{:S(2)}) copy-start(f32[24,256]{1,0:T(8,128)} %copy-done.18) | copy-start | bytes 73732
  101.0 15.7 %collective-permute-start.4 = (bf16[25,64,128]{2,1,0:T(8,128)(2,1)S(1)}, bf16[25,64,128]{2,1,0:T(8,128)(2,1)S(1)}, u32[]{:S(2)}, u32[]{:S(2)}) collective-permute-start(bf16[25,64,128]{2,1,0:T(8,128)(2,1)S(1)} %pad_maximum_fusion.2), channel_id=1, source_target_pairs={{1,5},{3,7},{5,9},{7,11},{9,13},{11,15},{4,0},{6,2},{8,4},{10,6},{... | collective-permute-start | bytes 1228808 | tf_op jit(solution)/shard_map/ppermute | solution.py:99
  117.0 16.5 %copy-start.5 = (f32[1536,256]{1,0:T(8,128)S(1)}, f32[1536,256]{1,0:T(8,128)}, u32[]{:S(2)}) copy-start(f32[1536,256]{1,0:T(8,128)} %copy.37) | copy-start | bytes 4718596
  117.0 16.5 %copy-start.12 = (f32[24,256]{1,0:T(8,128)S(1)}, f32[24,256]{1,0:T(8,128)}, u32[]{:S(2)}) copy-start(f32[24,256]{1,0:T(8,128)} %copy-done.11) | copy-start | bytes 73732
  117.0 16.5 %copy-start.17 = (f32[24,256]{1,0:T(8,128)S(1)}, f32[24,256]{1,0:T(8,128)}, u32[]{:S(2)}) copy-start(f32[24,256]{1,0:T(8,128)} %copy-done.16) | copy-start | bytes 73732
  117.0 16.0 %collective-permute-start.5 = (bf16[25,64,128]{2,1,0:T(8,128)(2,1)S(1)}, bf16[25,64,128]{2,1,0:T(8,128)(2,1)S(1)}, u32[]{:S(2)}, u32[]{:S(2)}) collective-permute-start(bf16[25,64,128]{2,1,0:T(8,128)(2,1)S(1)} %pad_maximum_fusion.3), channel_id=1, source_target_pairs={{1,9},{3,11},{5,13},{7,15},{8,0},{10,2},{12,4},{14,6},{17,25},{19,... | collective-permute-start | bytes 1228808 | tf_op jit(solution)/shard_map/ppermute | solution.py:99
  133.4 4.0 %collective-permute-start.6 = (bf16[24,64,128]{2,1,0:T(8,128)(2,1)S(1)}, bf16[24,64,128]{2,1,0:T(8,128)(2,1)S(1)}, u32[]{:S(2)}, u32[]{:S(2)}) collective-permute-start(bf16[24,64,128]{2,1,0:T(8,128)(2,1)S(1)} %fusion.159), channel_id=1, source_target_pairs={{0,1},{1,0},{2,3},{3,2},{4,5},{5,4},{6,7},{7,6},{8,9},{9,8},{10,11... | collective-permute-start | bytes 1179656 | tf_op jit(solution)/shard_map/ppermute | solution.py:125
  (24 other events, 98.7 us)

commit v4 on v3

--- a/solution.py
+++ b/solution.py
@@ -102,7 +102,7 @@
     return got_decay, got[:heads].astype(jnp.float32)
 
 
-def exchange(forward, backward):
+def exchange(forward, backward, ties):
     size, me = lax.axis_size("seq"), lax.axis_index("seq")
     chips, chip, is_one = size // 2, me // 2, me % 2 == 1
     swap = [(2 * k + d, 2 * k + 1 - d) for k in range(chips) for d in range(2)]
@@ -111,8 +111,12 @@
     first = transfer(pick(backward, forward), swap)
     run = combine(first, mine)
     done = (jnp.ones_like(mine[0]), jnp.zeros_like(mine[1]))
-    shift = 1
+    shift, level, tied = 1, 0, []
     while shift < chips:
+        if level < len(ties) and ties[level] is not None:
+            run, held = lax.optimization_barrier((run, ties[level]))
+            tied.append(held)
+        level += 1
         pairs = [(2 * k + 1, 2 * (k + shift) + 1) for k in range(chips - shift)]
         pairs += [(2 * (k + shift), 2 * k) for k in range(chips - shift)]
         valid = jnp.where(is_one, chip >= shift, chip + shift < chips)
@@ -124,7 +128,7 @@
         shift *= 2
     other = lax.ppermute(done[1].astype(jnp.bfloat16), "seq", swap).astype(jnp.float32)
     mine_in = first[0][:, None, None] * done[1] + first[1]
-    return jnp.where(is_one, mine_in, other), jnp.where(is_one, other, mine_in)
+    return jnp.where(is_one, mine_in, other), jnp.where(is_one, other, mine_in), tied
 
 
 def per_device(
@@ -151,12 +155,14 @@
     ).astype(jnp.bfloat16)
     normed = rms_scale(embedded.astype(jnp.float32), norm_gain).astype(jnp.bfloat16)
     turned = (((0,), (1,)), ((), ()))
-    projected = lax.dot_general(
-        in_weight, normed, turned, preferred_element_type=jnp.float32
+    conv_input = lax.dot_general(
+        in_weight[:, E:], normed, turned, preferred_element_type=jnp.float32
     ).astype(jnp.bfloat16)
     dt_raw = lax.dot_general(dt_weight, normed, turned, preferred_element_type=jnp.float32)
-    gate_part = projected[:E].astype(jnp.float32)
-    conv_input = projected[E:]
+    gate_part = lax.dot_general(
+        in_weight[:, :E], normed, turned, preferred_element_type=jnp.float32
+    ).astype(jnp.bfloat16).astype(jnp.float32)
+    gate_silu = jax.nn.silu(gate_part)
     sides = halo(normed, in_weight, KERNEL - 1)
     padded = jnp.concatenate(
         [sides[:, : KERNEL - 1], conv_input, sides[:, KERNEL - 1 :]], axis=1
@@ -171,18 +177,27 @@
         step_size = jax.nn.softplus(dt_raw + dt_bias[direction][:, None])
         decay_rate = -jnp.exp(a_log[direction])
         parts.append(local_terms(activated, step_size, decay_rate, direction == 1))
-    incomings = exchange(
-        (parts[0][2], parts[0][1]), (parts[1][2], parts[1][1])
-    )
+    fwd_in, bwd_in, tied = exchange(
+        (parts[0][2], parts[0][1]),
+        (parts[1][2], parts[1][1]),
+        [None, (gate_silu, parts[0][0]), parts[1][0]],
+    )
+    if len(tied) == 2:
+        (gate_silu, within_fwd), within_bwd = tied
+    else:
+        within_fwd, within_bwd = parts[0][0], parts[1][0]
+    incomings = (fwd_in, bwd_in)
+    withins = (within_fwd, within_bwd)
     total = jnp.zeros((HEADS, HEAD_DIM, rows), jnp.float32)
     for direction in range(2):
-        within, own_state, device_decay, decay_to, read_map = parts[direction]
+        _, own_state, device_decay, decay_to, read_map = parts[direction]
+        within = withins[direction]
         incoming = incomings[direction]
         carried = lax.dot_general(
             incoming, read_map, (((2,), (0,)), ((), ())), precision=fast
         ) * decay_to[:, None, :]
         total = total + within + carried
-    gated = total.reshape(E, rows) * jax.nn.silu(gate_part)
+    gated = total.reshape(E, rows) * gate_silu
     mean_sq = jnp.mean(gated * gated, axis=0, keepdims=True)
     mixed = (gated * lax.rsqrt(mean_sq + epsilon) * out_gain[:, None]).astype(jnp.bfloat16)
     hidden = embedded.astype(jnp.float32) + lax.dot_general(

time: 150 us -> 147 us (0.980)
  local copies, waits for them, and re-layouts: 13.9 us -> 8.73 us
  other arithmetic: 9.13 us -> 12.8 us
  waiting for transfers between devices: 68.2 us -> 66.6 us
    ppermute x4, waiting for transfers between devices: 34.9 us -> 30.4 us  [transfer(): got = lax.ppermute(payload, 'seq', pairs)]
    ppermute x1, waiting for transfers between devices: 0.01 us -> 2.48 us  [halo(): after = lax.ppermute(normed[:width], 'seq', down)]
    unnamed x80 -> x66, local copies, waits for them, and re-layouts: 2.75 us -> 0.7 us
    dot_general x1 -> x2, matrix products: 7.47 us -> 9.41 us  [the longest x1 5.12 us: per_device(): lax.dot_general(in_weight[:, :E], normed, turned, preferred_element_type=...]
    ppermute x1, waiting for transfers between devices: 0.01 us -> 1.71 us  [exchange(): lax.ppermute(done[1].astype(jnp.bfloat16), 'seq', swap).astype(jnp.float32)]
    slice x4, local copies, waits for them, and re-layouts: 7.94 us -> 6.39 us  [local_terms(): signal = activated[:E].reshape(HEADS, HEAD_DIM, rows)]
    reshape x1, local copies, waits for them, and re-layouts: 2 us -> 0.47 us  [per_device(): gated = total.reshape(E, rows) * gate_silu]
  transfers between devices with their start and end apart: 8 -> 8, of which waited for: 5 -> 6; matrix products, arithmetic and copies ran while one was open for 12% -> 8% of each run, Pallas kernels for 0% -> 0%
where the time goes in v4:
time: 147 us
  waiting for transfers between devices  66.6 us (45%)
  matrix products  38.4 us (26%)
  starting transfers between devices  18.6 us (13%)
  other arithmetic  12.8 us (9%)
  local copies, waits for them, and re-layouts  8.73 us (6%)
    all_to_all x1, waiting for transfers between devices, route_tiles(): lax.all_to_all(send, 'seq', 0, 0, tiled=True)  32 us
    ppermute x4, waiting for transfers between devices, transfer(): got = lax.ppermute(payload, 'seq', pairs)  30.4 us
    dot_general x2, matrix products, local_terms(): lax.dot_general(signal, mixing, (((2,), (2,)), ((0,), (0,))), precision=f...  7.79 us
    all_to_all x1, starting transfers between devices, route_tiles(): lax.all_to_all(send, 'seq', 0, 0, tiled=True)  7.56 us
    ppermute x4, starting transfers between devices, transfer(): got = lax.ppermute(payload, 'seq', pairs)  6.61 us
    slice x4, local copies, waits for them, and re-layouts, local_terms(): signal = activated[:E].reshape(HEADS, HEAD_DIM, rows)  6.39 us
    dot_general x1, matrix products, per_device(): lax.dot_general(in_weight[:, :E], normed, turned, preferred_element_type=...  5.12 us
    dot_general x1, matrix products, per_device(): lax.dot_general(mixed, out_weight, (((0,), (0,)), ((), ())), preferred_el...  4.66 us
  transfers between devices with their start and end apart: 8, of which 6 were waited for; matrix products, arithmetic and copies ran while one was open for 8% of the time, Pallas kernels for 0%

profile of v4, /device:TPU:0, one launch (start us, length us, event | category | flops | bytes accessed | tf_op | source)
XLA Modules:
  0.0 146.5 jit_solution(3596181637784204346)
XLA Ops:
  3.1 3.7 %convolution_convert_fusion = bf16[512,1664]{1,0:T(8,128)(2,1)} fusion(bf16[512,1]{1,0:T(8,128)(2,1)S(1)} %broadcast_in_dim.48, bf16[512,1536]{1,0:T(8,128)(2,1)} %param.14, s32[512]{0:T(512)S(1)} %add_select_fusion.2), kind=kOutput, calls=%fused_computation.32 | convolution fusion | flops 878641152 | bytes 3279872 | tf_op jit(solution)/shard_map/dot_general | solution.py:35
  6.8 7.6 %all-to-all-start = ((bf16[16,32,1664]{2,1,0:T(8,128)(2,1)}), bf16[16,32,1664]{2,1,0:T(8,128)(2,1)S(1)}, u32[]{:S(2)}, u32[]{:S(2)}) async-start(bf16[16,32,1664]{2,1,0:T(8,128)(2,1)} %bitcast.3), calls=%async_computation | async-start | bytes 3407872 | tf_op jit(solution)/shard_map/all_to_all | solution.py:37
  16.5 32.0 %all-to-all-done = bf16[16,32,1664]{2,1,0:T(8,128)(2,1)S(1)} async-done(((bf16[16,32,1664]{2,1,0:T(8,128)(2,1)}), bf16[16,32,1664]{2,1,0:T(8,128)(2,1)S(1)}, u32[]{:S(2)}, u32[]{:S(2)}) %all-to-all-start) | async-done | bytes 1703968 | tf_op jit(solution)/shard_map/all_to_all | solution.py:37
  48.7 4.2 %multiply_reduce_fusion.1 = (f32[256]{0:T(256)S(1)}, f32[256,1536]{1,0:T(8,128)S(1)}) fusion(f32[1536]{0:T(1024)S(1)} %copy-done.28, bf16[1536,1536]{1,0:T(8,128)(2,1)} %param.17, bf16[512,1664]{1,0:T(8,128)(2,1)S(1)} %bitcast.150, s32[512]{0:T(512)S(1)} %add_reduce_fusion), kind=kOutput, calls=%fused_computation.76 | convolution fusion | flops 1613102848 | bytes 7875584 | tf_op jit(solution)/shard_map/dot_general | solution.py:154
  56.0 4.3 %fusion.46 = bf16[1792,256]{0,1:T(8,128)(2,1)S(1)} fusion(bf16[256,1536]{1,0:T(8,128)(2,1)S(1)} %multiply_convert_fusion.1, bf16[1536,3328]{1,0:T(8,128)(2,1)} %param.20), kind=kOutput, calls=%fused_computation.43 | convolution fusion | flops 1409744896 | bytes 7208960 | tf_op jit(solution)/shard_map/dot_general | solution.py:158
  60.3 5.1 %divide_multiply_fusion.2 = f32[1536,256]{0,1:T(8,128)} fusion(bf16[256,1536]{1,0:T(8,128)(2,1)S(1)} %multiply_convert_fusion.1, bf16[1536,3328]{1,0:T(8,128)(2,1)} %param.20), kind=kOutput, calls=%fused_computation.70 | convolution fusion | flops 1210318848 | bytes 7077888 | tf_op jit(solution)/shard_map/dot_general | solution.py:162
  65.5 2.9 %collective-permute-start = (bf16[3,1536]{1,0:T(4,128)(2,1)S(1)}, bf16[3,1536]{1,0:T(4,128)(2,1)S(1)}, u32[]{:S(2)}, u32[]{:S(2)}) collective-permute-start(bf16[3,1536]{1,0:T(4,128)(2,1)S(1)} %get-tuple-element.44), channel_id=1, source_target_pairs={{0,1},{1,2},{2,3},{3,4},{4,5},{5,6},{6,7},{7,8},{8,9},{9,10},{10,1... | collective-permute-start | bytes 27656 | tf_op jit(solution)/shard_map/ppermute | solution.py:50
  70.4 2.5 %collective-permute-done.1 = bf16[3,1536]{1,0:T(4,128)(2,1)S(1)} collective-permute-done((bf16[3,1536]{1,0:T(4,128)(2,1)S(1)}, bf16[3,1536]{1,0:T(4,128)(2,1)S(1)}, u32[]{:S(2)}, u32[]{:S(2)}) %collective-permute-start.1) | collective-permute-done | bytes 9248 | tf_op jit(solution)/shard_map/ppermute | solution.py:51
  74.5 3.3 %divide_multiply_fusion = (f32[1792,256]{0,1:T(8,128)}, f32[1792,256]{0,1:T(8,128)S(1)}) fusion(f32[1792,262]{0,1:T(8,128)S(1)} %maximum_convert_fusion, f32[1792]{0:T(1024)S(1)} %copy-done.20, f32[1792]{0:T(1024)S(1)} %copy-done.21, f32[1792]{0:T(1024)S(1)} %get-tuple-element.20, f32[1792]{0:T(1024)S(1)} %get-tuple-element.19, ...), kind=kLoop, calls=%fused_computation.60 | loop fusion | flops 11010048 | bytes 16586752 | tf_op jit(solution)/shard_map/jit(silu)/mul | solution.py:176
  78.0 1.7 %copy.36 = f32[1536,256]{1,0:T(8,128)} copy(f32[1536,256]{0,1:T(8,128)S(1)} %slice.211) | data formatting | bytes 3145728 | tf_op jit(solution)/shard_map/slice | solution.py:60
  79.6 2.7 %slice.216 = f32[1536,256]{0,1:T(8,128)} slice(f32[1792,256]{0,1:T(8,128)} %get-tuple-element.42), slice={[0:1536], [0:256]} | slice | bytes 3145728 | tf_op jit(solution)/shard_map/slice | solution.py:60
  82.3 1.9 %copy.38 = f32[1536,256]{1,0:T(8,128)S(1)} copy(f32[1536,256]{0,1:T(8,128)} %slice.216) | data formatting | bytes 3145728 | tf_op jit(solution)/shard_map/slice | solution.py:60
  84.2 1.8 %fusion.71 = f32[24,64,128]{2,1,0:T(8,128)S(1)} fusion(f32[24,64,256]{2,1,0:T(8,128)S(1)} %bitcast.142, f32[24,256]{1,0:T(8,128)} %get-tuple-element.49, f32[1792,256]{0,1:T(8,128)} %get-tuple-element.42), kind=kOutput, calls=%fused_computation.71 | convolution fusion | flops 302383104 | bytes 2514944 | tf_op jit(solution)/shard_map/dot_general | solution.py:82
  86.9 2.5 %collective-permute-start.2 = (bf16[25,64,128]{2,1,0:T(8,128)(2,1)S(1)}, bf16[25,64,128]{2,1,0:T(8,128)(2,1)S(1)}, u32[]{:S(2)}, u32[]{:S(2)}) collective-permute-start(bf16[25,64,128]{2,1,0:T(8,128)(2,1)S(1)} %pad_maximum_fusion), channel_id=1, source_target_pairs={{0,1},{1,0},{2,3},{3,2},{4,5},{5,4},{6,7},{7,6},{8,9},{9,8},{10,11... | collective-permute-start | bytes 1228808 | tf_op jit(solution)/shard_map/ppermute | solution.py:99
  92.7 3.9 %fusion.6 = f32[24,64,256]{2,1,0:T(8,128)S(1)} fusion(f32[24,64,256]{2,1,0:T(8,128)S(1)} %bitcast.143, f32[24,256]{1,0:T(8,128)S(1)} %copy-done.7, f32[24,256]{1,0:T(8,128)S(1)} %copy-done.15, f32[256,256]{1,0:T(8,128)S(1)} %fusion.104, pred[256,256]{1,0:T(8,128)(4,1)S(1)} %copy-done.10), kind=kOutput, calls=%fused_computation.6 | convolution fusion | flops 610271232 | bytes 3522560 | tf_op jit(solution)/shard_map/dot_general | solution.py:80
  96.6 7.3 %collective-permute-done.3 = bf16[25,64,128]{2,1,0:T(8,128)(2,1)S(1)} collective-permute-done((bf16[25,64,128]{2,1,0:T(8,128)(2,1)S(1)}, bf16[25,64,128]{2,1,0:T(8,128)(2,1)S(1)}, u32[]{:S(2)}, u32[]{:S(2)}) %collective-permute-start.3) | collective-permute-done | bytes 409632 | tf_op jit(solution)/shard_map/ppermute | solution.py:99
  104.4 1.5 %collective-permute-start.4 = (bf16[25,64,128]{2,1,0:T(8,128)(2,1)S(1)}, bf16[25,64,128]{2,1,0:T(8,128)(2,1)S(1)}, u32[]{:S(2)}, u32[]{:S(2)}) collective-permute-start(bf16[25,64,128]{2,1,0:T(8,128)(2,1)S(1)} %pad_maximum_fusion.2), channel_id=1, source_target_pairs={{1,5},{3,7},{5,9},{7,11},{9,13},{11,15},{4,0},{6,2},{8,4},{10,6},{... | collective-permute-start | bytes 1228808 | tf_op jit(solution)/shard_map/ppermute | solution.py:99
  105.9 3.9 %fusion = f32[24,64,256]{2,1,0:T(8,128)S(1)} fusion(f32[24,64,256]{2,1,0:T(8,128)S(1)} %bitcast.146, f32[24,256]{1,0:T(8,128)S(1)} %copy-done.5, f32[24,256]{1,0:T(8,128)S(1)} %copy-done.13, f32[256,256]{1,0:T(8,128)S(1)} %fusion.101, pred[256,256]{1,0:T(8,128)(4,1)S(1)} %copy-done.9), kind=kOutput, calls=%fused_computation | convolution fusion | flops 610271232 | bytes 3522560 | tf_op jit(solution)/shard_map/dot_general | solution.py:80
  109.8 9.3 %collective-permute-done.4 = bf16[25,64,128]{2,1,0:T(8,128)(2,1)S(1)} collective-permute-done((bf16[25,64,128]{2,1,0:T(8,128)(2,1)S(1)}, bf16[25,64,128]{2,1,0:T(8,128)(2,1)S(1)}, u32[]{:S(2)}, u32[]{:S(2)}) %collective-permute-start.4) | collective-permute-done | bytes 409632 | tf_op jit(solution)/shard_map/ppermute | solution.py:99
  120.6 13.8 %collective-permute-done.5 = bf16[25,64,128]{2,1,0:T(8,128)(2,1)S(1)} collective-permute-done((bf16[25,64,128]{2,1,0:T(8,128)(2,1)S(1)}, bf16[25,64,128]{2,1,0:T(8,128)(2,1)S(1)}, u32[]{:S(2)}, u32[]{:S(2)}) %collective-permute-start.5) | collective-permute-done | bytes 409632 | tf_op jit(solution)/shard_map/ppermute | solution.py:99
  134.9 1.7 %collective-permute-done.6 = bf16[24,64,128]{2,1,0:T(8,128)(2,1)S(1)} collective-permute-done((bf16[24,64,128]{2,1,0:T(8,128)(2,1)S(1)}, bf16[24,64,128]{2,1,0:T(8,128)(2,1)S(1)}, u32[]{:S(2)}, u32[]{:S(2)}) %collective-permute-start.6) | collective-permute-done | bytes 393248 | tf_op jit(solution)/shard_map/ppermute | solution.py:129
  136.6 1.9 %fusion.82 = f32[24,64,256]{2,1,0:T(8,128)S(1)} fusion(bf16[24,64,128]{2,1,0:T(8,128)(2,1)S(1)} %collective-permute-done.6, f32[24]{0:T(128)S(1)} %bitcast.152, pred[]{:T(512)S(6)} %eq.69, bf16[25,64,128]{2,1,0:T(8,128)(2,1)S(1)} %collective-permute-done.2, f32[1792,256]{0,1:T(8,128)} %get-tuple-element.42, ...), kind=kOutput, calls=%fused_computation.92 | convolution fusion | flops 304349184 | bytes 3671553 | tf_op jit(solution)/shard_map/dot_general | solution.py:196
  140.0 1.9 %multiply_reduce_fusion = (f32[256]{0:T(256)S(1)}, f32[1536,256]{0,1:T(8,128)S(1)}) fusion(f32[1536,256]{0,1:T(8,128)S(1)} %copy.42, f32[1536,256]{0,1:T(8,128)} %divide_multiply_fusion.2), kind=kLoop, calls=%fused_computation.68 | loop fusion | flops 1179392 | bytes 4719616 | tf_op jit(solution)/shard_map/reduce_sum | solution.py:201
  141.9 4.7 %fusion.33 = bf16[256,1536]{1,0:T(8,128)(2,1)} fusion(f32[256,1536]{1,0:T(8,128)S(1)} %copy-done.3, bf16[1536,1536]{1,0:T(8,128)(2,1)} %param.27, f32[1536,256]{0,1:T(8,128)S(1)} %get-tuple-element.34, f32[1536]{0:T(1024)S(1)} %copy-done.29, f32[256]{0:T(256)S(1)} %add_rsqrt_fusion), kind=kOutput, calls=%fused_computation.37 | convolution fusion | flops 1209925632 | bytes 8657920 | tf_op jit(solution)/shard_map/dot_general | solution.py:203
  (130 shorter events, 19.3 us)
Async XLA Ops:
  0.0 53.2 %copy-start = (bf16[1536,24]{0,1:T(8,128)(2,1)S(1)}, bf16[1536,24]{0,1:T(8,128)(2,1)}, u32[]{:S(2)}) copy-start(bf16[1536,24]{0,1:T(8,128)(2,1)} %param.21) | copy-start | bytes 221188
  6.8 8.9 %copy-start.22 = (f32[2,1792]{1,0:T(2,128)S(1)}, f32[2,1792]{1,0:T(2,128)}, u32[]{:S(2)}) copy-start(f32[2,1792]{1,0:T(2,128)} %param.23) | copy-start | bytes 43012
  6.8 9.0 %copy-start.11 = (f32[2,4,1792]{2,1,0:T(4,128)S(1)}, f32[2,4,1792]{2,1,0:T(4,128)}, u32[]{:S(2)}) copy-start(f32[2,4,1792]{2,1,0:T(4,128)} %param.22) | copy-start | bytes 172036
  6.8 9.7 %copy-start.26 = (f32[2,24]{1,0:T(2,128)S(1)}, f32[2,24]{1,0:T(2,128)}, u32[]{:S(2)}) copy-start(f32[2,24]{1,0:T(2,128)} %param.24) | copy-start | bytes 580
  6.8 9.7 %copy-start.27 = (f32[2,24]{1,0:T(2,128)S(1)}, f32[2,24]{1,0:T(2,128)}, u32[]{:S(2)}) copy-start(f32[2,24]{1,0:T(2,128)} %param.25) | copy-start | bytes 580
  6.8 41.9 %copy-start.28 = (f32[1536]{0:T(1024)S(1)}, f32[1536]{0:T(1024)}, u32[]{:S(2)}) copy-start(f32[1536]{0:T(1024)} %param.18) | copy-start | bytes 18436
  6.8 41.7 %all-to-all-start = ((bf16[16,32,1664]{2,1,0:T(8,128)(2,1)}), bf16[16,32,1664]{2,1,0:T(8,128)(2,1)S(1)}, u32[]{:S(2)}, u32[]{:S(2)}) async-start(bf16[16,32,1664]{2,1,0:T(8,128)(2,1)} %bitcast.3), calls=%async_computation | async-start | bytes 3407872 | tf_op jit(solution)/shard_map/all_to_all | solution.py:37
  48.7 4.3 %copy-start.23 = (f32[1536]{0:T(1024)S(1)}, f32[1536]{0:T(1024)}, u32[]{:S(2)}) copy-start(f32[1536]{0:T(1024)} %param.19) | copy-start | bytes 18436
  53.5 6.7 %copy-start.4 = (f32[24,256]{1,0:T(8,128)}, f32[24,256]{1,0:T(8,128)S(1)}, u32[]{:S(2)}) copy-start(f32[24,256]{1,0:T(8,128)S(1)} %get-tuple-element.52) | copy-start | bytes 73732
  53.6 6.7 %copy-start.6 = (f32[24,256]{1,0:T(8,128)}, f32[24,256]{1,0:T(8,128)S(1)}, u32[]{:S(2)}) copy-start(f32[24,256]{1,0:T(8,128)S(1)} %get-tuple-element.53) | copy-start | bytes 73732
  53.8 6.5 %copy-start.12 = (f32[24,256]{1,0:T(8,128)}, f32[24,256]{1,0:T(8,128)S(1)}, u32[]{:S(2)}) copy-start(f32[24,256]{1,0:T(8,128)S(1)} %fusion.111) | copy-start | bytes 73732
  54.0 6.3 %copy-start.14 = (f32[24,256]{1,0:T(8,128)}, f32[24,256]{1,0:T(8,128)S(1)}, u32[]{:S(2)}) copy-start(f32[24,256]{1,0:T(8,128)S(1)} %fusion.110) | copy-start | bytes 73732
  56.0 16.9 %slice-start = ((s8[10223616]{0:T(1024)(128)(4,1)}), s8[4194304]{0:T(1024)(128)(4,1)S(1)}, s32[]{:S(2)}) async-start(s8[10223616]{0:T(1024)(128)(4,1)} %bitcast.147), calls=%async_computation.1 | async-start | bytes 8388608
  56.0 16.9 %slice-start.1 = ((s8[10223616]{0:T(1024)(128)(4,1)}), s8[4194304]{0:T(1024)(128)(4,1)S(1)}, s32[]{:S(2)}) async-start(s8[10223616]{0:T(1024)(128)(4,1)} %bitcast.147), calls=%async_computation.2 | async-start | bytes 8388608
  60.3 12.6 %slice-start.2 = ((s8[10223616]{0:T(1024)(128)(4,1)}), s8[1835008]{0:T(1024)(128)(4,1)S(1)}, s32[]{:S(2)}) async-start(s8[10223616]{0:T(1024)(128)(4,1)} %bitcast.147), calls=%async_computation.3 | async-start | bytes 3670016
  65.5 5.0 %collective-permute-start = (bf16[3,1536]{1,0:T(4,128)(2,1)S(1)}, bf16[3,1536]{1,0:T(4,128)(2,1)S(1)}, u32[]{:S(2)}, u32[]{:S(2)}) collective-permute-start(bf16[3,1536]{1,0:T(4,128)(2,1)S(1)} %get-tuple-element.44), channel_id=1, source_target_pairs={{0,1},{1,2},{2,3},{3,4},{4,5},{5,6},{6,7},{7,8},{8,9},{9,10},{10,1... | collective-permute-start | bytes 27656 | tf_op jit(solution)/shard_map/ppermute | solution.py:50
  68.3 4.6 %collective-permute-start.1 = (bf16[3,1536]{1,0:T(4,128)(2,1)S(1)}, bf16[3,1536]{1,0:T(4,128)(2,1)S(1)}, u32[]{:S(2)}, u32[]{:S(2)}) collective-permute-start(bf16[3,1536]{1,0:T(4,128)(2,1)S(1)} %get-tuple-element.45), channel_id=1, source_target_pairs={{1,0},{2,1},{3,2},{4,3},{5,4},{6,5},{7,6},{8,7},{9,8},{10,9},{11,1... | collective-permute-start | bytes 27656 | tf_op jit(solution)/shard_map/ppermute | solution.py:51
  86.8 4.2 %copy-start.25 = (f32[24]{0:T(128)S(1)}, f32[24]{0:T(128)}, u32[]{:S(2)}) copy-start(f32[24]{0:T(128)} %get-tuple-element.28) | copy-start | bytes 292
  86.8 4.2 %copy-start.24 = (f32[24]{0:T(128)S(1)}, f32[24]{0:T(128)}, u32[]{:S(2)}) copy-start(f32[24]{0:T(128)} %broadcast_select_fusion.1) | copy-start | bytes 292
  86.9 4.1 %collective-permute-start.2 = (bf16[25,64,128]{2,1,0:T(8,128)(2,1)S(1)}, bf16[25,64,128]{2,1,0:T(8,128)(2,1)S(1)}, u32[]{:S(2)}, u32[]{:S(2)}) collective-permute-start(bf16[25,64,128]{2,1,0:T(8,128)(2,1)S(1)} %pad_maximum_fusion), channel_id=1, source_target_pairs={{0,1},{1,0},{2,3},{3,2},{4,5},{5,4},{6,7},{7,6},{8,9},{9,8},{10,11... | collective-permute-start | bytes 1228808 | tf_op jit(solution)/shard_map/ppermute | solution.py:99
  91.4 12.6 %collective-permute-start.3 = (bf16[25,64,128]{2,1,0:T(8,128)(2,1)S(1)}, bf16[25,64,128]{2,1,0:T(8,128)(2,1)S(1)}, u32[]{:S(2)}, u32[]{:S(2)}) collective-permute-start(bf16[25,64,128]{2,1,0:T(8,128)(2,1)S(1)} %pad_maximum_fusion.1), channel_id=1, source_target_pairs={{1,3},{3,5},{5,7},{7,9},{9,11},{11,13},{13,15},{2,0},{4,2},{6,4},{... | collective-permute-start | bytes 1228808 | tf_op jit(solution)/shard_map/ppermute | solution.py:99
  104.4 14.7 %collective-permute-start.4 = (bf16[25,64,128]{2,1,0:T(8,128)(2,1)S(1)}, bf16[25,64,128]{2,1,0:T(8,128)(2,1)S(1)}, u32[]{:S(2)}, u32[]{:S(2)}) collective-permute-start(bf16[25,64,128]{2,1,0:T(8,128)(2,1)S(1)} %pad_maximum_fusion.2), channel_id=1, source_target_pairs={{1,5},{3,7},{5,9},{7,11},{9,13},{11,15},{4,0},{6,2},{8,4},{10,6},{... | collective-permute-start | bytes 1228808 | tf_op jit(solution)/shard_map/ppermute | solution.py:99
  119.3 15.1 %collective-permute-start.5 = (bf16[25,64,128]{2,1,0:T(8,128)(2,1)S(1)}, bf16[25,64,128]{2,1,0:T(8,128)(2,1)S(1)}, u32[]{:S(2)}, u32[]{:S(2)}) collective-permute-start(bf16[25,64,128]{2,1,0:T(8,128)(2,1)S(1)} %pad_maximum_fusion.3), channel_id=1, source_target_pairs={{1,9},{3,11},{5,13},{7,15},{8,0},{10,2},{12,4},{14,6},{17,25},{19,... | collective-permute-start | bytes 1228808 | tf_op jit(solution)/shard_map/ppermute | solution.py:99
  134.8 1.8 %collective-permute-start.6 = (bf16[24,64,128]{2,1,0:T(8,128)(2,1)S(1)}, bf16[24,64,128]{2,1,0:T(8,128)(2,1)S(1)}, u32[]{:S(2)}, u32[]{:S(2)}) collective-permute-start(bf16[24,64,128]{2,1,0:T(8,128)(2,1)S(1)} %fusion.174), channel_id=1, source_target_pairs={{0,1},{1,0},{2,3},{3,2},{4,5},{5,4},{6,7},{7,6},{8,9},{9,8},{10,11... | collective-permute-start | bytes 1179656 | tf_op jit(solution)/shard_map/ppermute | solution.py:129
  (17 other events, 28.2 us)

commit v5 on v4

--- a/solution.py
+++ b/solution.py
@@ -102,13 +102,17 @@
     return got_decay, got[:heads].astype(jnp.float32)
 
 
-def exchange(forward, backward, ties):
+def exchange(forward, backward, ties, late, late_input):
     size, me = lax.axis_size("seq"), lax.axis_index("seq")
     chips, chip, is_one = size // 2, me // 2, me % 2 == 1
     swap = [(2 * k + d, 2 * k + 1 - d) for k in range(chips) for d in range(2)]
     pick = lambda a, b: jax.tree.map(lambda x, y: jnp.where(is_one, x, y), a, b)
     mine = pick(forward, backward)
     first = transfer(pick(backward, forward), swap)
+    first_state, late_input = lax.optimization_barrier((first[1], late_input))
+    first = (first[0], first_state)
+    ties = list(ties)
+    ties[1] = (late(late_input), ties[1])
     run = combine(first, mine)
     done = (jnp.ones_like(mine[0]), jnp.zeros_like(mine[1]))
     shift, level, tied = 1, 0, []
@@ -159,10 +163,12 @@
         in_weight[:, E:], normed, turned, preferred_element_type=jnp.float32
     ).astype(jnp.bfloat16)
     dt_raw = lax.dot_general(dt_weight, normed, turned, preferred_element_type=jnp.float32)
-    gate_part = lax.dot_general(
-        in_weight[:, :E], normed, turned, preferred_element_type=jnp.float32
-    ).astype(jnp.bfloat16).astype(jnp.float32)
-    gate_silu = jax.nn.silu(gate_part)
+    def gate_of(values):
+        gate_part = lax.dot_general(
+            in_weight[:, :E], values, turned, preferred_element_type=jnp.float32
+        ).astype(jnp.bfloat16).astype(jnp.float32)
+        return jax.nn.silu(gate_part)
+
     sides = halo(normed, in_weight, KERNEL - 1)
     padded = jnp.concatenate(
         [sides[:, : KERNEL - 1], conv_input, sides[:, KERNEL - 1 :]], axis=1
@@ -180,12 +186,14 @@
     fwd_in, bwd_in, tied = exchange(
         (parts[0][2], parts[0][1]),
         (parts[1][2], parts[1][1]),
-        [None, (gate_silu, parts[0][0]), parts[1][0]],
+        [None, parts[0][0], parts[1][0]],
+        gate_of,
+        normed,
     )
     if len(tied) == 2:
         (gate_silu, within_fwd), within_bwd = tied
     else:
-        within_fwd, within_bwd = parts[0][0], parts[1][0]
+        within_fwd, within_bwd, gate_silu = parts[0][0], parts[1][0], gate_of(normed)
     incomings = (fwd_in, bwd_in)
     withins = (within_fwd, within_bwd)
     total = jnp.zeros((HEADS, HEAD_DIM, rows), jnp.float32)

time: 147 us -> 148 us (level)
  matrix products: 38.4 us -> 41.3 us
  waiting for transfers between devices: 66.6 us -> 63.9 us
    dot_general x1, matrix products: 0.82 us -> 3.38 us  [halo(): lax.dot_general(in_weight[:, E:], rows, (((0,), (1,)), ((), ())), preferr...]
    ppermute x1, waiting for transfers between devices: 2.48 us -> 0.01 us  [halo(): after = lax.ppermute(normed[:width], 'seq', down)]
  transfers between devices with their start and end apart: 8 -> 8, of which waited for: 6 -> 5; matrix products, arithmetic and copies ran while one was open for 8% -> 13% of each run, Pallas kernels for 0% -> 0%
where the time goes in v5:
time: 148 us; the launch traced here: 147 us
  waiting for transfers between devices  63.9 us (43%)
  matrix products  41.3 us (28%)
  starting transfers between devices  18.7 us (13%)
  other arithmetic  11.8 us (8%)
  local copies, waits for them, and re-layouts  10.1 us (7%)
    all_to_all x1, waiting for transfers between devices, route_tiles(): lax.all_to_all(send, 'seq', 0, 0, tiled=True)  32 us
    ppermute x4, waiting for transfers between devices, transfer(): got = lax.ppermute(payload, 'seq', pairs)  30.2 us
    dot_general x2, matrix products, local_terms(): lax.dot_general(signal, mixing, (((2,), (2,)), ((0,), (0,))), precision=f...  7.79 us
    slice x4, local copies, waits for them, and re-layouts, local_terms(): signal = activated[:E].reshape(HEADS, HEAD_DIM, rows)  7.71 us
    all_to_all x1, starting transfers between devices, route_tiles(): lax.all_to_all(send, 'seq', 0, 0, tiled=True)  7.56 us
    ppermute x4, starting transfers between devices, transfer(): got = lax.ppermute(payload, 'seq', pairs)  6.79 us
    dot_general x1, matrix products, gate_of(): lax.dot_general(in_weight[:, :E], values, turned, preferred_element_type=...  4.96 us
    dot_general x1, matrix products, per_device(): lax.dot_general(mixed, out_weight, (((0,), (0,)), ((), ())), preferred_el...  4.65 us
  transfers between devices with their start and end apart: 8, of which 5 were waited for; matrix products, arithmetic and copies ran while one was open for 13% of the time, Pallas kernels for 0%

profile of v5, /device:TPU:0, one launch (start us, length us, event | category | flops | bytes accessed | tf_op | source)
XLA Modules:
  0.0 147.3 jit_solution(1497783173610241515)
XLA Ops:
  3.1 3.7 %convolution_convert_fusion = bf16[512,1664]{1,0:T(8,128)(2,1)} fusion(bf16[512,1]{1,0:T(8,128)(2,1)S(1)} %broadcast_in_dim.48, bf16[512,1536]{1,0:T(8,128)(2,1)} %param.14, s32[512]{0:T(512)S(1)} %add_select_fusion.2), kind=kOutput, calls=%fused_computation.32 | convolution fusion | flops 878641152 | bytes 3279872 | tf_op jit(solution)/shard_map/dot_general | solution.py:35
  6.8 7.6 %all-to-all-start = ((bf16[16,32,1664]{2,1,0:T(8,128)(2,1)}), bf16[16,32,1664]{2,1,0:T(8,128)(2,1)S(1)}, u32[]{:S(2)}, u32[]{:S(2)}) async-start(bf16[16,32,1664]{2,1,0:T(8,128)(2,1)} %bitcast.3), calls=%async_computation | async-start | bytes 3407872 | tf_op jit(solution)/shard_map/all_to_all | solution.py:37
  16.5 32.0 %all-to-all-done = bf16[16,32,1664]{2,1,0:T(8,128)(2,1)S(1)} async-done(((bf16[16,32,1664]{2,1,0:T(8,128)(2,1)}), bf16[16,32,1664]{2,1,0:T(8,128)(2,1)S(1)}, u32[]{:S(2)}, u32[]{:S(2)}) %all-to-all-start) | async-done | bytes 1703968 | tf_op jit(solution)/shard_map/all_to_all | solution.py:37
  48.7 4.2 %multiply_reduce_fusion.1 = (f32[256]{0:T(256)S(1)}, f32[256,1536]{1,0:T(8,128)S(1)}) fusion(f32[1536]{0:T(1024)S(1)} %copy-done.33, bf16[1536,1536]{1,0:T(8,128)(2,1)} %param.17, bf16[512,1664]{1,0:T(8,128)(2,1)S(1)} %bitcast.148, s32[512]{0:T(512)S(1)} %add_reduce_fusion), kind=kOutput, calls=%fused_computation.76 | convolution fusion | flops 1613102848 | bytes 7875584 | tf_op jit(solution)/shard_map/dot_general | solution.py:158
  56.0 2.9 %collective-permute-start = (bf16[3,1536]{1,0:T(4,128)(2,1)S(1)}, bf16[3,1536]{1,0:T(4,128)(2,1)S(1)}, u32[]{:S(2)}, u32[]{:S(2)}) collective-permute-start(bf16[3,1536]{1,0:T(4,128)(2,1)S(1)} %get-tuple-element.50), channel_id=1, source_target_pairs={{0,1},{1,2},{2,3},{3,4},{4,5},{5,6},{6,7},{7,8},{8,9},{9,10},{10,1... | collective-permute-start | bytes 27656 | tf_op jit(solution)/shard_map/ppermute | solution.py:50
  58.9 1.5 collective-permute-start.1
  60.3 4.1 %fusion.46 = bf16[1792,256]{0,1:T(8,128)(2,1)S(1)} fusion(bf16[256,1536]{1,0:T(8,128)(2,1)S(1)} %multiply_convert_fusion.1, bf16[1536,3328]{1,0:T(8,128)(2,1)} %param.20), kind=kOutput, calls=%fused_computation.43 | convolution fusion | flops 1409744896 | bytes 7208960 | tf_op jit(solution)/shard_map/dot_general | solution.py:162
  65.2 3.4 %fusion.52 = bf16[1792,6]{0,1:T(8,128)(2,1)S(1)} fusion(bf16[1536,3328]{1,0:T(8,128)(2,1)} %param.20, bf16[3,1536]{1,0:T(4,128)(2,1)S(1)} %collective-permute-done.1, bf16[3,1536]{1,0:T(4,128)(2,1)S(1)} %collective-permute-done), kind=kOutput, calls=%fused_computation.45 | convolution fusion | flops 33077760 | bytes 5544960 | tf_op jit(solution)/shard_map/dot_general | solution.py:53
  69.3 2.3 %divide_multiply_fusion = (f32[1792,256]{0,1:T(8,128)S(1)}, f32[1792,256]{0,1:T(8,128)S(1)}) fusion(f32[1792,262]{0,1:T(8,128)S(1)} %maximum_convert_fusion, f32[1792]{0:T(1024)S(1)} %copy-done.25, f32[1792]{0:T(1024)S(1)} %copy-done.26, f32[1792]{0:T(1024)S(1)} %get-tuple-element.24, f32[1792]{0:T(1024)S(1)} %get-tuple-element.23, ...), kind=kLoop, calls=%fused_computation.60 | loop fusion | flops 11010048 | bytes 16586752 | tf_op jit(solution)/shard_map/jit(silu)/mul | solution.py:182
  76.6 1.9 %copy.38 = f32[1536,256]{1,0:T(8,128)S(1)} copy(f32[1536,256]{0,1:T(8,128)} %slice.216) | data formatting | bytes 3145728 | tf_op jit(solution)/shard_map/slice | solution.py:60
  78.5 3.1 %copy.36 = f32[1536,256]{1,0:T(8,128)} copy(f32[1536,256]{0,1:T(8,128)} %slice.211) | data formatting | bytes 3145728 | tf_op jit(solution)/shard_map/slice | solution.py:60
  81.6 1.8 %fusion.71 = f32[24,64,128]{2,1,0:T(8,128)S(1)} fusion(f32[24,64,256]{2,1,0:T(8,128)S(1)} %bitcast.142, f32[24,256]{1,0:T(8,128)} %get-tuple-element.55, f32[1792,256]{0,1:T(8,128)} %copy-done.1), kind=kOutput, calls=%fused_computation.71 | convolution fusion | flops 302383104 | bytes 2514944 | tf_op jit(solution)/shard_map/dot_general | solution.py:82
  84.3 2.7 %collective-permute-start.2 = (bf16[25,64,128]{2,1,0:T(8,128)(2,1)S(1)}, bf16[25,64,128]{2,1,0:T(8,128)(2,1)S(1)}, u32[]{:S(2)}, u32[]{:S(2)}) collective-permute-start(bf16[25,64,128]{2,1,0:T(8,128)(2,1)S(1)} %pad_maximum_fusion), channel_id=1, source_target_pairs={{0,1},{1,0},{2,3},{3,2},{4,5},{5,4},{6,7},{7,6},{8,9},{9,8},{10,11... | collective-permute-start | bytes 1228808 | tf_op jit(solution)/shard_map/ppermute | solution.py:99
  87.0 3.9 %fusion.6 = f32[24,64,256]{2,1,0:T(8,128)S(1)} fusion(f32[24,64,256]{2,1,0:T(8,128)S(1)} %bitcast.143, f32[24,256]{1,0:T(8,128)S(1)} %copy-done.12, f32[24,256]{1,0:T(8,128)S(1)} %copy-done.20, f32[256,256]{1,0:T(8,128)S(1)} %copy-done.8, pred[256,256]{1,0:T(8,128)(4,1)S(1)} %copy-done.15), kind=kOutput, calls=%fused_computation.6 | convolution fusion | flops 610271232 | bytes 3522560 | tf_op jit(solution)/shard_map/dot_general | solution.py:80
  92.7 5.0 %divide_multiply_fusion.2 = f32[1536,256]{0,1:T(8,128)} fusion(bf16[256,1536]{1,0:T(8,128)(2,1)S(1)} %copy-done.4, bf16[1536,3328]{1,0:T(8,128)(2,1)} %param.20), kind=kOutput, calls=%fused_computation.70 | convolution fusion | flops 1210318848 | bytes 7077888 | tf_op jit(solution)/shard_map/dot_general | solution.py:167
  97.6 5.4 %collective-permute-done.3 = bf16[25,64,128]{2,1,0:T(8,128)(2,1)S(1)} collective-permute-done((bf16[25,64,128]{2,1,0:T(8,128)(2,1)S(1)}, bf16[25,64,128]{2,1,0:T(8,128)(2,1)S(1)}, u32[]{:S(2)}, u32[]{:S(2)}) %collective-permute-start.3) | collective-permute-done | bytes 409632 | tf_op jit(solution)/shard_map/ppermute | solution.py:99
  103.3 1.5 %collective-permute-start.4 = (bf16[25,64,128]{2,1,0:T(8,128)(2,1)S(1)}, bf16[25,64,128]{2,1,0:T(8,128)(2,1)S(1)}, u32[]{:S(2)}, u32[]{:S(2)}) collective-permute-start(bf16[25,64,128]{2,1,0:T(8,128)(2,1)S(1)} %pad_maximum_fusion.2), channel_id=1, source_target_pairs={{1,5},{3,7},{5,9},{7,11},{9,13},{11,15},{4,0},{6,2},{8,4},{10,6},{... | collective-permute-start | bytes 1228808 | tf_op jit(solution)/shard_map/ppermute | solution.py:99
  104.9 3.9 %fusion = f32[24,64,256]{2,1,0:T(8,128)S(1)} fusion(f32[24,64,256]{2,1,0:T(8,128)S(1)} %bitcast.146, f32[24,256]{1,0:T(8,128)S(1)} %copy-done.10, f32[24,256]{1,0:T(8,128)S(1)} %copy-done.18, f32[256,256]{1,0:T(8,128)S(1)} %copy-done.7, pred[256,256]{1,0:T(8,128)(4,1)S(1)} %copy-done.14), kind=kOutput, calls=%fused_computation | convolution fusion | flops 610271232 | bytes 3522560 | tf_op jit(solution)/shard_map/dot_general | solution.py:80
  108.8 10.1 %collective-permute-done.4 = bf16[25,64,128]{2,1,0:T(8,128)(2,1)S(1)} collective-permute-done((bf16[25,64,128]{2,1,0:T(8,128)(2,1)S(1)}, bf16[25,64,128]{2,1,0:T(8,128)(2,1)S(1)}, u32[]{:S(2)}, u32[]{:S(2)}) %collective-permute-start.4) | collective-permute-done | bytes 409632 | tf_op jit(solution)/shard_map/ppermute | solution.py:99
  120.5 14.8 %collective-permute-done.5 = bf16[25,64,128]{2,1,0:T(8,128)(2,1)S(1)} collective-permute-done((bf16[25,64,128]{2,1,0:T(8,128)(2,1)S(1)}, bf16[25,64,128]{2,1,0:T(8,128)(2,1)S(1)}, u32[]{:S(2)}, u32[]{:S(2)}) %collective-permute-start.5) | collective-permute-done | bytes 409632 | tf_op jit(solution)/shard_map/ppermute | solution.py:99
  135.7 1.7 %collective-permute-done.6 = bf16[24,64,128]{2,1,0:T(8,128)(2,1)S(1)} collective-permute-done((bf16[24,64,128]{2,1,0:T(8,128)(2,1)S(1)}, bf16[24,64,128]{2,1,0:T(8,128)(2,1)S(1)}, u32[]{:S(2)}, u32[]{:S(2)}) %collective-permute-start.6) | collective-permute-done | bytes 393248 | tf_op jit(solution)/shard_map/ppermute | solution.py:133
  137.4 1.8 %fusion.81 = f32[24,64,256]{2,1,0:T(8,128)S(1)} fusion(bf16[24,64,128]{2,1,0:T(8,128)(2,1)S(1)} %collective-permute-done.6, pred[]{:T(512)S(6)} %eq.69, f32[1792,256]{0,1:T(8,128)} %copy-done.1, f32[24,64,128]{2,1,0:T(8,128)S(1)} %slice_convert_fusion, f32[24]{0:T(128)S(1)} %get-tuple-element.43, f32[24]{0:T(128)S(1)} %get-tuple-element.39, ...), kind=kOutput, calls=%fused_computation.89 | convolution fusion | flops 304152576 | bytes 4064769 | tf_op jit(solution)/shard_map/dot_general | solution.py:204
  140.7 1.9 %multiply_reduce_fusion = (f32[256]{0:T(256)S(1)}, f32[1536,256]{0,1:T(8,128)S(1)}) fusion(f32[1536,256]{0,1:T(8,128)S(1)} %copy.42, f32[1536,256]{0,1:T(8,128)} %divide_multiply_fusion.2), kind=kLoop, calls=%fused_computation.68 | loop fusion | flops 1179392 | bytes 4719616 | tf_op jit(solution)/shard_map/reduce_sum | solution.py:209
  142.6 4.7 %fusion.33 = bf16[256,1536]{1,0:T(8,128)(2,1)} fusion(f32[256,1536]{1,0:T(8,128)S(1)} %copy-done.6, bf16[1536,1536]{1,0:T(8,128)(2,1)} %param.27, f32[1536,256]{0,1:T(8,128)S(1)} %get-tuple-element.38, f32[1536]{0:T(1024)S(1)} %copy-done.34, f32[256]{0:T(256)S(1)} %add_rsqrt_fusion), kind=kOutput, calls=%fused_computation.37 | convolution fusion | flops 1209925632 | bytes 8657920 | tf_op jit(solution)/shard_map/dot_general | solution.py:211
  (134 shorter events, 20.1 us)
Async XLA Ops:
  0.0 53.2 %copy-start = (bf16[1536,24]{0,1:T(8,128)(2,1)S(1)}, bf16[1536,24]{0,1:T(8,128)(2,1)}, u32[]{:S(2)}) copy-start(bf16[1536,24]{0,1:T(8,128)(2,1)} %param.21) | copy-start | bytes 221188
  6.8 8.9 %copy-start.27 = (f32[2,1792]{1,0:T(2,128)S(1)}, f32[2,1792]{1,0:T(2,128)}, u32[]{:S(2)}) copy-start(f32[2,1792]{1,0:T(2,128)} %param.23) | copy-start | bytes 43012
  6.8 8.9 %copy-start.16 = (f32[2,4,1792]{2,1,0:T(4,128)S(1)}, f32[2,4,1792]{2,1,0:T(4,128)}, u32[]{:S(2)}) copy-start(f32[2,4,1792]{2,1,0:T(4,128)} %param.22) | copy-start | bytes 172036
  6.8 9.7 %copy-start.31 = (f32[2,24]{1,0:T(2,128)S(1)}, f32[2,24]{1,0:T(2,128)}, u32[]{:S(2)}) copy-start(f32[2,24]{1,0:T(2,128)} %param.24) | copy-start | bytes 580
  6.8 9.7 %copy-start.32 = (f32[2,24]{1,0:T(2,128)S(1)}, f32[2,24]{1,0:T(2,128)}, u32[]{:S(2)}) copy-start(f32[2,24]{1,0:T(2,128)} %param.25) | copy-start | bytes 580
  6.8 41.9 %copy-start.33 = (f32[1536]{0:T(1024)S(1)}, f32[1536]{0:T(1024)}, u32[]{:S(2)}) copy-start(f32[1536]{0:T(1024)} %param.18) | copy-start | bytes 18436
  6.8 41.7 %all-to-all-start = ((bf16[16,32,1664]{2,1,0:T(8,128)(2,1)}), bf16[16,32,1664]{2,1,0:T(8,128)(2,1)S(1)}, u32[]{:S(2)}, u32[]{:S(2)}) async-start(bf16[16,32,1664]{2,1,0:T(8,128)(2,1)} %bitcast.3), calls=%async_computation | async-start | bytes 3407872 | tf_op jit(solution)/shard_map/all_to_all | solution.py:37
  48.7 4.3 %copy-start.28 = (f32[1536]{0:T(1024)S(1)}, f32[1536]{0:T(1024)}, u32[]{:S(2)}) copy-start(f32[1536]{0:T(1024)} %param.19) | copy-start | bytes 18436
  53.2 11.4 %copy-start.3 = (bf16[256,1536]{1,0:T(8,128)(2,1)}, bf16[256,1536]{1,0:T(8,128)(2,1)S(1)}, u32[]{:S(2)}) copy-start(bf16[256,1536]{1,0:T(8,128)(2,1)S(1)} %multiply_convert_fusion.1) | copy-start | bytes 2359300
  53.6 11.0 %copy-start.9 = (f32[24,256]{1,0:T(8,128)}, f32[24,256]{1,0:T(8,128)S(1)}, u32[]{:S(2)}) copy-start(f32[24,256]{1,0:T(8,128)S(1)} %get-tuple-element.58) | copy-start | bytes 73732
  53.6 11.0 %copy-start.11 = (f32[24,256]{1,0:T(8,128)}, f32[24,256]{1,0:T(8,128)S(1)}, u32[]{:S(2)}) copy-start(f32[24,256]{1,0:T(8,128)S(1)} %get-tuple-element.59) | copy-start | bytes 73732
  53.8 10.8 %copy-start.17 = (f32[24,256]{1,0:T(8,128)}, f32[24,256]{1,0:T(8,128)S(1)}, u32[]{:S(2)}) copy-start(f32[24,256]{1,0:T(8,128)S(1)} %fusion.107) | copy-start | bytes 73732
  54.0 10.5 %copy-start.19 = (f32[24,256]{1,0:T(8,128)}, f32[24,256]{1,0:T(8,128)S(1)}, u32[]{:S(2)}) copy-start(f32[24,256]{1,0:T(8,128)S(1)} %fusion.106) | copy-start | bytes 73732
  56.0 9.2 %collective-permute-start = (bf16[3,1536]{1,0:T(4,128)(2,1)S(1)}, bf16[3,1536]{1,0:T(4,128)(2,1)S(1)}, u32[]{:S(2)}, u32[]{:S(2)}) collective-permute-start(bf16[3,1536]{1,0:T(4,128)(2,1)S(1)} %get-tuple-element.50), channel_id=1, source_target_pairs={{0,1},{1,2},{2,3},{3,4},{4,5},{5,6},{6,7},{7,8},{8,9},{9,10},{10,1... | collective-permute-start | bytes 27656 | tf_op jit(solution)/shard_map/ppermute | solution.py:50
  58.9 6.3 %collective-permute-start.1 = (bf16[3,1536]{1,0:T(4,128)(2,1)S(1)}, bf16[3,1536]{1,0:T(4,128)(2,1)S(1)}, u32[]{:S(2)}, u32[]{:S(2)}) collective-permute-start(bf16[3,1536]{1,0:T(4,128)(2,1)S(1)} %get-tuple-element.51), channel_id=1, source_target_pairs={{1,0},{2,1},{3,2},{4,3},{5,4},{6,5},{7,6},{8,7},{9,8},{10,9},{11,1... | collective-permute-start | bytes 27656 | tf_op jit(solution)/shard_map/ppermute | solution.py:51
  83.4 3.6 %copy-start.8 = (f32[256,256]{1,0:T(8,128)S(1)}, f32[256,256]{1,0:T(8,128)}, u32[]{:S(2)}) copy-start(f32[256,256]{1,0:T(8,128)} %fusion.100) | copy-start | bytes 786436
  83.4 3.6 %copy-start.12 = (f32[24,256]{1,0:T(8,128)S(1)}, f32[24,256]{1,0:T(8,128)}, u32[]{:S(2)}) copy-start(f32[24,256]{1,0:T(8,128)} %copy-done.11) | copy-start | bytes 73732
  84.3 6.6 %copy-start.30 = (f32[24]{0:T(128)S(1)}, f32[24]{0:T(128)}, u32[]{:S(2)}) copy-start(f32[24]{0:T(128)} %get-tuple-element.32) | copy-start | bytes 292
  84.3 6.8 %copy-start.29 = (f32[24]{0:T(128)S(1)}, f32[24]{0:T(128)}, u32[]{:S(2)}) copy-start(f32[24]{0:T(128)} %broadcast_select_fusion.1) | copy-start | bytes 292
  84.3 6.6 %collective-permute-start.2 = (bf16[25,64,128]{2,1,0:T(8,128)(2,1)S(1)}, bf16[25,64,128]{2,1,0:T(8,128)(2,1)S(1)}, u32[]{:S(2)}, u32[]{:S(2)}) collective-permute-start(bf16[25,64,128]{2,1,0:T(8,128)(2,1)S(1)} %pad_maximum_fusion), channel_id=1, source_target_pairs={{0,1},{1,0},{2,3},{3,2},{4,5},{5,4},{6,7},{7,6},{8,9},{9,8},{10,11... | collective-permute-start | bytes 1228808 | tf_op jit(solution)/shard_map/ppermute | solution.py:99
  91.3 11.7 %collective-permute-start.3 = (bf16[25,64,128]{2,1,0:T(8,128)(2,1)S(1)}, bf16[25,64,128]{2,1,0:T(8,128)(2,1)S(1)}, u32[]{:S(2)}, u32[]{:S(2)}) collective-permute-start(bf16[25,64,128]{2,1,0:T(8,128)(2,1)S(1)} %pad_maximum_fusion.1), channel_id=1, source_target_pairs={{1,3},{3,5},{5,7},{7,9},{9,11},{11,13},{13,15},{2,0},{4,2},{6,4},{... | collective-permute-start | bytes 1228808 | tf_op jit(solution)/shard_map/ppermute | solution.py:99
  103.3 15.5 %collective-permute-start.4 = (bf16[25,64,128]{2,1,0:T(8,128)(2,1)S(1)}, bf16[25,64,128]{2,1,0:T(8,128)(2,1)S(1)}, u32[]{:S(2)}, u32[]{:S(2)}) collective-permute-start(bf16[25,64,128]{2,1,0:T(8,128)(2,1)S(1)} %pad_maximum_fusion.2), channel_id=1, source_target_pairs={{1,5},{3,7},{5,9},{7,11},{9,13},{11,15},{4,0},{6,2},{8,4},{10,6},{... | collective-permute-start | bytes 1228808 | tf_op jit(solution)/shard_map/ppermute | solution.py:99
  119.2 16.1 %collective-permute-start.5 = (bf16[25,64,128]{2,1,0:T(8,128)(2,1)S(1)}, bf16[25,64,128]{2,1,0:T(8,128)(2,1)S(1)}, u32[]{:S(2)}, u32[]{:S(2)}) collective-permute-start(bf16[25,64,128]{2,1,0:T(8,128)(2,1)S(1)} %pad_maximum_fusion.3), channel_id=1, source_target_pairs={{1,9},{3,11},{5,13},{7,15},{8,0},{10,2},{12,4},{14,6},{17,25},{19,... | collective-permute-start | bytes 1228808 | tf_op jit(solution)/shard_map/ppermute | solution.py:99
  135.6 1.8 %collective-permute-start.6 = (bf16[24,64,128]{2,1,0:T(8,128)(2,1)S(1)}, bf16[24,64,128]{2,1,0:T(8,128)(2,1)S(1)}, u32[]{:S(2)}, u32[]{:S(2)}) collective-permute-start(bf16[24,64,128]{2,1,0:T(8,128)(2,1)S(1)} %fusion.87), channel_id=1, source_target_pairs={{0,1},{1,0},{2,3},{3,2},{4,5},{5,4},{6,7},{7,6},{8,9},{9,8},{10,11... | collective-permute-start | bytes 1179656 | tf_op jit(solution)/shard_map/ppermute | solution.py:133
  (19 other events, 32.7 us)

commit v6 on v5

--- a/solution.py
+++ b/solution.py
@@ -109,10 +109,11 @@
     pick = lambda a, b: jax.tree.map(lambda x, y: jnp.where(is_one, x, y), a, b)
     mine = pick(forward, backward)
     first = transfer(pick(backward, forward), swap)
-    first_state, late_input = lax.optimization_barrier((first[1], late_input))
-    first = (first[0], first_state)
     ties = list(ties)
-    ties[1] = (late(late_input), ties[1])
+    if late is not None:
+        first_state, late_input = lax.optimization_barrier((first[1], late_input))
+        first = (first[0], first_state)
+        ties[1] = (late(late_input), ties[1])
     run = combine(first, mine)
     done = (jnp.ones_like(mine[0]), jnp.zeros_like(mine[1]))
     shift, level, tied = 1, 0, []
@@ -183,13 +184,23 @@
         step_size = jax.nn.softplus(dt_raw + dt_bias[direction][:, None])
         decay_rate = -jnp.exp(a_log[direction])
         parts.append(local_terms(activated, step_size, decay_rate, direction == 1))
-    fwd_in, bwd_in, tied = exchange(
-        (parts[0][2], parts[0][1]),
-        (parts[1][2], parts[1][1]),
+    half = HEADS // 2
+    low_f, low_b, tied = exchange(
+        (parts[0][2][:half], parts[0][1][:half]),
+        (parts[1][2][:half], parts[1][1][:half]),
         [None, parts[0][0], parts[1][0]],
         gate_of,
         normed,
     )
+    high_f, high_b, _ = exchange(
+        (parts[0][2][half:], parts[0][1][half:]),
+        (parts[1][2][half:], parts[1][1][half:]),
+        [],
+        None,
+        None,
+    )
+    fwd_in = jnp.concatenate([low_f, high_f], axis=0)
+    bwd_in = jnp.concatenate([low_b, high_b], axis=0)
     if len(tied) == 2:
         (gate_silu, within_fwd), within_bwd = tied
     else:

time: 148 us -> 150 us (1.014)
  starting transfers between devices: 18.7 us -> 22.6 us
  local copies, waits for them, and re-layouts: 10.1 us -> 7.76 us
    ppermute x4 -> x8, starting transfers between devices: 6.79 us -> 10.8 us  [transfer(): got = lax.ppermute(payload, 'seq', pairs)]
    slice x4, local copies, waits for them, and re-layouts: 7.71 us -> 5.11 us  [local_terms(): signal = activated[:E].reshape(HEADS, HEAD_DIM, rows)]
    ppermute x4 -> x8, waiting for transfers between devices: 30.2 us -> 29.6 us  [transfer(): got = lax.ppermute(payload, 'seq', pairs)]
  transfers between devices with their start and end apart: 8 -> 13, of which waited for: 5 -> 8; matrix products, arithmetic and copies ran while one was open for 13% -> 14% of each run, Pallas kernels for 0% -> 0%
where the time goes in v6:
time: 150 us; the launch traced here: 149 us
  waiting for transfers between devices  62.7 us (42%)
  matrix products  42.5 us (28%)
  starting transfers between devices  22.6 us (15%)
  other arithmetic  11.9 us (8%)
  local copies, waits for them, and re-layouts  7.76 us (5%)
  between operations  1.61 us (1%)
    all_to_all x1, waiting for transfers between devices, route_tiles(): lax.all_to_all(send, 'seq', 0, 0, tiled=True)  32 us
    ppermute x8, waiting for transfers between devices, transfer(): got = lax.ppermute(payload, 'seq', pairs)  29.6 us
    ppermute x8, starting transfers between devices, transfer(): got = lax.ppermute(payload, 'seq', pairs)  10.8 us
    dot_general x2, matrix products, local_terms(): lax.dot_general(signal, mixing, (((2,), (2,)), ((0,), (0,))), precision=f...  7.8 us
    all_to_all x1, starting transfers between devices, route_tiles(): lax.all_to_all(send, 'seq', 0, 0, tiled=True)  7.56 us
    slice x4, local copies, waits for them, and re-layouts, local_terms(): signal = activated[:E].reshape(HEADS, HEAD_DIM, rows)  5.11 us
    dot_general x1, matrix products, gate_of(): lax.dot_general(in_weight[:, :E], values, turned, preferred_element_type=...  4.96 us
    dot_general x1, matrix products, per_device(): lax.dot_general(mixed, out_weight, (((0,), (0,)), ((), ())), preferred_el...  4.65 us
  transfers between devices with their start and end apart: 13, of which 8 were waited for; matrix products, arithmetic and copies ran while one was open for 14% of the time, Pallas kernels for 0%

profile of v6, /device:TPU:0, one launch (start us, length us, event | category | flops | bytes accessed | tf_op | source)
XLA Modules:
  0.0 149.1 jit_solution(18407100987935988382)
XLA Ops:
  3.1 3.8 %convolution_convert_fusion = bf16[512,1664]{1,0:T(8,128)(2,1)} fusion(bf16[512,1]{1,0:T(8,128)(2,1)S(1)} %broadcast_in_dim.62, bf16[512,1536]{1,0:T(8,128)(2,1)} %param.14, s32[512]{0:T(512)S(1)} %add_select_fusion.2), kind=kOutput, calls=%fused_computation.32 | convolution fusion | flops 878641152 | bytes 3279872 | tf_op jit(solution)/shard_map/dot_general | solution.py:35
  6.8 7.6 %all-to-all-start = ((bf16[16,32,1664]{2,1,0:T(8,128)(2,1)}), bf16[16,32,1664]{2,1,0:T(8,128)(2,1)S(1)}, u32[]{:S(2)}, u32[]{:S(2)}) async-start(bf16[16,32,1664]{2,1,0:T(8,128)(2,1)} %bitcast.3), calls=%async_computation | async-start | bytes 3407872 | tf_op jit(solution)/shard_map/all_to_all | solution.py:37
  16.6 32.0 %all-to-all-done = bf16[16,32,1664]{2,1,0:T(8,128)(2,1)S(1)} async-done(((bf16[16,32,1664]{2,1,0:T(8,128)(2,1)}), bf16[16,32,1664]{2,1,0:T(8,128)(2,1)S(1)}, u32[]{:S(2)}, u32[]{:S(2)}) %all-to-all-start) | async-done | bytes 1703968 | tf_op jit(solution)/shard_map/all_to_all | solution.py:37
  48.7 4.2 %multiply_reduce_fusion.1 = (f32[256]{0:T(256)S(1)}, f32[256,1536]{1,0:T(8,128)S(1)}) fusion(f32[1536]{0:T(1024)S(1)} %copy-done.35, bf16[1536,1536]{1,0:T(8,128)(2,1)} %param.17, bf16[512,1664]{1,0:T(8,128)(2,1)S(1)} %bitcast.164, s32[512]{0:T(512)S(1)} %add_reduce_fusion), kind=kOutput, calls=%fused_computation.76 | convolution fusion | flops 1613102848 | bytes 7875584 | tf_op jit(solution)/shard_map/dot_general | solution.py:159
  55.1 2.9 %collective-permute-start = (bf16[3,1536]{1,0:T(4,128)(2,1)S(1)}, bf16[3,1536]{1,0:T(4,128)(2,1)S(1)}, u32[]{:S(2)}, u32[]{:S(2)}) collective-permute-start(bf16[3,1536]{1,0:T(4,128)(2,1)S(1)} %get-tuple-element.70), channel_id=1, source_target_pairs={{0,1},{1,2},{2,3},{3,4},{4,5},{5,6},{6,7},{7,8},{8,9},{9,10},{10,1... | collective-permute-start | bytes 27656 | tf_op jit(solution)/shard_map/ppermute | solution.py:50
  59.3 4.1 %fusion.46 = bf16[1792,256]{0,1:T(8,128)(2,1)S(1)} fusion(bf16[256,1536]{1,0:T(8,128)(2,1)S(1)} %multiply_convert_fusion.1, bf16[1536,3328]{1,0:T(8,128)(2,1)} %param.20), kind=kOutput, calls=%fused_computation.43 | convolution fusion | flops 1409744896 | bytes 7208960 | tf_op jit(solution)/shard_map/dot_general | solution.py:163
  64.2 3.4 %fusion.52 = bf16[1792,6]{0,1:T(8,128)(2,1)S(1)} fusion(bf16[1536,3328]{1,0:T(8,128)(2,1)} %param.20, bf16[3,1536]{1,0:T(4,128)(2,1)S(1)} %collective-permute-done.1, bf16[3,1536]{1,0:T(4,128)(2,1)S(1)} %collective-permute-done), kind=kOutput, calls=%fused_computation.45 | convolution fusion | flops 33077760 | bytes 5544960 | tf_op jit(solution)/shard_map/dot_general | solution.py:53
  68.3 2.5 %divide_multiply_fusion.1 = (f32[1792,256]{0,1:T(8,128)S(1)}, f32[1792,256]{0,1:T(8,128)S(1)}) fusion(f32[1792,262]{0,1:T(8,128)S(1)} %maximum_convert_fusion, f32[1792]{0:T(1024)S(1)} %copy-done.22, f32[1792]{0:T(1024)S(1)} %copy-done.23, f32[1792]{0:T(1024)S(1)} %copy-done.24, f32[1792]{0:T(1024)S(1)} %get-tuple-element.23, ...), kind=kLoop, calls=%fused_computation.61 | loop fusion | flops 11010048 | bytes 16586752 | tf_op jit(solution)/shard_map/jit(silu)/mul | solution.py:183
  74.7 1.6 %copy.36 = f32[1536,256]{1,0:T(8,128)} copy(f32[1536,256]{0,1:T(8,128)S(1)} %slice.283) | data formatting | bytes 3145728 | tf_op jit(solution)/shard_map/slice | solution.py:60
  76.3 1.9 %copy.38 = f32[1536,256]{1,0:T(8,128)S(1)} copy(f32[1536,256]{0,1:T(8,128)} %slice.289) | data formatting | bytes 3145728 | tf_op jit(solution)/shard_map/slice | solution.py:60
  78.2 2.2 %fusion.73 = f32[24,64,128]{2,1,0:T(8,128)S(1)} fusion(f32[24,64,256]{2,1,0:T(8,128)} %bitcast.160, f32[24,256]{1,0:T(8,128)} %get-tuple-element.96, f32[1792,256]{0,1:T(8,128)S(1)} %get-tuple-element.60), kind=kOutput, calls=%fused_computation.73 | convolution fusion | flops 302383104 | bytes 2514944 | tf_op jit(solution)/shard_map/dot_general | solution.py:82
  80.5 1.8 %fusion.71 = f32[24,64,128]{2,1,0:T(8,128)S(1)} fusion(f32[24,64,256]{2,1,0:T(8,128)S(1)} %bitcast.158, f32[24,256]{1,0:T(8,128)S(1)} %get-tuple-element.75, f32[1792,256]{0,1:T(8,128)} %copy-done.1), kind=kOutput, calls=%fused_computation.71 | convolution fusion | flops 302383104 | bytes 2514944 | tf_op jit(solution)/shard_map/dot_general | solution.py:82
  82.5 2.7 %collective-permute-start.7 = (bf16[13,64,128]{2,1,0:T(8,128)(2,1)S(1)}, bf16[13,64,128]{2,1,0:T(8,128)(2,1)S(1)}, u32[]{:S(2)}, u32[]{:S(2)}) collective-permute-start(bf16[13,64,128]{2,1,0:T(8,128)(2,1)S(1)} %pad_maximum_fusion.4), channel_id=1, source_target_pairs={{0,1},{1,0},{2,3},{3,2},{4,5},{5,4},{6,7},{7,6},{8,9},{9,8},{10,11... | collective-permute-start | bytes 638984 | tf_op jit(solution)/shard_map/ppermute | solution.py:99
  85.2 3.9 %fusion = f32[24,64,256]{2,1,0:T(8,128)S(1)} fusion(f32[24,64,256]{2,1,0:T(8,128)S(1)} %bitcast.161, f32[24,256]{1,0:T(8,128)S(1)} %copy-done.12, f32[24,256]{1,0:T(8,128)S(1)} %copy-done.20, f32[256,256]{1,0:T(8,128)S(1)} %copy-done.8, pred[256,256]{1,0:T(8,128)(4,1)S(1)} %copy-done.14), kind=kOutput, calls=%fused_computation | convolution fusion | flops 610271232 | bytes 3522560 | tf_op jit(solution)/shard_map/dot_general | solution.py:80
  89.1 3.9 %fusion.6 = f32[24,64,256]{2,1,0:T(8,128)S(1)} fusion(f32[24,64,256]{2,1,0:T(8,128)S(1)} %bitcast.159, f32[24,256]{1,0:T(8,128)S(1)} %copy-done.10, f32[24,256]{1,0:T(8,128)S(1)} %copy-done.18, f32[256,256]{1,0:T(8,128)S(1)} %copy-done.7, pred[256,256]{1,0:T(8,128)(4,1)S(1)} %copy-done.13), kind=kOutput, calls=%fused_computation.6 | convolution fusion | flops 610271232 | bytes 3522560 | tf_op jit(solution)/shard_map/dot_general | solution.py:80
  96.3 1.5 %collective-permute-start.8 = (bf16[13,64,128]{2,1,0:T(8,128)(2,1)S(1)}, bf16[13,64,128]{2,1,0:T(8,128)(2,1)S(1)}, u32[]{:S(2)}, u32[]{:S(2)}) collective-permute-start(bf16[13,64,128]{2,1,0:T(8,128)(2,1)S(1)} %pad_maximum_fusion.5), channel_id=1, source_target_pairs={{1,3},{3,5},{5,7},{7,9},{9,11},{11,13},{13,15},{2,0},{4,2},{6,4},{... | collective-permute-start | bytes 638984 | tf_op jit(solution)/shard_map/ppermute | solution.py:99
  97.9 5.0 %divide_multiply_fusion.2 = f32[1536,256]{0,1:T(8,128)} fusion(bf16[256,1536]{1,0:T(8,128)(2,1)S(1)} %copy-done.4, bf16[1536,3328]{1,0:T(8,128)(2,1)} %param.20), kind=kOutput, calls=%fused_computation.70 | convolution fusion | flops 1210318848 | bytes 7077888 | tf_op jit(solution)/shard_map/dot_general | solution.py:168
  102.8 4.0 %collective-permute-done.8 = bf16[13,64,128]{2,1,0:T(8,128)(2,1)S(1)} collective-permute-done((bf16[13,64,128]{2,1,0:T(8,128)(2,1)S(1)}, bf16[13,64,128]{2,1,0:T(8,128)(2,1)S(1)}, u32[]{:S(2)}, u32[]{:S(2)}) %collective-permute-start.8) | collective-permute-done | bytes 213024 | tf_op jit(solution)/shard_map/ppermute | solution.py:99
  109.9 10.7 %collective-permute-done.9 = bf16[13,64,128]{2,1,0:T(8,128)(2,1)S(1)} collective-permute-done((bf16[13,64,128]{2,1,0:T(8,128)(2,1)S(1)}, bf16[13,64,128]{2,1,0:T(8,128)(2,1)S(1)}, u32[]{:S(2)}, u32[]{:S(2)}) %collective-permute-start.9) | collective-permute-done | bytes 213024 | tf_op jit(solution)/shard_map/ppermute | solution.py:99
  124.4 10.7 %collective-permute-done.10 = bf16[13,64,128]{2,1,0:T(8,128)(2,1)S(1)} collective-permute-done((bf16[13,64,128]{2,1,0:T(8,128)(2,1)S(1)}, bf16[13,64,128]{2,1,0:T(8,128)(2,1)S(1)}, u32[]{:S(2)}, u32[]{:S(2)}) %collective-permute-start.10) | collective-permute-done | bytes 213024 | tf_op jit(solution)/shard_map/ppermute | solution.py:99
  135.4 2.0 %collective-permute-done.5 = bf16[13,64,128]{2,1,0:T(8,128)(2,1)S(1)} collective-permute-done((bf16[13,64,128]{2,1,0:T(8,128)(2,1)S(1)}, bf16[13,64,128]{2,1,0:T(8,128)(2,1)S(1)}, u32[]{:S(2)}, u32[]{:S(2)}) %collective-permute-start.5) | collective-permute-done | bytes 213024 | tf_op jit(solution)/shard_map/ppermute | solution.py:99
  139.4 1.7 %fusion.78 = f32[24,64,256]{2,1,0:T(8,128)S(1)} fusion(f32[12,64,128]{2,1,0:T(8,128)S(1)} %get-tuple-element.69, f32[12,64,128]{2,1,0:T(8,128)S(1)} %get-tuple-element.67, f32[1792,256]{0,1:T(8,128)} %copy-done.1), kind=kOutput, calls=%fused_computation.80 | convolution fusion | flops 302186496 | bytes 2490368 | tf_op jit(solution)/shard_map/dot_general | solution.py:215
  142.6 1.9 %multiply_reduce_fusion = (f32[256]{0:T(256)S(1)}, f32[1536,256]{0,1:T(8,128)S(1)}) fusion(f32[1536,256]{0,1:T(8,128)S(1)} %copy.42, f32[1536,256]{0,1:T(8,128)} %divide_multiply_fusion.2), kind=kLoop, calls=%fused_computation.68 | loop fusion | flops 1179392 | bytes 4719616 | tf_op jit(solution)/shard_map/reduce_sum | solution.py:220
  144.4 4.7 %fusion.33 = bf16[256,1536]{1,0:T(8,128)(2,1)} fusion(f32[256,1536]{1,0:T(8,128)S(1)} %copy-done.6, bf16[1536,1536]{1,0:T(8,128)(2,1)} %param.27, f32[1536,256]{0,1:T(8,128)S(1)} %get-tuple-element.34, f32[1536]{0:T(1024)S(1)} %copy-done.36, f32[256]{0:T(256)S(1)} %add_rsqrt_fusion), kind=kOutput, calls=%fused_computation.37 | convolution fusion | flops 1209925632 | bytes 8657920 | tf_op jit(solution)/shard_map/dot_general | solution.py:222
  (171 shorter events, 27.0 us)
Async XLA Ops:
  0.0 53.2 %copy-start = (bf16[1536,24]{0,1:T(8,128)(2,1)S(1)}, bf16[1536,24]{0,1:T(8,128)(2,1)}, u32[]{:S(2)}) copy-start(bf16[1536,24]{0,1:T(8,128)(2,1)} %param.21) | copy-start | bytes 221188
  6.8 8.9 %copy-start.27 = (f32[2,1792]{1,0:T(2,128)S(1)}, f32[2,1792]{1,0:T(2,128)}, u32[]{:S(2)}) copy-start(f32[2,1792]{1,0:T(2,128)} %param.23) | copy-start | bytes 43012
  6.8 9.0 %copy-start.16 = (f32[2,4,1792]{2,1,0:T(4,128)S(1)}, f32[2,4,1792]{2,1,0:T(4,128)}, u32[]{:S(2)}) copy-start(f32[2,4,1792]{2,1,0:T(4,128)} %param.22) | copy-start | bytes 172036
  6.8 9.7 %copy-start.33 = (f32[2,24]{1,0:T(2,128)S(1)}, f32[2,24]{1,0:T(2,128)}, u32[]{:S(2)}) copy-start(f32[2,24]{1,0:T(2,128)} %param.24) | copy-start | bytes 580
  6.8 9.7 %copy-start.34 = (f32[2,24]{1,0:T(2,128)S(1)}, f32[2,24]{1,0:T(2,128)}, u32[]{:S(2)}) copy-start(f32[2,24]{1,0:T(2,128)} %param.25) | copy-start | bytes 580
  6.8 41.9 %copy-start.35 = (f32[1536]{0:T(1024)S(1)}, f32[1536]{0:T(1024)}, u32[]{:S(2)}) copy-start(f32[1536]{0:T(1024)} %param.18) | copy-start | bytes 18436
  6.8 41.7 %all-to-all-start = ((bf16[16,32,1664]{2,1,0:T(8,128)(2,1)}), bf16[16,32,1664]{2,1,0:T(8,128)(2,1)S(1)}, u32[]{:S(2)}, u32[]{:S(2)}) async-start(bf16[16,32,1664]{2,1,0:T(8,128)(2,1)} %bitcast.3), calls=%async_computation | async-start | bytes 3407872 | tf_op jit(solution)/shard_map/all_to_all | solution.py:37
  53.2 10.3 %copy-start.3 = (bf16[256,1536]{1,0:T(8,128)(2,1)}, bf16[256,1536]{1,0:T(8,128)(2,1)S(1)}, u32[]{:S(2)}) copy-start(bf16[256,1536]{1,0:T(8,128)(2,1)S(1)} %multiply_convert_fusion.1) | copy-start | bytes 2359300
  53.6 9.9 %copy-start.9 = (f32[24,256]{1,0:T(8,128)}, f32[24,256]{1,0:T(8,128)S(1)}, u32[]{:S(2)}) copy-start(f32[24,256]{1,0:T(8,128)S(1)} %get-tuple-element.78) | copy-start | bytes 73732
  53.6 9.9 %copy-start.11 = (f32[24,256]{1,0:T(8,128)}, f32[24,256]{1,0:T(8,128)S(1)}, u32[]{:S(2)}) copy-start(f32[24,256]{1,0:T(8,128)S(1)} %get-tuple-element.79) | copy-start | bytes 73732
  53.8 9.7 %copy-start.17 = (f32[24,256]{1,0:T(8,128)}, f32[24,256]{1,0:T(8,128)S(1)}, u32[]{:S(2)}) copy-start(f32[24,256]{1,0:T(8,128)S(1)} %fusion.116) | copy-start | bytes 73732
  54.2 9.3 %copy-start.19 = (f32[24,256]{1,0:T(8,128)}, f32[24,256]{1,0:T(8,128)S(1)}, u32[]{:S(2)}) copy-start(f32[24,256]{1,0:T(8,128)S(1)} %fusion.117) | copy-start | bytes 73732
  55.1 9.1 %collective-permute-start = (bf16[3,1536]{1,0:T(4,128)(2,1)S(1)}, bf16[3,1536]{1,0:T(4,128)(2,1)S(1)}, u32[]{:S(2)}, u32[]{:S(2)}) collective-permute-start(bf16[3,1536]{1,0:T(4,128)(2,1)S(1)} %get-tuple-element.70), channel_id=1, source_target_pairs={{0,1},{1,2},{2,3},{3,4},{4,5},{5,6},{6,7},{7,8},{8,9},{9,10},{10,1... | collective-permute-start | bytes 27656 | tf_op jit(solution)/shard_map/ppermute | solution.py:50
  58.0 6.2 %collective-permute-start.1 = (bf16[3,1536]{1,0:T(4,128)(2,1)S(1)}, bf16[3,1536]{1,0:T(4,128)(2,1)S(1)}, u32[]{:S(2)}, u32[]{:S(2)}) collective-permute-start(bf16[3,1536]{1,0:T(4,128)(2,1)S(1)} %get-tuple-element.71), channel_id=1, source_target_pairs={{1,0},{2,1},{3,2},{4,3},{5,4},{6,5},{7,6},{8,7},{9,8},{10,9},{11,1... | collective-permute-start | bytes 27656 | tf_op jit(solution)/shard_map/ppermute | solution.py:51
  82.5 10.6 %collective-permute-start.7 = (bf16[13,64,128]{2,1,0:T(8,128)(2,1)S(1)}, bf16[13,64,128]{2,1,0:T(8,128)(2,1)S(1)}, u32[]{:S(2)}, u32[]{:S(2)}) collective-permute-start(bf16[13,64,128]{2,1,0:T(8,128)(2,1)S(1)} %pad_maximum_fusion.4), channel_id=1, source_target_pairs={{0,1},{1,0},{2,3},{3,2},{4,5},{5,4},{6,7},{7,6},{8,9},{9,8},{10,11... | collective-permute-start | bytes 638984 | tf_op jit(solution)/shard_map/ppermute | solution.py:99
  93.2 1.5 %collective-permute-start.2 = (bf16[13,64,128]{2,1,0:T(8,128)(2,1)S(1)}, bf16[13,64,128]{2,1,0:T(8,128)(2,1)S(1)}, u32[]{:S(2)}, u32[]{:S(2)}) collective-permute-start(bf16[13,64,128]{2,1,0:T(8,128)(2,1)S(1)} %pad_maximum_fusion), channel_id=1, source_target_pairs={{0,1},{1,0},{2,3},{3,2},{4,5},{5,4},{6,7},{7,6},{8,9},{9,8},{10,11... | collective-permute-start | bytes 638984 | tf_op jit(solution)/shard_map/ppermute | solution.py:99
  95.0 13.3 %collective-permute-start.3 = (bf16[13,64,128]{2,1,0:T(8,128)(2,1)S(1)}, bf16[13,64,128]{2,1,0:T(8,128)(2,1)S(1)}, u32[]{:S(2)}, u32[]{:S(2)}) collective-permute-start(bf16[13,64,128]{2,1,0:T(8,128)(2,1)S(1)} %pad_maximum_fusion.1), channel_id=1, source_target_pairs={{1,3},{3,5},{5,7},{7,9},{9,11},{11,13},{13,15},{2,0},{4,2},{6,4},{... | collective-permute-start | bytes 638984 | tf_op jit(solution)/shard_map/ppermute | solution.py:99
  96.3 10.5 %collective-permute-start.8 = (bf16[13,64,128]{2,1,0:T(8,128)(2,1)S(1)}, bf16[13,64,128]{2,1,0:T(8,128)(2,1)S(1)}, u32[]{:S(2)}, u32[]{:S(2)}) collective-permute-start(bf16[13,64,128]{2,1,0:T(8,128)(2,1)S(1)} %pad_maximum_fusion.5), channel_id=1, source_target_pairs={{1,3},{3,5},{5,7},{7,9},{9,11},{11,13},{13,15},{2,0},{4,2},{6,4},{... | collective-permute-start | bytes 638984 | tf_op jit(solution)/shard_map/ppermute | solution.py:99
  107.0 13.6 %collective-permute-start.9 = (bf16[13,64,128]{2,1,0:T(8,128)(2,1)S(1)}, bf16[13,64,128]{2,1,0:T(8,128)(2,1)S(1)}, u32[]{:S(2)}, u32[]{:S(2)}) collective-permute-start(bf16[13,64,128]{2,1,0:T(8,128)(2,1)S(1)} %pad_maximum_fusion.6), channel_id=1, source_target_pairs={{1,5},{3,7},{5,9},{7,11},{9,13},{11,15},{4,0},{6,2},{8,4},{10,6},{... | collective-permute-start | bytes 638984 | tf_op jit(solution)/shard_map/ppermute | solution.py:99
  108.6 14.3 %collective-permute-start.4 = (bf16[13,64,128]{2,1,0:T(8,128)(2,1)S(1)}, bf16[13,64,128]{2,1,0:T(8,128)(2,1)S(1)}, u32[]{:S(2)}, u32[]{:S(2)}) collective-permute-start(bf16[13,64,128]{2,1,0:T(8,128)(2,1)S(1)} %pad_maximum_fusion.2), channel_id=1, source_target_pairs={{1,5},{3,7},{5,9},{7,11},{9,13},{11,15},{4,0},{6,2},{8,4},{10,6},{... | collective-permute-start | bytes 638984 | tf_op jit(solution)/shard_map/ppermute | solution.py:99
  120.9 14.2 %collective-permute-start.10 = (bf16[13,64,128]{2,1,0:T(8,128)(2,1)S(1)}, bf16[13,64,128]{2,1,0:T(8,128)(2,1)S(1)}, u32[]{:S(2)}, u32[]{:S(2)}) collective-permute-start(bf16[13,64,128]{2,1,0:T(8,128)(2,1)S(1)} %pad_maximum_fusion.7), channel_id=1, source_target_pairs={{1,9},{3,11},{5,13},{7,15},{8,0},{10,2},{12,4},{14,6},{17,25},{19,... | collective-permute-start | bytes 638984 | tf_op jit(solution)/shard_map/ppermute | solution.py:99
  123.1 14.3 %collective-permute-start.5 = (bf16[13,64,128]{2,1,0:T(8,128)(2,1)S(1)}, bf16[13,64,128]{2,1,0:T(8,128)(2,1)S(1)}, u32[]{:S(2)}, u32[]{:S(2)}) collective-permute-start(bf16[13,64,128]{2,1,0:T(8,128)(2,1)S(1)} %pad_maximum_fusion.3), channel_id=1, source_target_pairs={{1,9},{3,11},{5,13},{7,15},{8,0},{10,2},{12,4},{14,6},{17,25},{19,... | collective-permute-start | bytes 638984 | tf_op jit(solution)/shard_map/ppermute | solution.py:99
  135.3 2.4 %collective-permute-start.11 = (bf16[12,64,128]{2,1,0:T(8,128)(2,1)S(1)}, bf16[12,64,128]{2,1,0:T(8,128)(2,1)S(1)}, u32[]{:S(2)}, u32[]{:S(2)}) collective-permute-start(bf16[12,64,128]{2,1,0:T(8,128)(2,1)S(1)} %fusion.209), channel_id=1, source_target_pairs={{0,1},{1,0},{2,3},{3,2},{4,5},{5,4},{6,7},{7,6},{8,9},{9,8},{10,11... | collective-permute-start | bytes 589832 | tf_op jit(solution)/shard_map/ppermute | solution.py:134
  137.6 1.5 %collective-permute-start.6 = (bf16[12,64,128]{2,1,0:T(8,128)(2,1)S(1)}, bf16[12,64,128]{2,1,0:T(8,128)(2,1)S(1)}, u32[]{:S(2)}, u32[]{:S(2)}) collective-permute-start(bf16[12,64,128]{2,1,0:T(8,128)(2,1)S(1)} %fusion.101), channel_id=1, source_target_pairs={{0,1},{1,0},{2,3},{3,2},{4,5},{5,4},{6,7},{7,6},{8,9},{9,8},{10,11... | collective-permute-start | bytes 589832 | tf_op jit(solution)/shard_map/ppermute | solution.py:134
  (26 other events, 90.5 us)

commit v7 on v4

--- a/solution.py
+++ b/solution.py
@@ -26,21 +26,21 @@
     owners = jnp.where(is_live, tile_pos // rows, devices)
     one_hot = (owners[:, None] == jnp.arange(devices, dtype=jnp.int32)[None, :]).astype(jnp.int32)
     ranking = jnp.sum(jnp.cumsum(one_hot, axis=0) * one_hot, axis=1) - 1
-    target = jnp.where(is_live, owners * capacity + ranking, -1)
-    match = target[None, :] == jnp.arange(devices * capacity, dtype=jnp.int32)[:, None]
+    target = jnp.where(is_live, owners * capacity + ranking, devices * capacity)
+    picked = jnp.full((devices * capacity,), slots, jnp.int32)
+    picked = picked.at[target].set(jnp.arange(slots, dtype=jnp.int32), mode="drop")
     row_column = (tile_pos % rows + 1).astype(jnp.bfloat16)[:, None]
     source = jnp.concatenate(
         [tile_embeds, jnp.pad(row_column, ((0, 0), (0, 127)))], axis=1
     )
-    send = jnp.dot(match.astype(jnp.bfloat16), source, preferred_element_type=jnp.float32)
-    send = send.astype(jnp.bfloat16).reshape(devices, capacity, width + 128)
+    send = jnp.take(source, picked, axis=0, mode="fill", fill_value=0)
+    send = send.reshape(devices, capacity, width + 128)
     arrived = lax.all_to_all(send, "seq", 0, 0, tiled=True).reshape(devices * capacity, width + 128)
     arrived_rows = arrived[:, width].astype(jnp.float32).astype(jnp.int32) - 1
-    place = arrived_rows[None, :] == jnp.arange(rows, dtype=jnp.int32)[:, None]
-    tiles = jnp.dot(
-        place.astype(jnp.bfloat16), arrived[:, :width], preferred_element_type=jnp.float32
-    )
-    return tiles.astype(jnp.bfloat16)
+    spots = jnp.where(arrived_rows >= 0, arrived_rows, rows)
+    placed = jnp.zeros((rows,), jnp.int32)
+    placed = placed.at[spots].set(jnp.arange(devices * capacity, dtype=jnp.int32), mode="drop")
+    return jnp.take(arrived[:, :width], placed, axis=0, mode="clip")
 
 
 def halo(normed, in_weight, width):

time: 147 us -> 152 us (1.034)
  local copies, waits for them, and re-layouts: 8.73 us -> 16.3 us
  matrix products: 38.4 us -> 31.9 us
  other arithmetic: 12.8 us -> 15.9 us
    scatter x0 -> x2, local copies, waits for them, and re-layouts: none -> 4.87 us  [the longest x1 2.44 us: route_tiles(): placed.at[spots]]
    dot_general x1 -> x0, matrix products: 3.73 us -> none  [route_tiles(): jnp.dot(match.astype(jnp.bfloat16), source, preferred_element_type=jnp.fl...]
    gather x0 -> x2, local copies, waits for them, and re-layouts: none -> 3.6 us  [the longest x1 2.33 us: route_tiles(): send = jnp.take(source, picked, axis=0, mode='fill', fill_value=0)]
    dot_general x1, matrix products: 5.12 us -> 2.63 us  [per_device(): lax.dot_general(in_weight[:, :E], normed, turned, preferred_element_type=...]
    select_n x1 -> x4, other arithmetic: 0.01 us -> 1.62 us  [the longest x2 1.44 us: route_tiles(): send = jnp.take(source, picked, axis=0, mode='fill', fill_value=0)]
    concatenate x0 -> x1, other arithmetic: none -> 1.53 us  [route_tiles(): jnp.concatenate([tile_embeds, jnp.pad(row_column, ((0, 0), (0, 127)))], a...]
where the time goes in v7:
time: 152 us; the launch traced here: 151 us
  waiting for transfers between devices  67.1 us (44%)
  matrix products  31.9 us (21%)
  starting transfers between devices  18.6 us (12%)
  local copies, waits for them, and re-layouts  16.3 us (11%)
  other arithmetic  15.9 us (10%)
  between operations  1.53 us (1%)
    all_to_all x1, waiting for transfers between devices, route_tiles(): lax.all_to_all(send, 'seq', 0, 0, tiled=True)  32.5 us
    ppermute x4, waiting for transfers between devices, transfer(): got = lax.ppermute(payload, 'seq', pairs)  30.4 us
    dot_general x2, matrix products, local_terms(): lax.dot_general(signal, mixing, (((2,), (2,)), ((0,), (0,))), precision=f...  7.79 us
    all_to_all x1, starting transfers between devices, route_tiles(): lax.all_to_all(send, 'seq', 0, 0, tiled=True)  7.55 us
    ppermute x4, starting transfers between devices, transfer(): got = lax.ppermute(payload, 'seq', pairs)  6.61 us
    slice x4, local copies, waits for them, and re-layouts, local_terms(): signal = activated[:E].reshape(HEADS, HEAD_DIM, rows)  6.39 us
    dot_general x1, matrix products, per_device(): lax.dot_general(mixed, out_weight, (((0,), (0,)), ((), ())), preferred_el...  4.66 us
    dot_general x1, matrix products, per_device(): lax.dot_general(in_weight[:, E:], normed, turned, preferred_element_type=...  4.28 us
  transfers between devices with their start and end apart: 8, of which 6 were waited for; matrix products, arithmetic and copies ran while one was open for 8% of the time, Pallas kernels for 0%

profile of v7, /device:TPU:0, one launch (start us, length us, event | category | flops | bytes accessed | tf_op | source)
XLA Modules:
  0.0 151.3 jit_solution(10348670232478989572)
XLA Ops:
  2.9 2.4 %scatter_custom_fusion = s32[512]{0:T(512)S(1)} fusion(s32[512]{0:T(512)S(1)} %compare_select_fusion.5, s32[512]{0:T(512)S(1)} %iota.44, s32[]{:T(128)} %constant.92.clone.1), kind=kCustom, calls=%fused_computation.219 | custom fusion | bytes 2052 | tf_op jit(solution)/shard_map/scatter | solution.py:31
  7.2 2.3 %gather_fusion = bf16[512,1664]{1,0:T(8,128)(2,1)S(1)} fusion(bf16[512,1664]{1,0:T(8,128)(2,1)S(1)} %fusion.63, s32[1024]{0:T(1024)S(1)} %pad_clamp_fusion.1), kind=kCustom, calls=%fused_computation | custom fusion | bytes 3409920 | tf_op jit(solution)/shard_map/jit(_take)/gather | solution.py:36
  11.0 7.6 %all-to-all-start = ((bf16[16,32,1664]{2,1,0:T(8,128)(2,1)}), bf16[16,32,1664]{2,1,0:T(8,128)(2,1)S(1)}, u32[]{:S(2)}, u32[]{:S(2)}) async-start(bf16[16,32,1664]{2,1,0:T(8,128)(2,1)} %broadcast_select_fusion), calls=%async_computation | async-start | bytes 3407872 | tf_op jit(solution)/shard_map/all_to_all | solution.py:38
  20.1 32.5 %all-to-all-done = bf16[16,32,1664]{2,1,0:T(8,128)(2,1)S(1)} async-done(((bf16[16,32,1664]{2,1,0:T(8,128)(2,1)}), bf16[16,32,1664]{2,1,0:T(8,128)(2,1)S(1)}, u32[]{:S(2)}, u32[]{:S(2)}) %all-to-all-start) | async-done | bytes 1703968 | tf_op jit(solution)/shard_map/all_to_all | solution.py:38
  52.9 2.4 %scatter_custom_fusion.1 = s32[256]{0:T(256)S(1)} fusion(s32[512]{0:T(512)S(1)} %fusion.85, s32[512]{0:T(512)S(1)} %iota.45, s32[]{:T(128)} %constant.94.clone.1), kind=kCustom, calls=%fused_computation.248 | custom fusion | bytes 1028 | tf_op jit(solution)/shard_map/scatter | solution.py:42
  56.7 4.0 %multiply_reduce_fusion.1 = (f32[256]{0:T(256)S(1)}, f32[256,1536]{1,0:T(8,128)S(1)}) fusion(f32[1536]{0:T(1024)S(1)} %copy-done.22, bf16[256,1536]{1,0:T(8,128)(2,1)S(1)} %gather_fusion.1, bf16[1536,1536]{1,0:T(8,128)(2,1)} %param.17), kind=kOutput, calls=%fused_computation.75 | convolution fusion | flops 1209925376 | bytes 7085056 | tf_op jit(solution)/shard_map/dot_general | solution.py:154
  63.8 4.3 %fusion.46 = bf16[1792,256]{0,1:T(8,128)(2,1)S(1)} fusion(bf16[256,1536]{1,0:T(8,128)(2,1)S(1)} %multiply_convert_fusion.1, bf16[1536,3328]{1,0:T(8,128)(2,1)} %param.20), kind=kOutput, calls=%fused_computation.45 | convolution fusion | flops 1409744896 | bytes 7208960 | tf_op jit(solution)/shard_map/dot_general | solution.py:158
  68.1 2.6 %divide_multiply_fusion.2 = f32[1536,256]{0,1:T(8,128)} fusion(bf16[256,1536]{1,0:T(8,128)(2,1)S(1)} %multiply_convert_fusion.1, bf16[1536,3328]{1,0:T(8,128)(2,1)S(1)} %bitcast.152), kind=kOutput, calls=%fused_computation.69 | convolution fusion | flops 1210318848 | bytes 7077888 | tf_op jit(solution)/shard_map/dot_general | solution.py:162
  70.7 2.9 %collective-permute-start = (bf16[3,1536]{1,0:T(4,128)(2,1)S(1)}, bf16[3,1536]{1,0:T(4,128)(2,1)S(1)}, u32[]{:S(2)}, u32[]{:S(2)}) collective-permute-start(bf16[3,1536]{1,0:T(4,128)(2,1)S(1)} %get-tuple-element.44), channel_id=1, source_target_pairs={{0,1},{1,2},{2,3},{3,4},{4,5},{5,6},{6,7},{7,8},{8,9},{9,10},{10,1... | collective-permute-start | bytes 27656 | tf_op jit(solution)/shard_map/ppermute | solution.py:50
  75.7 2.5 %collective-permute-done.1 = bf16[3,1536]{1,0:T(4,128)(2,1)S(1)} collective-permute-done((bf16[3,1536]{1,0:T(4,128)(2,1)S(1)}, bf16[3,1536]{1,0:T(4,128)(2,1)S(1)}, u32[]{:S(2)}, u32[]{:S(2)}) %collective-permute-start.1) | collective-permute-done | bytes 9248 | tf_op jit(solution)/shard_map/ppermute | solution.py:51
  79.2 3.3 %divide_multiply_fusion = (f32[1792,256]{0,1:T(8,128)}, f32[1792,256]{0,1:T(8,128)S(1)}) fusion(f32[1792,262]{0,1:T(8,128)S(1)} %maximum_convert_fusion, f32[1792]{0:T(1024)S(1)} %get-tuple-element.25, f32[1792]{0:T(1024)S(1)} %get-tuple-element.26, f32[1792]{0:T(1024)S(1)} %get-tuple-element.20, f32[1792]{0:T(1024)S(1)} %get-tuple-element.19, ...), kind=kLoop, calls=%fused_computation.62 | loop fusion | flops 11010048 | bytes 16586752 | tf_op jit(solution)/shard_map/jit(silu)/mul | solution.py:176
  84.4 2.7 %slice.220 = f32[1536,256]{0,1:T(8,128)} slice(f32[1792,256]{0,1:T(8,128)} %get-tuple-element.42), slice={[0:1536], [0:256]} | slice | bytes 3145728 | tf_op jit(solution)/shard_map/slice | solution.py:60
  87.0 1.9 %copy.28 = f32[1536,256]{1,0:T(8,128)S(1)} copy(f32[1536,256]{0,1:T(8,128)} %slice.220) | data formatting | bytes 3145728 | tf_op jit(solution)/shard_map/slice | solution.py:60
  88.9 1.8 %fusion.66 = f32[24,64,128]{2,1,0:T(8,128)S(1)} fusion(f32[24,64,256]{2,1,0:T(8,128)S(1)} %bitcast.146, f32[24,256]{1,0:T(8,128)} %get-tuple-element.49, f32[1792,256]{0,1:T(8,128)} %get-tuple-element.42), kind=kOutput, calls=%fused_computation.70 | convolution fusion | flops 302383104 | bytes 2514944 | tf_op jit(solution)/shard_map/dot_general | solution.py:82
  91.7 2.5 %collective-permute-start.2 = (bf16[25,64,128]{2,1,0:T(8,128)(2,1)S(1)}, bf16[25,64,128]{2,1,0:T(8,128)(2,1)S(1)}, u32[]{:S(2)}, u32[]{:S(2)}) collective-permute-start(bf16[25,64,128]{2,1,0:T(8,128)(2,1)S(1)} %pad_maximum_fusion), channel_id=1, source_target_pairs={{0,1},{1,0},{2,3},{3,2},{4,5},{5,4},{6,7},{7,6},{8,9},{9,8},{10,11... | collective-permute-start | bytes 1228808 | tf_op jit(solution)/shard_map/ppermute | solution.py:99
  97.4 3.9 %fusion.6 = f32[24,64,256]{2,1,0:T(8,128)S(1)} fusion(f32[24,64,256]{2,1,0:T(8,128)S(1)} %bitcast.147, f32[24,256]{1,0:T(8,128)S(1)} %copy-done.7, f32[24,256]{1,0:T(8,128)S(1)} %copy-done.15, f32[256,256]{1,0:T(8,128)S(1)} %fusion.94, pred[256,256]{1,0:T(8,128)(4,1)S(1)} %copy-done.10), kind=kOutput, calls=%fused_computation.10 | convolution fusion | flops 610271232 | bytes 3522560 | tf_op jit(solution)/shard_map/dot_general | solution.py:80
  101.3 7.3 %collective-permute-done.3 = bf16[25,64,128]{2,1,0:T(8,128)(2,1)S(1)} collective-permute-done((bf16[25,64,128]{2,1,0:T(8,128)(2,1)S(1)}, bf16[25,64,128]{2,1,0:T(8,128)(2,1)S(1)}, u32[]{:S(2)}, u32[]{:S(2)}) %collective-permute-start.3) | collective-permute-done | bytes 409632 | tf_op jit(solution)/shard_map/ppermute | solution.py:99
  110.7 3.9 %fusion = f32[24,64,256]{2,1,0:T(8,128)S(1)} fusion(f32[24,64,256]{2,1,0:T(8,128)S(1)} %bitcast.150, f32[24,256]{1,0:T(8,128)S(1)} %copy-done.5, f32[24,256]{1,0:T(8,128)S(1)} %copy-done.13, f32[256,256]{1,0:T(8,128)S(1)} %fusion.91, pred[256,256]{1,0:T(8,128)(4,1)S(1)} %copy-done.9), kind=kOutput, calls=%fused_computation.4 | convolution fusion | flops 610271232 | bytes 3522560 | tf_op jit(solution)/shard_map/dot_general | solution.py:80
  114.6 9.3 %collective-permute-done.4 = bf16[25,64,128]{2,1,0:T(8,128)(2,1)S(1)} collective-permute-done((bf16[25,64,128]{2,1,0:T(8,128)(2,1)S(1)}, bf16[25,64,128]{2,1,0:T(8,128)(2,1)S(1)}, u32[]{:S(2)}, u32[]{:S(2)}) %collective-permute-start.4) | collective-permute-done | bytes 409632 | tf_op jit(solution)/shard_map/ppermute | solution.py:99
  125.4 13.8 %collective-permute-done.5 = bf16[25,64,128]{2,1,0:T(8,128)(2,1)S(1)} collective-permute-done((bf16[25,64,128]{2,1,0:T(8,128)(2,1)S(1)}, bf16[25,64,128]{2,1,0:T(8,128)(2,1)S(1)}, u32[]{:S(2)}, u32[]{:S(2)}) %collective-permute-start.5) | collective-permute-done | bytes 409632 | tf_op jit(solution)/shard_map/ppermute | solution.py:99
  139.7 1.7 %collective-permute-done.6 = bf16[24,64,128]{2,1,0:T(8,128)(2,1)S(1)} collective-permute-done((bf16[24,64,128]{2,1,0:T(8,128)(2,1)S(1)}, bf16[24,64,128]{2,1,0:T(8,128)(2,1)S(1)}, u32[]{:S(2)}, u32[]{:S(2)}) %collective-permute-start.6) | collective-permute-done | bytes 393248 | tf_op jit(solution)/shard_map/ppermute | solution.py:129
  141.4 1.9 %fusion.74 = f32[24,64,256]{2,1,0:T(8,128)S(1)} fusion(bf16[24,64,128]{2,1,0:T(8,128)(2,1)S(1)} %collective-permute-done.6, f32[24]{0:T(128)S(1)} %bitcast.154, pred[]{:T(512)S(6)} %eq.37, bf16[25,64,128]{2,1,0:T(8,128)(2,1)S(1)} %collective-permute-done.2, f32[1792,256]{0,1:T(8,128)} %get-tuple-element.42, ...), kind=kOutput, calls=%fused_computation.89 | convolution fusion | flops 304349184 | bytes 3671553 | tf_op jit(solution)/shard_map/dot_general | solution.py:196
  144.7 1.9 %multiply_reduce_fusion = (f32[256]{0:T(256)S(1)}, f32[1536,256]{0,1:T(8,128)S(1)}) fusion(f32[1536,256]{0,1:T(8,128)S(1)} %copy.32, f32[1536,256]{0,1:T(8,128)} %divide_multiply_fusion.2), kind=kLoop, calls=%fused_computation.67 | loop fusion | flops 1179392 | bytes 4719616 | tf_op jit(solution)/shard_map/reduce_sum | solution.py:201
  146.6 4.7 %fusion.33 = bf16[256,1536]{1,0:T(8,128)(2,1)} fusion(f32[256,1536]{1,0:T(8,128)S(1)} %copy-done.3, bf16[1536,1536]{1,0:T(8,128)(2,1)} %param.27, f32[1536,256]{0,1:T(8,128)S(1)} %get-tuple-element.34, f32[1536]{0:T(1024)S(1)} %copy-done.23, f32[256]{0:T(256)S(1)} %add_rsqrt_fusion), kind=kOutput, calls=%fused_computation.40 | convolution fusion | flops 1209925632 | bytes 8657920 | tf_op jit(solution)/shard_map/dot_general | solution.py:203
  (131 shorter events, 25.8 us)
Async XLA Ops:
  0.0 60.9 %copy-start = (bf16[1536,24]{0,1:T(8,128)(2,1)S(1)}, bf16[1536,24]{0,1:T(8,128)(2,1)}, u32[]{:S(2)}) copy-start(bf16[1536,24]{0,1:T(8,128)(2,1)} %param.21) | copy-start | bytes 221188
  11.0 8.9 %copy-start.16 = (f32[2,1792]{1,0:T(2,128)S(1)}, f32[2,1792]{1,0:T(2,128)}, u32[]{:S(2)}) copy-start(f32[2,1792]{1,0:T(2,128)} %param.23) | copy-start | bytes 43012
  11.0 9.0 %copy-start.11 = (f32[2,4,1792]{2,1,0:T(4,128)S(1)}, f32[2,4,1792]{2,1,0:T(4,128)}, u32[]{:S(2)}) copy-start(f32[2,4,1792]{2,1,0:T(4,128)} %param.22) | copy-start | bytes 172036
  11.0 9.1 %copy-start.20 = (f32[2,24]{1,0:T(2,128)S(1)}, f32[2,24]{1,0:T(2,128)}, u32[]{:S(2)}) copy-start(f32[2,24]{1,0:T(2,128)} %param.24) | copy-start | bytes 580
  11.0 9.1 %copy-start.21 = (f32[2,24]{1,0:T(2,128)S(1)}, f32[2,24]{1,0:T(2,128)}, u32[]{:S(2)}) copy-start(f32[2,24]{1,0:T(2,128)} %param.25) | copy-start | bytes 580
  11.0 41.7 %all-to-all-start = ((bf16[16,32,1664]{2,1,0:T(8,128)(2,1)}), bf16[16,32,1664]{2,1,0:T(8,128)(2,1)S(1)}, u32[]{:S(2)}, u32[]{:S(2)}) async-start(bf16[16,32,1664]{2,1,0:T(8,128)(2,1)} %broadcast_select_fusion), calls=%async_computation | async-start | bytes 3407872 | tf_op jit(solution)/shard_map/all_to_all | solution.py:38
  56.7 4.0 %copy-start.17 = (f32[1536]{0:T(1024)S(1)}, f32[1536]{0:T(1024)}, u32[]{:S(2)}) copy-start(f32[1536]{0:T(1024)} %param.19) | copy-start | bytes 18436
  56.7 11.4 %slice-start = ((s8[10223616]{0:T(1024)(128)(4,1)}), s8[4194304]{0:T(1024)(128)(4,1)S(1)}, s32[]{:S(2)}) async-start(s8[10223616]{0:T(1024)(128)(4,1)} %bitcast.151), calls=%async_computation.1 | async-start | bytes 8388608
  56.7 11.4 %slice-start.1 = ((s8[10223616]{0:T(1024)(128)(4,1)}), s8[4194304]{0:T(1024)(128)(4,1)S(1)}, s32[]{:S(2)}) async-start(s8[10223616]{0:T(1024)(128)(4,1)} %bitcast.151), calls=%async_computation.2 | async-start | bytes 8388608
  60.7 2.6 %copy-start.2 = (f32[256,1536]{1,0:T(8,128)}, f32[256,1536]{1,0:T(8,128)S(1)}, u32[]{:S(2)}) copy-start(f32[256,1536]{1,0:T(8,128)S(1)} %get-tuple-element.65) | copy-start | bytes 4718596
  63.8 4.3 %slice-start.2 = ((s8[10223616]{0:T(1024)(128)(4,1)}), s8[1835008]{0:T(1024)(128)(4,1)S(1)}, s32[]{:S(2)}) async-start(s8[10223616]{0:T(1024)(128)(4,1)} %bitcast.151), calls=%async_computation.3 | async-start | bytes 3670016
  70.7 5.0 %collective-permute-start = (bf16[3,1536]{1,0:T(4,128)(2,1)S(1)}, bf16[3,1536]{1,0:T(4,128)(2,1)S(1)}, u32[]{:S(2)}, u32[]{:S(2)}) collective-permute-start(bf16[3,1536]{1,0:T(4,128)(2,1)S(1)} %get-tuple-element.44), channel_id=1, source_target_pairs={{0,1},{1,2},{2,3},{3,4},{4,5},{5,6},{6,7},{7,8},{8,9},{9,10},{10,1... | collective-permute-start | bytes 27656 | tf_op jit(solution)/shard_map/ppermute | solution.py:50
  73.6 4.6 %collective-permute-start.1 = (bf16[3,1536]{1,0:T(4,128)(2,1)S(1)}, bf16[3,1536]{1,0:T(4,128)(2,1)S(1)}, u32[]{:S(2)}, u32[]{:S(2)}) collective-permute-start(bf16[3,1536]{1,0:T(4,128)(2,1)S(1)} %get-tuple-element.45), channel_id=1, source_target_pairs={{1,0},{2,1},{3,2},{4,3},{5,4},{6,5},{7,6},{8,7},{9,8},{10,9},{11,1... | collective-permute-start | bytes 27656 | tf_op jit(solution)/shard_map/ppermute | solution.py:51
  91.6 4.2 %copy-start.19 = (f32[24]{0:T(128)S(1)}, f32[24]{0:T(128)}, u32[]{:S(2)}) copy-start(f32[24]{0:T(128)} %get-tuple-element.28) | copy-start | bytes 292
  91.6 4.2 %copy-start.18 = (f32[24]{0:T(128)S(1)}, f32[24]{0:T(128)}, u32[]{:S(2)}) copy-start(f32[24]{0:T(128)} %broadcast_select_fusion.2) | copy-start | bytes 292
  91.7 4.1 %collective-permute-start.2 = (bf16[25,64,128]{2,1,0:T(8,128)(2,1)S(1)}, bf16[25,64,128]{2,1,0:T(8,128)(2,1)S(1)}, u32[]{:S(2)}, u32[]{:S(2)}) collective-permute-start(bf16[25,64,128]{2,1,0:T(8,128)(2,1)S(1)} %pad_maximum_fusion), channel_id=1, source_target_pairs={{0,1},{1,0},{2,3},{3,2},{4,5},{5,4},{6,7},{7,6},{8,9},{9,8},{10,11... | collective-permute-start | bytes 1228808 | tf_op jit(solution)/shard_map/ppermute | solution.py:99
  94.4 3.0 %copy-start.7 = (f32[24,256]{1,0:T(8,128)S(1)}, f32[24,256]{1,0:T(8,128)}, u32[]{:S(2)}) copy-start(f32[24,256]{1,0:T(8,128)} %copy-done.6) | copy-start | bytes 73732
  94.5 3.0 %copy-start.10 = (pred[256,256]{1,0:T(8,128)(4,1)S(1)}, pred[256,256]{1,0:T(8,128)(4,1)}, u32[]{:S(2)}) copy-start(pred[256,256]{1,0:T(8,128)(4,1)} %iota_compare_fusion.1) | copy-start | bytes 196612
  94.5 3.0 %copy-start.15 = (f32[24,256]{1,0:T(8,128)S(1)}, f32[24,256]{1,0:T(8,128)}, u32[]{:S(2)}) copy-start(f32[24,256]{1,0:T(8,128)} %copy-done.14) | copy-start | bytes 73732
  96.1 12.6 %collective-permute-start.3 = (bf16[25,64,128]{2,1,0:T(8,128)(2,1)S(1)}, bf16[25,64,128]{2,1,0:T(8,128)(2,1)S(1)}, u32[]{:S(2)}, u32[]{:S(2)}) collective-permute-start(bf16[25,64,128]{2,1,0:T(8,128)(2,1)S(1)} %pad_maximum_fusion.1), channel_id=1, source_target_pairs={{1,3},{3,5},{5,7},{7,9},{9,11},{11,13},{13,15},{2,0},{4,2},{6,4},{... | collective-permute-start | bytes 1228808 | tf_op jit(solution)/shard_map/ppermute | solution.py:99
  108.7 2.0 %copy-start.9 = (pred[256,256]{1,0:T(8,128)(4,1)S(1)}, pred[256,256]{1,0:T(8,128)(4,1)}, u32[]{:S(2)}) copy-start(pred[256,256]{1,0:T(8,128)(4,1)} %iota_compare_fusion.2) | copy-start | bytes 196612
  109.1 14.7 %collective-permute-start.4 = (bf16[25,64,128]{2,1,0:T(8,128)(2,1)S(1)}, bf16[25,64,128]{2,1,0:T(8,128)(2,1)S(1)}, u32[]{:S(2)}, u32[]{:S(2)}) collective-permute-start(bf16[25,64,128]{2,1,0:T(8,128)(2,1)S(1)} %pad_maximum_fusion.2), channel_id=1, source_target_pairs={{1,5},{3,7},{5,9},{7,11},{9,13},{11,15},{4,0},{6,2},{8,4},{10,6},{... | collective-permute-start | bytes 1228808 | tf_op jit(solution)/shard_map/ppermute | solution.py:99
  124.1 15.1 %collective-permute-start.5 = (bf16[25,64,128]{2,1,0:T(8,128)(2,1)S(1)}, bf16[25,64,128]{2,1,0:T(8,128)(2,1)S(1)}, u32[]{:S(2)}, u32[]{:S(2)}) collective-permute-start(bf16[25,64,128]{2,1,0:T(8,128)(2,1)S(1)} %pad_maximum_fusion.3), channel_id=1, source_target_pairs={{1,9},{3,11},{5,13},{7,15},{8,0},{10,2},{12,4},{14,6},{17,25},{19,... | collective-permute-start | bytes 1228808 | tf_op jit(solution)/shard_map/ppermute | solution.py:99
  139.6 1.8 %collective-permute-start.6 = (bf16[24,64,128]{2,1,0:T(8,128)(2,1)S(1)}, bf16[24,64,128]{2,1,0:T(8,128)(2,1)S(1)}, u32[]{:S(2)}, u32[]{:S(2)}) collective-permute-start(bf16[24,64,128]{2,1,0:T(8,128)(2,1)S(1)} %fusion.165), channel_id=1, source_target_pairs={{0,1},{1,0},{2,3},{3,2},{4,5},{5,4},{6,7},{7,6},{8,9},{9,8},{10,11... | collective-permute-start | bytes 1179656 | tf_op jit(solution)/shard_map/ppermute | solution.py:129
  (11 other events, 18.8 us)

commit v8 on v4

--- a/solution.py
+++ b/solution.py
@@ -199,7 +199,9 @@
         total = total + within + carried
     gated = total.reshape(E, rows) * gate_silu
     mean_sq = jnp.mean(gated * gated, axis=0, keepdims=True)
-    mixed = (gated * lax.rsqrt(mean_sq + epsilon) * out_gain[:, None]).astype(jnp.bfloat16)
+    mixed = lax.optimization_barrier(
+        (gated * lax.rsqrt(mean_sq + epsilon) * out_gain[:, None]).astype(jnp.bfloat16)
+    )
     hidden = embedded.astype(jnp.float32) + lax.dot_general(
         mixed, out_weight, (((0,), (0,)), ((), ())), preferred_element_type=jnp.float32
     )

time: 147 us -> 148 us (level)
  no operation moved by 1% of the time
where the time goes in v8:
time: 148 us
  waiting for transfers between devices  66.6 us (45%)
  matrix products  38.3 us (26%)
  starting transfers between devices  18.6 us (13%)
  other arithmetic  12.9 us (9%)
  local copies, waits for them, and re-layouts  9.9 us (7%)
    all_to_all x1, waiting for transfers between devices, route_tiles(): lax.all_to_all(send, 'seq', 0, 0, tiled=True)  32 us
    ppermute x4, waiting for transfers between devices, transfer(): got = lax.ppermute(payload, 'seq', pairs)  30.4 us
    dot_general x2, matrix products, local_terms(): lax.dot_general(signal, mixing, (((2,), (2,)), ((0,), (0,))), precision=f...  7.79 us
    all_to_all x1, starting transfers between devices, route_tiles(): lax.all_to_all(send, 'seq', 0, 0, tiled=True)  7.56 us
    ppermute x4, starting transfers between devices, transfer(): got = lax.ppermute(payload, 'seq', pairs)  6.61 us
    slice x4, local copies, waits for them, and re-layouts, local_terms(): signal = activated[:E].reshape(HEADS, HEAD_DIM, rows)  6.39 us
    dot_general x1, matrix products, per_device(): lax.dot_general(in_weight[:, :E], normed, turned, preferred_element_type=...  5.12 us
    dot_general x1, matrix products, per_device(): lax.dot_general(mixed, out_weight, (((0,), (0,)), ((), ())), preferred_el...  4.6 us
  transfers between devices with their start and end apart: 8, of which 6 were waited for; matrix products, arithmetic and copies ran while one was open for 8% of the time, Pallas kernels for 0%

profile of v8, /device:TPU:0, one launch (start us, length us, event | category | flops | bytes accessed | tf_op | source)
XLA Modules:
  0.0 147.7 jit_solution(7270401464844786529)
XLA Ops:
  3.1 3.7 %convolution_convert_fusion = bf16[512,1664]{1,0:T(8,128)(2,1)} fusion(bf16[512,1]{1,0:T(8,128)(2,1)S(1)} %broadcast_in_dim.48, bf16[512,1536]{1,0:T(8,128)(2,1)} %param.14, s32[512]{0:T(512)S(1)} %add_select_fusion.2), kind=kOutput, calls=%fused_computation.32 | convolution fusion | flops 878641152 | bytes 3279872 | tf_op jit(solution)/shard_map/dot_general | solution.py:35
  6.8 7.6 %all-to-all-start = ((bf16[16,32,1664]{2,1,0:T(8,128)(2,1)}), bf16[16,32,1664]{2,1,0:T(8,128)(2,1)S(1)}, u32[]{:S(2)}, u32[]{:S(2)}) async-start(bf16[16,32,1664]{2,1,0:T(8,128)(2,1)} %bitcast.3), calls=%async_computation | async-start | bytes 3407872 | tf_op jit(solution)/shard_map/all_to_all | solution.py:37
  16.5 32.0 %all-to-all-done = bf16[16,32,1664]{2,1,0:T(8,128)(2,1)S(1)} async-done(((bf16[16,32,1664]{2,1,0:T(8,128)(2,1)}), bf16[16,32,1664]{2,1,0:T(8,128)(2,1)S(1)}, u32[]{:S(2)}, u32[]{:S(2)}) %all-to-all-start) | async-done | bytes 1703968 | tf_op jit(solution)/shard_map/all_to_all | solution.py:37
  48.7 4.2 %multiply_reduce_fusion.1 = (f32[256]{0:T(256)S(1)}, f32[256,1536]{1,0:T(8,128)S(1)}) fusion(f32[1536]{0:T(1024)S(1)} %copy-done.29, bf16[1536,1536]{1,0:T(8,128)(2,1)} %param.17, bf16[512,1664]{1,0:T(8,128)(2,1)S(1)} %bitcast.151, s32[512]{0:T(512)S(1)} %add_reduce_fusion), kind=kOutput, calls=%fused_computation.76 | convolution fusion | flops 1613102848 | bytes 7875584 | tf_op jit(solution)/shard_map/dot_general | solution.py:154
  56.0 4.3 %fusion.46 = bf16[1792,256]{0,1:T(8,128)(2,1)S(1)} fusion(bf16[256,1536]{1,0:T(8,128)(2,1)S(1)} %multiply_convert_fusion.1, bf16[1536,3328]{1,0:T(8,128)(2,1)} %param.20), kind=kOutput, calls=%fused_computation.43 | convolution fusion | flops 1409744896 | bytes 7208960 | tf_op jit(solution)/shard_map/dot_general | solution.py:158
  60.3 5.1 %divide_multiply_fusion.2 = f32[1536,256]{0,1:T(8,128)} fusion(bf16[256,1536]{1,0:T(8,128)(2,1)S(1)} %multiply_convert_fusion.1, bf16[1536,3328]{1,0:T(8,128)(2,1)} %param.20), kind=kOutput, calls=%fused_computation.70 | convolution fusion | flops 1210318848 | bytes 7077888 | tf_op jit(solution)/shard_map/dot_general | solution.py:162
  65.5 2.9 %collective-permute-start = (bf16[3,1536]{1,0:T(4,128)(2,1)S(1)}, bf16[3,1536]{1,0:T(4,128)(2,1)S(1)}, u32[]{:S(2)}, u32[]{:S(2)}) collective-permute-start(bf16[3,1536]{1,0:T(4,128)(2,1)S(1)} %get-tuple-element.44), channel_id=1, source_target_pairs={{0,1},{1,2},{2,3},{3,4},{4,5},{5,6},{6,7},{7,8},{8,9},{9,10},{10,1... | collective-permute-start | bytes 27656 | tf_op jit(solution)/shard_map/ppermute | solution.py:50
  70.4 2.5 %collective-permute-done.1 = bf16[3,1536]{1,0:T(4,128)(2,1)S(1)} collective-permute-done((bf16[3,1536]{1,0:T(4,128)(2,1)S(1)}, bf16[3,1536]{1,0:T(4,128)(2,1)S(1)}, u32[]{:S(2)}, u32[]{:S(2)}) %collective-permute-start.1) | collective-permute-done | bytes 9248 | tf_op jit(solution)/shard_map/ppermute | solution.py:51
  74.5 3.3 %divide_multiply_fusion = (f32[1792,256]{0,1:T(8,128)}, f32[1792,256]{0,1:T(8,128)S(1)}) fusion(f32[1792,262]{0,1:T(8,128)S(1)} %maximum_convert_fusion, f32[1792]{0:T(1024)S(1)} %copy-done.20, f32[1792]{0:T(1024)S(1)} %copy-done.21, f32[1792]{0:T(1024)S(1)} %get-tuple-element.20, f32[1792]{0:T(1024)S(1)} %get-tuple-element.19, ...), kind=kLoop, calls=%fused_computation.60 | loop fusion | flops 11010048 | bytes 16586752 | tf_op jit(solution)/shard_map/jit(silu)/mul | solution.py:176
  78.0 1.7 %copy.36 = f32[1536,256]{1,0:T(8,128)} copy(f32[1536,256]{0,1:T(8,128)S(1)} %slice.211) | data formatting | bytes 3145728 | tf_op jit(solution)/shard_map/slice | solution.py:60
  79.6 2.7 %slice.216 = f32[1536,256]{0,1:T(8,128)} slice(f32[1792,256]{0,1:T(8,128)} %get-tuple-element.42), slice={[0:1536], [0:256]} | slice | bytes 3145728 | tf_op jit(solution)/shard_map/slice | solution.py:60
  82.3 1.9 %copy.38 = f32[1536,256]{1,0:T(8,128)S(1)} copy(f32[1536,256]{0,1:T(8,128)} %slice.216) | data formatting | bytes 3145728 | tf_op jit(solution)/shard_map/slice | solution.py:60
  84.2 1.8 %fusion.71 = f32[24,64,128]{2,1,0:T(8,128)S(1)} fusion(f32[24,64,256]{2,1,0:T(8,128)S(1)} %bitcast.143, f32[24,256]{1,0:T(8,128)} %get-tuple-element.49, f32[1792,256]{0,1:T(8,128)} %get-tuple-element.42), kind=kOutput, calls=%fused_computation.71 | convolution fusion | flops 302383104 | bytes 2514944 | tf_op jit(solution)/shard_map/dot_general | solution.py:82
  86.9 2.5 %collective-permute-start.2 = (bf16[25,64,128]{2,1,0:T(8,128)(2,1)S(1)}, bf16[25,64,128]{2,1,0:T(8,128)(2,1)S(1)}, u32[]{:S(2)}, u32[]{:S(2)}) collective-permute-start(bf16[25,64,128]{2,1,0:T(8,128)(2,1)S(1)} %pad_maximum_fusion), channel_id=1, source_target_pairs={{0,1},{1,0},{2,3},{3,2},{4,5},{5,4},{6,7},{7,6},{8,9},{9,8},{10,11... | collective-permute-start | bytes 1228808 | tf_op jit(solution)/shard_map/ppermute | solution.py:99
  92.7 3.9 %fusion.6 = f32[24,64,256]{2,1,0:T(8,128)S(1)} fusion(f32[24,64,256]{2,1,0:T(8,128)S(1)} %bitcast.144, f32[24,256]{1,0:T(8,128)S(1)} %copy-done.7, f32[24,256]{1,0:T(8,128)S(1)} %copy-done.15, f32[256,256]{1,0:T(8,128)S(1)} %fusion.102, pred[256,256]{1,0:T(8,128)(4,1)S(1)} %copy-done.10), kind=kOutput, calls=%fused_computation.6 | convolution fusion | flops 610271232 | bytes 3522560 | tf_op jit(solution)/shard_map/dot_general | solution.py:80
  96.6 7.3 %collective-permute-done.3 = bf16[25,64,128]{2,1,0:T(8,128)(2,1)S(1)} collective-permute-done((bf16[25,64,128]{2,1,0:T(8,128)(2,1)S(1)}, bf16[25,64,128]{2,1,0:T(8,128)(2,1)S(1)}, u32[]{:S(2)}, u32[]{:S(2)}) %collective-permute-start.3) | collective-permute-done | bytes 409632 | tf_op jit(solution)/shard_map/ppermute | solution.py:99
  104.4 1.5 %collective-permute-start.4 = (bf16[25,64,128]{2,1,0:T(8,128)(2,1)S(1)}, bf16[25,64,128]{2,1,0:T(8,128)(2,1)S(1)}, u32[]{:S(2)}, u32[]{:S(2)}) collective-permute-start(bf16[25,64,128]{2,1,0:T(8,128)(2,1)S(1)} %pad_maximum_fusion.2), channel_id=1, source_target_pairs={{1,5},{3,7},{5,9},{7,11},{9,13},{11,15},{4,0},{6,2},{8,4},{10,6},{... | collective-permute-start | bytes 1228808 | tf_op jit(solution)/shard_map/ppermute | solution.py:99
  105.9 3.9 %fusion = f32[24,64,256]{2,1,0:T(8,128)S(1)} fusion(f32[24,64,256]{2,1,0:T(8,128)S(1)} %bitcast.147, f32[24,256]{1,0:T(8,128)S(1)} %copy-done.5, f32[24,256]{1,0:T(8,128)S(1)} %copy-done.13, f32[256,256]{1,0:T(8,128)S(1)} %fusion.99, pred[256,256]{1,0:T(8,128)(4,1)S(1)} %copy-done.9), kind=kOutput, calls=%fused_computation | convolution fusion | flops 610271232 | bytes 3522560 | tf_op jit(solution)/shard_map/dot_general | solution.py:80
  109.8 9.3 %collective-permute-done.4 = bf16[25,64,128]{2,1,0:T(8,128)(2,1)S(1)} collective-permute-done((bf16[25,64,128]{2,1,0:T(8,128)(2,1)S(1)}, bf16[25,64,128]{2,1,0:T(8,128)(2,1)S(1)}, u32[]{:S(2)}, u32[]{:S(2)}) %collective-permute-start.4) | collective-permute-done | bytes 409632 | tf_op jit(solution)/shard_map/ppermute | solution.py:99
  120.6 13.8 %collective-permute-done.5 = bf16[25,64,128]{2,1,0:T(8,128)(2,1)S(1)} collective-permute-done((bf16[25,64,128]{2,1,0:T(8,128)(2,1)S(1)}, bf16[25,64,128]{2,1,0:T(8,128)(2,1)S(1)}, u32[]{:S(2)}, u32[]{:S(2)}) %collective-permute-start.5) | collective-permute-done | bytes 409632 | tf_op jit(solution)/shard_map/ppermute | solution.py:99
  134.9 1.7 %collective-permute-done.6 = bf16[24,64,128]{2,1,0:T(8,128)(2,1)S(1)} collective-permute-done((bf16[24,64,128]{2,1,0:T(8,128)(2,1)S(1)}, bf16[24,64,128]{2,1,0:T(8,128)(2,1)S(1)}, u32[]{:S(2)}, u32[]{:S(2)}) %collective-permute-start.6) | collective-permute-done | bytes 393248 | tf_op jit(solution)/shard_map/ppermute | solution.py:129
  136.6 1.9 %fusion.82 = f32[24,64,256]{2,1,0:T(8,128)S(1)} fusion(bf16[24,64,128]{2,1,0:T(8,128)(2,1)S(1)} %collective-permute-done.6, f32[24]{0:T(128)S(1)} %bitcast.153, pred[]{:T(512)S(6)} %eq.69, bf16[25,64,128]{2,1,0:T(8,128)(2,1)S(1)} %collective-permute-done.2, f32[1792,256]{0,1:T(8,128)} %get-tuple-element.42, ...), kind=kOutput, calls=%fused_computation.92 | convolution fusion | flops 304349184 | bytes 3671553 | tf_op jit(solution)/shard_map/dot_general | solution.py:196
  140.0 1.7 %multiply_reduce_fusion = (f32[256]{0:T(256)S(1)}, f32[1536,256]{0,1:T(8,128)S(1)}) fusion(f32[1536,256]{0,1:T(8,128)S(1)} %copy.42, f32[1536,256]{0,1:T(8,128)} %divide_multiply_fusion.2), kind=kLoop, calls=%fused_computation.68 | loop fusion | flops 1179392 | bytes 4719616 | tf_op jit(solution)/shard_map/reduce_sum | solution.py:201
  143.1 4.6 %fusion.33 = bf16[256,1536]{1,0:T(8,128)(2,1)} fusion(f32[256,1536]{1,0:T(8,128)S(1)} %copy-done.3, bf16[1536,256]{0,1:T(8,128)(2,1)S(1)} %multiply_convert_fusion, bf16[1536,1536]{1,0:T(8,128)(2,1)} %param.27), kind=kOutput, calls=%fused_computation.37 | convolution fusion | flops 1208745984 | bytes 7864320 | tf_op jit(solution)/shard_map/dot_general | solution.py:205
  (131 shorter events, 20.6 us)
Async XLA Ops:
  0.0 53.2 %copy-start = (bf16[1536,24]{0,1:T(8,128)(2,1)S(1)}, bf16[1536,24]{0,1:T(8,128)(2,1)}, u32[]{:S(2)}) copy-start(bf16[1536,24]{0,1:T(8,128)(2,1)} %param.21) | copy-start | bytes 221188
  6.8 8.9 %copy-start.22 = (f32[2,1792]{1,0:T(2,128)S(1)}, f32[2,1792]{1,0:T(2,128)}, u32[]{:S(2)}) copy-start(f32[2,1792]{1,0:T(2,128)} %param.23) | copy-start | bytes 43012
  6.8 9.0 %copy-start.11 = (f32[2,4,1792]{2,1,0:T(4,128)S(1)}, f32[2,4,1792]{2,1,0:T(4,128)}, u32[]{:S(2)}) copy-start(f32[2,4,1792]{2,1,0:T(4,128)} %param.22) | copy-start | bytes 172036
  6.8 9.7 %copy-start.27 = (f32[2,24]{1,0:T(2,128)S(1)}, f32[2,24]{1,0:T(2,128)}, u32[]{:S(2)}) copy-start(f32[2,24]{1,0:T(2,128)} %param.24) | copy-start | bytes 580
  6.8 9.7 %copy-start.28 = (f32[2,24]{1,0:T(2,128)S(1)}, f32[2,24]{1,0:T(2,128)}, u32[]{:S(2)}) copy-start(f32[2,24]{1,0:T(2,128)} %param.25) | copy-start | bytes 580
  6.8 41.9 %copy-start.29 = (f32[1536]{0:T(1024)S(1)}, f32[1536]{0:T(1024)}, u32[]{:S(2)}) copy-start(f32[1536]{0:T(1024)} %param.18) | copy-start | bytes 18436
  6.8 41.7 %all-to-all-start = ((bf16[16,32,1664]{2,1,0:T(8,128)(2,1)}), bf16[16,32,1664]{2,1,0:T(8,128)(2,1)S(1)}, u32[]{:S(2)}, u32[]{:S(2)}) async-start(bf16[16,32,1664]{2,1,0:T(8,128)(2,1)} %bitcast.3), calls=%async_computation | async-start | bytes 3407872 | tf_op jit(solution)/shard_map/all_to_all | solution.py:37
  48.7 4.3 %copy-start.23 = (f32[1536]{0:T(1024)S(1)}, f32[1536]{0:T(1024)}, u32[]{:S(2)}) copy-start(f32[1536]{0:T(1024)} %param.19) | copy-start | bytes 18436
  53.5 6.7 %copy-start.4 = (f32[24,256]{1,0:T(8,128)}, f32[24,256]{1,0:T(8,128)S(1)}, u32[]{:S(2)}) copy-start(f32[24,256]{1,0:T(8,128)S(1)} %get-tuple-element.52) | copy-start | bytes 73732
  53.6 6.7 %copy-start.6 = (f32[24,256]{1,0:T(8,128)}, f32[24,256]{1,0:T(8,128)S(1)}, u32[]{:S(2)}) copy-start(f32[24,256]{1,0:T(8,128)S(1)} %get-tuple-element.53) | copy-start | bytes 73732
  53.8 6.5 %copy-start.12 = (f32[24,256]{1,0:T(8,128)}, f32[24,256]{1,0:T(8,128)S(1)}, u32[]{:S(2)}) copy-start(f32[24,256]{1,0:T(8,128)S(1)} %fusion.109) | copy-start | bytes 73732
  54.0 6.3 %copy-start.14 = (f32[24,256]{1,0:T(8,128)}, f32[24,256]{1,0:T(8,128)S(1)}, u32[]{:S(2)}) copy-start(f32[24,256]{1,0:T(8,128)S(1)} %fusion.108) | copy-start | bytes 73732
  56.0 16.9 %slice-start = ((s8[10223616]{0:T(1024)(128)(4,1)}), s8[4194304]{0:T(1024)(128)(4,1)S(1)}, s32[]{:S(2)}) async-start(s8[10223616]{0:T(1024)(128)(4,1)} %bitcast.148), calls=%async_computation.1 | async-start | bytes 8388608
  56.0 16.9 %slice-start.1 = ((s8[10223616]{0:T(1024)(128)(4,1)}), s8[4194304]{0:T(1024)(128)(4,1)S(1)}, s32[]{:S(2)}) async-start(s8[10223616]{0:T(1024)(128)(4,1)} %bitcast.148), calls=%async_computation.2 | async-start | bytes 8388608
  60.3 12.6 %slice-start.2 = ((s8[10223616]{0:T(1024)(128)(4,1)}), s8[1835008]{0:T(1024)(128)(4,1)S(1)}, s32[]{:S(2)}) async-start(s8[10223616]{0:T(1024)(128)(4,1)} %bitcast.148), calls=%async_computation.3 | async-start | bytes 3670016
  65.5 5.0 %collective-permute-start = (bf16[3,1536]{1,0:T(4,128)(2,1)S(1)}, bf16[3,1536]{1,0:T(4,128)(2,1)S(1)}, u32[]{:S(2)}, u32[]{:S(2)}) collective-permute-start(bf16[3,1536]{1,0:T(4,128)(2,1)S(1)} %get-tuple-element.44), channel_id=1, source_target_pairs={{0,1},{1,2},{2,3},{3,4},{4,5},{5,6},{6,7},{7,8},{8,9},{9,10},{10,1... | collective-permute-start | bytes 27656 | tf_op jit(solution)/shard_map/ppermute | solution.py:50
  68.3 4.6 %collective-permute-start.1 = (bf16[3,1536]{1,0:T(4,128)(2,1)S(1)}, bf16[3,1536]{1,0:T(4,128)(2,1)S(1)}, u32[]{:S(2)}, u32[]{:S(2)}) collective-permute-start(bf16[3,1536]{1,0:T(4,128)(2,1)S(1)} %get-tuple-element.45), channel_id=1, source_target_pairs={{1,0},{2,1},{3,2},{4,3},{5,4},{6,5},{7,6},{8,7},{9,8},{10,9},{11,1... | collective-permute-start | bytes 27656 | tf_op jit(solution)/shard_map/ppermute | solution.py:51
  86.8 4.2 %copy-start.26 = (f32[24]{0:T(128)S(1)}, f32[24]{0:T(128)}, u32[]{:S(2)}) copy-start(f32[24]{0:T(128)} %get-tuple-element.28) | copy-start | bytes 292
  86.8 4.2 %copy-start.25 = (f32[24]{0:T(128)S(1)}, f32[24]{0:T(128)}, u32[]{:S(2)}) copy-start(f32[24]{0:T(128)} %broadcast_select_fusion.1) | copy-start | bytes 292
  86.9 4.1 %collective-permute-start.2 = (bf16[25,64,128]{2,1,0:T(8,128)(2,1)S(1)}, bf16[25,64,128]{2,1,0:T(8,128)(2,1)S(1)}, u32[]{:S(2)}, u32[]{:S(2)}) collective-permute-start(bf16[25,64,128]{2,1,0:T(8,128)(2,1)S(1)} %pad_maximum_fusion), channel_id=1, source_target_pairs={{0,1},{1,0},{2,3},{3,2},{4,5},{5,4},{6,7},{7,6},{8,9},{9,8},{10,11... | collective-permute-start | bytes 1228808 | tf_op jit(solution)/shard_map/ppermute | solution.py:99
  91.4 12.6 %collective-permute-start.3 = (bf16[25,64,128]{2,1,0:T(8,128)(2,1)S(1)}, bf16[25,64,128]{2,1,0:T(8,128)(2,1)S(1)}, u32[]{:S(2)}, u32[]{:S(2)}) collective-permute-start(bf16[25,64,128]{2,1,0:T(8,128)(2,1)S(1)} %pad_maximum_fusion.1), channel_id=1, source_target_pairs={{1,3},{3,5},{5,7},{7,9},{9,11},{11,13},{13,15},{2,0},{4,2},{6,4},{... | collective-permute-start | bytes 1228808 | tf_op jit(solution)/shard_map/ppermute | solution.py:99
  104.4 14.7 %collective-permute-start.4 = (bf16[25,64,128]{2,1,0:T(8,128)(2,1)S(1)}, bf16[25,64,128]{2,1,0:T(8,128)(2,1)S(1)}, u32[]{:S(2)}, u32[]{:S(2)}) collective-permute-start(bf16[25,64,128]{2,1,0:T(8,128)(2,1)S(1)} %pad_maximum_fusion.2), channel_id=1, source_target_pairs={{1,5},{3,7},{5,9},{7,11},{9,13},{11,15},{4,0},{6,2},{8,4},{10,6},{... | collective-permute-start | bytes 1228808 | tf_op jit(solution)/shard_map/ppermute | solution.py:99
  119.3 15.1 %collective-permute-start.5 = (bf16[25,64,128]{2,1,0:T(8,128)(2,1)S(1)}, bf16[25,64,128]{2,1,0:T(8,128)(2,1)S(1)}, u32[]{:S(2)}, u32[]{:S(2)}) collective-permute-start(bf16[25,64,128]{2,1,0:T(8,128)(2,1)S(1)} %pad_maximum_fusion.3), channel_id=1, source_target_pairs={{1,9},{3,11},{5,13},{7,15},{8,0},{10,2},{12,4},{14,6},{17,25},{19,... | collective-permute-start | bytes 1228808 | tf_op jit(solution)/shard_map/ppermute | solution.py:99
  134.8 1.8 %collective-permute-start.6 = (bf16[24,64,128]{2,1,0:T(8,128)(2,1)S(1)}, bf16[24,64,128]{2,1,0:T(8,128)(2,1)S(1)}, u32[]{:S(2)}, u32[]{:S(2)}) collective-permute-start(bf16[24,64,128]{2,1,0:T(8,128)(2,1)S(1)} %fusion.172), channel_id=1, source_target_pairs={{0,1},{1,0},{2,3},{3,2},{4,5},{5,4},{6,7},{7,6},{8,9},{9,8},{10,11... | collective-permute-start | bytes 1179656 | tf_op jit(solution)/shard_map/ppermute | solution.py:129
  (17 other events, 27.6 us)

commit v9 on v4

--- a/solution.py
+++ b/solution.py
@@ -128,7 +128,7 @@
         shift *= 2
     other = lax.ppermute(done[1].astype(jnp.bfloat16), "seq", swap).astype(jnp.float32)
     mine_in = first[0][:, None, None] * done[1] + first[1]
-    return jnp.where(is_one, mine_in, other), jnp.where(is_one, other, mine_in), tied
+    return mine_in, other, tied, is_one
 
 
 def per_device(
@@ -177,7 +177,7 @@
         step_size = jax.nn.softplus(dt_raw + dt_bias[direction][:, None])
         decay_rate = -jnp.exp(a_log[direction])
         parts.append(local_terms(activated, step_size, decay_rate, direction == 1))
-    fwd_in, bwd_in, tied = exchange(
+    mine_in, other_in, tied, is_one = exchange(
         (parts[0][2], parts[0][1]),
         (parts[1][2], parts[1][1]),
         [None, (gate_silu, parts[0][0]), parts[1][0]],
@@ -186,17 +186,16 @@
         (gate_silu, within_fwd), within_bwd = tied
     else:
         within_fwd, within_bwd = parts[0][0], parts[1][0]
-    incomings = (fwd_in, bwd_in)
-    withins = (within_fwd, within_bwd)
-    total = jnp.zeros((HEADS, HEAD_DIM, rows), jnp.float32)
-    for direction in range(2):
-        _, own_state, device_decay, decay_to, read_map = parts[direction]
-        within = withins[direction]
-        incoming = incomings[direction]
+    reads = (parts[0][4], parts[1][4])
+    decays_to = (parts[0][3], parts[1][3])
+    total = within_fwd + within_bwd
+    for incoming, first, second in ((mine_in, 0, 1), (other_in, 1, 0)):
+        read_map = jnp.where(is_one, reads[first], reads[second])
+        decay_to = jnp.where(is_one, decays_to[first], decays_to[second])
         carried = lax.dot_general(
             incoming, read_map, (((2,), (0,)), ((), ())), precision=fast
         ) * decay_to[:, None, :]
-        total = total + within + carried
+        total = total + carried
     gated = total.reshape(E, rows) * gate_silu
     mean_sq = jnp.mean(gated * gated, axis=0, keepdims=True)
     mixed = (gated * lax.rsqrt(mean_sq + epsilon) * out_gain[:, None]).astype(jnp.bfloat16)

time: 147 us -> 146 us (level)
  waiting for transfers between devices: 66.6 us -> 64.3 us
    ppermute x1, waiting for transfers between devices: 1.71 us -> 0.01 us  [exchange(): lax.ppermute(done[1].astype(jnp.bfloat16), 'seq', swap).astype(jnp.float32)]
  transfers between devices with their start and end apart: 8 -> 8, of which waited for: 6 -> 5; matrix products, arithmetic and copies ran while one was open for 8% -> 10% of each run, Pallas kernels for 0% -> 0%
where the time goes in v9:
time: 146 us; the launch traced here: 145 us
  waiting for transfers between devices  64.3 us (44%)
  matrix products  39.6 us (27%)
  starting transfers between devices  18.6 us (13%)
  other arithmetic  11.9 us (8%)
  local copies, waits for them, and re-layouts  9.31 us (6%)
  between operations  1.49 us (1%)
    all_to_all x1, waiting for transfers between devices, route_tiles(): lax.all_to_all(send, 'seq', 0, 0, tiled=True)  31.4 us
    ppermute x4, waiting for transfers between devices, transfer(): got = lax.ppermute(payload, 'seq', pairs)  30.4 us
    dot_general x2, matrix products, local_terms(): lax.dot_general(signal, mixing, (((2,), (2,)), ((0,), (0,))), precision=f...  7.78 us
    all_to_all x1, starting transfers between devices, route_tiles(): lax.all_to_all(send, 'seq', 0, 0, tiled=True)  7.56 us
    ppermute x4, starting transfers between devices, transfer(): got = lax.ppermute(payload, 'seq', pairs)  6.6 us
    dot_general x1, matrix products, per_device(): lax.dot_general(in_weight[:, :E], normed, turned, preferred_element_type=...  5.1 us
    slice x4, local copies, waits for them, and re-layouts, local_terms(): signal = activated[:E].reshape(HEADS, HEAD_DIM, rows)  5.1 us
    dot_general x1, matrix products, per_device(): lax.dot_general(mixed, out_weight, (((0,), (0,)), ((), ())), preferred_el...  4.67 us
  transfers between devices with their start and end apart: 8, of which 5 were waited for; matrix products, arithmetic and copies ran while one was open for 10% of the time, Pallas kernels for 0%

profile of v9, /device:TPU:0, one launch (start us, length us, event | category | flops | bytes accessed | tf_op | source)
XLA Modules:
  0.0 145.2 jit_solution(3257103985265724235)
XLA Ops:
  3.1 3.7 %convolution_convert_fusion = bf16[512,1664]{1,0:T(8,128)(2,1)} fusion(bf16[512,1]{1,0:T(8,128)(2,1)S(1)} %broadcast_in_dim.48, bf16[512,1536]{1,0:T(8,128)(2,1)} %param.14, s32[512]{0:T(512)S(1)} %add_select_fusion.2), kind=kOutput, calls=%fused_computation.32 | convolution fusion | flops 878641152 | bytes 3279872 | tf_op jit(solution)/shard_map/dot_general | solution.py:35
  6.8 7.6 %all-to-all-start = ((bf16[16,32,1664]{2,1,0:T(8,128)(2,1)}), bf16[16,32,1664]{2,1,0:T(8,128)(2,1)S(1)}, u32[]{:S(2)}, u32[]{:S(2)}) async-start(bf16[16,32,1664]{2,1,0:T(8,128)(2,1)} %bitcast.3), calls=%async_computation | async-start | bytes 3407872 | tf_op jit(solution)/shard_map/all_to_all | solution.py:37
  17.2 31.4 %all-to-all-done = bf16[16,32,1664]{2,1,0:T(8,128)(2,1)S(1)} async-done(((bf16[16,32,1664]{2,1,0:T(8,128)(2,1)}), bf16[16,32,1664]{2,1,0:T(8,128)(2,1)S(1)}, u32[]{:S(2)}, u32[]{:S(2)}) %all-to-all-start) | async-done | bytes 1703968 | tf_op jit(solution)/shard_map/all_to_all | solution.py:37
  48.7 4.2 %multiply_reduce_fusion.1 = (f32[256]{0:T(256)S(1)}, f32[256,1536]{1,0:T(8,128)S(1)}) fusion(f32[1536]{0:T(1024)S(1)} %copy-done.33, bf16[1536,1536]{1,0:T(8,128)(2,1)} %param.17, bf16[512,1664]{1,0:T(8,128)(2,1)S(1)} %bitcast.151, s32[512]{0:T(512)S(1)} %add_reduce_fusion), kind=kOutput, calls=%fused_computation.76 | convolution fusion | flops 1613102848 | bytes 7875584 | tf_op jit(solution)/shard_map/dot_general | solution.py:154
  56.1 4.3 %fusion.46 = bf16[1792,256]{0,1:T(8,128)(2,1)S(1)} fusion(bf16[256,1536]{1,0:T(8,128)(2,1)S(1)} %multiply_convert_fusion.1, bf16[1536,3328]{1,0:T(8,128)(2,1)} %param.20), kind=kOutput, calls=%fused_computation.43 | convolution fusion | flops 1409744896 | bytes 7208960 | tf_op jit(solution)/shard_map/dot_general | solution.py:158
  60.4 5.1 %divide_multiply_fusion.2 = f32[1536,256]{0,1:T(8,128)} fusion(bf16[256,1536]{1,0:T(8,128)(2,1)S(1)} %multiply_convert_fusion.1, bf16[1536,3328]{1,0:T(8,128)(2,1)} %param.20), kind=kOutput, calls=%fused_computation.70 | convolution fusion | flops 1210318848 | bytes 7077888 | tf_op jit(solution)/shard_map/dot_general | solution.py:162
  65.5 2.9 %collective-permute-start = (bf16[3,1536]{1,0:T(4,128)(2,1)S(1)}, bf16[3,1536]{1,0:T(4,128)(2,1)S(1)}, u32[]{:S(2)}, u32[]{:S(2)}) collective-permute-start(bf16[3,1536]{1,0:T(4,128)(2,1)S(1)} %get-tuple-element.44), channel_id=1, source_target_pairs={{0,1},{1,2},{2,3},{3,4},{4,5},{5,6},{6,7},{7,8},{8,9},{9,10},{10,1... | collective-permute-start | bytes 27656 | tf_op jit(solution)/shard_map/ppermute | solution.py:50
  70.5 2.5 %collective-permute-done.1 = bf16[3,1536]{1,0:T(4,128)(2,1)S(1)} collective-permute-done((bf16[3,1536]{1,0:T(4,128)(2,1)S(1)}, bf16[3,1536]{1,0:T(4,128)(2,1)S(1)}, u32[]{:S(2)}, u32[]{:S(2)}) %collective-permute-start.1) | collective-permute-done | bytes 9248 | tf_op jit(solution)/shard_map/ppermute | solution.py:51
  74.6 2.3 %divide_multiply_fusion = (f32[1792,256]{0,1:T(8,128)S(1)}, f32[1792,256]{0,1:T(8,128)S(1)}) fusion(f32[1792,262]{0,1:T(8,128)S(1)} %maximum_convert_fusion, f32[1792]{0:T(1024)S(1)} %copy-done.25, f32[1792]{0:T(1024)S(1)} %copy-done.26, f32[1792]{0:T(1024)S(1)} %copy-done.20, f32[1792]{0:T(1024)S(1)} %copy-done.19, f32[1792]{0:T(1024)S(1)} %copy-done.17, ...), kind=kLoop, calls=%fused_computation.60 | loop fusion | flops 11010048 | bytes 16586752 | tf_op jit(solution)/shard_map/jit(silu)/mul | solution.py:176
  78.4 1.7 %copy.36 = f32[1536,256]{1,0:T(8,128)} copy(f32[1536,256]{0,1:T(8,128)S(1)} %slice.211) | data formatting | bytes 3145728 | tf_op jit(solution)/shard_map/slice | solution.py:60
  81.4 1.9 %copy.38 = f32[1536,256]{1,0:T(8,128)S(1)} copy(f32[1536,256]{0,1:T(8,128)} %slice.216) | data formatting | bytes 3145728 | tf_op jit(solution)/shard_map/slice | solution.py:60
  83.3 1.6 %fusion.71 = f32[24,64,128]{2,1,0:T(8,128)S(1)} fusion(f32[24,64,256]{2,1,0:T(8,128)S(1)} %bitcast.143, f32[24,256]{1,0:T(8,128)} %get-tuple-element.50, f32[1792,256]{0,1:T(8,128)S(1)} %get-tuple-element.42), kind=kOutput, calls=%fused_computation.71 | convolution fusion | flops 302383104 | bytes 2514944 | tf_op jit(solution)/shard_map/dot_general | solution.py:82
  85.0 1.7 %select_convert_fusion = (bf16[24,64,128]{2,1,0:T(8,128)(2,1)S(1)}, f32[24,64,128]{2,1,0:T(8,128)S(1)}) fusion(f32[24,64,128]{2,1,0:T(8,128)S(1)} %fusion.71, pred[]{:T(512)S(6)} %eq.69, f32[1792,256]{0,1:T(8,128)} %copy-done.1, f32[24,64,256]{2,1,0:T(8,128)S(1)} %bitcast.145, f32[24,256]{1,0:T(8,128)S(1)} %get-tuple-element.51), kind=kOutput, calls=%fused_computation.94 | convolution fusion | flops 302579712 | bytes 3694593 | tf_op jit(solution)/shard_map/dot_general | solution.py:82
  86.8 2.5 %collective-permute-start.2 = (bf16[25,64,128]{2,1,0:T(8,128)(2,1)S(1)}, bf16[25,64,128]{2,1,0:T(8,128)(2,1)S(1)}, u32[]{:S(2)}, u32[]{:S(2)}) collective-permute-start(bf16[25,64,128]{2,1,0:T(8,128)(2,1)S(1)} %pad_maximum_fusion), channel_id=1, source_target_pairs={{0,1},{1,0},{2,3},{3,2},{4,5},{5,4},{6,7},{7,6},{8,9},{9,8},{10,11... | collective-permute-start | bytes 1228808 | tf_op jit(solution)/shard_map/ppermute | solution.py:99
  92.5 3.9 %fusion.6 = f32[24,64,256]{2,1,0:T(8,128)S(1)} fusion(f32[24,64,256]{2,1,0:T(8,128)S(1)} %bitcast.144, f32[24,256]{1,0:T(8,128)S(1)} %copy-done.8, f32[24,256]{1,0:T(8,128)S(1)} %copy-done.16, f32[256,256]{1,0:T(8,128)S(1)} %fusion.106, pred[256,256]{1,0:T(8,128)(4,1)S(1)} %copy-done.11), kind=kOutput, calls=%fused_computation.6 | convolution fusion | flops 610271232 | bytes 3522560 | tf_op jit(solution)/shard_map/dot_general | solution.py:80
  96.4 7.3 %collective-permute-done.3 = bf16[25,64,128]{2,1,0:T(8,128)(2,1)S(1)} collective-permute-done((bf16[25,64,128]{2,1,0:T(8,128)(2,1)S(1)}, bf16[25,64,128]{2,1,0:T(8,128)(2,1)S(1)}, u32[]{:S(2)}, u32[]{:S(2)}) %collective-permute-start.3) | collective-permute-done | bytes 409632 | tf_op jit(solution)/shard_map/ppermute | solution.py:99
  104.2 1.5 %collective-permute-start.4 = (bf16[25,64,128]{2,1,0:T(8,128)(2,1)S(1)}, bf16[25,64,128]{2,1,0:T(8,128)(2,1)S(1)}, u32[]{:S(2)}, u32[]{:S(2)}) collective-permute-start(bf16[25,64,128]{2,1,0:T(8,128)(2,1)S(1)} %pad_maximum_fusion.2), channel_id=1, source_target_pairs={{1,5},{3,7},{5,9},{7,11},{9,13},{11,15},{4,0},{6,2},{8,4},{10,6},{... | collective-permute-start | bytes 1228808 | tf_op jit(solution)/shard_map/ppermute | solution.py:99
  105.7 3.9 %fusion = f32[24,64,256]{2,1,0:T(8,128)S(1)} fusion(f32[24,64,256]{2,1,0:T(8,128)S(1)} %bitcast.146, f32[24,256]{1,0:T(8,128)S(1)} %copy-done.6, f32[24,256]{1,0:T(8,128)S(1)} %copy-done.14, f32[256,256]{1,0:T(8,128)S(1)} %fusion.109, pred[256,256]{1,0:T(8,128)(4,1)S(1)} %copy-done.10), kind=kOutput, calls=%fused_computation | convolution fusion | flops 610271232 | bytes 3522560 | tf_op jit(solution)/shard_map/dot_general | solution.py:80
  109.6 9.3 %collective-permute-done.4 = bf16[25,64,128]{2,1,0:T(8,128)(2,1)S(1)} collective-permute-done((bf16[25,64,128]{2,1,0:T(8,128)(2,1)S(1)}, bf16[25,64,128]{2,1,0:T(8,128)(2,1)S(1)}, u32[]{:S(2)}, u32[]{:S(2)}) %collective-permute-start.4) | collective-permute-done | bytes 409632 | tf_op jit(solution)/shard_map/ppermute | solution.py:99
  120.5 13.8 %collective-permute-done.5 = bf16[25,64,128]{2,1,0:T(8,128)(2,1)S(1)} collective-permute-done((bf16[25,64,128]{2,1,0:T(8,128)(2,1)S(1)}, bf16[25,64,128]{2,1,0:T(8,128)(2,1)S(1)}, u32[]{:S(2)}, u32[]{:S(2)}) %collective-permute-start.5) | collective-permute-done | bytes 409632 | tf_op jit(solution)/shard_map/ppermute | solution.py:99
  134.7 1.8 %fusion.79 = f32[24,64,256]{2,1,0:T(8,128)S(1)} fusion(f32[24]{0:T(128)S(1)} %get-tuple-element.39, f32[24]{0:T(128)S(1)} %mul.372, f32[24]{0:T(128)S(1)} %bitcast.153, bf16[25,64,128]{2,1,0:T(8,128)(2,1)S(1)} %collective-permute-done.5, bf16[25,64,128]{2,1,0:T(8,128)(2,1)S(1)} %collective-permute-done.2, ...), kind=kOutput, calls=%fused_computation.87 | convolution fusion | flops 303988736 | bytes 3409409 | tf_op jit(solution)/shard_map/dot_general | solution.py:195
  136.6 1.6 %multiply_add_fusion = f32[24,64,256]{2,1,0:T(8,128)S(1)} fusion(f32[24,64,256]{2,1,0:T(8,128)S(1)} %fusion.79, f32[24,64,256]{2,1,0:T(8,128)S(1)} %fusion.6, f32[24,64,256]{2,1,0:T(8,128)S(1)} %fusion, bf16[24,64,128]{2,1,0:T(8,128)(2,1)S(1)} %collective-permute-done.6, f32[24,256]{1,0:T(8,128)S(1)} %get-tuple-element.47, ...), kind=kOutput, calls=%fused_computation.69 | convolution fusion | flops 303988736 | bytes 6995969 | tf_op jit(solution)/shard_map/dot_general | solution.py:195
  138.7 1.9 %multiply_reduce_fusion = (f32[256]{0:T(256)S(1)}, f32[1536,256]{0,1:T(8,128)S(1)}) fusion(f32[1536,256]{0,1:T(8,128)S(1)} %copy.42, f32[1536,256]{0,1:T(8,128)} %divide_multiply_fusion.2), kind=kLoop, calls=%fused_computation.68 | loop fusion | flops 1179392 | bytes 4719616 | tf_op jit(solution)/shard_map/reduce_sum | solution.py:200
  140.6 4.7 %fusion.33 = bf16[256,1536]{1,0:T(8,128)(2,1)} fusion(f32[256,1536]{1,0:T(8,128)S(1)} %copy-done.4, bf16[1536,1536]{1,0:T(8,128)(2,1)} %param.27, f32[1536,256]{0,1:T(8,128)S(1)} %get-tuple-element.34, f32[1536]{0:T(1024)S(1)} %copy-done.34, f32[256]{0:T(256)S(1)} %add_rsqrt_fusion), kind=kOutput, calls=%fused_computation.37 | convolution fusion | flops 1209925632 | bytes 8657920 | tf_op jit(solution)/shard_map/dot_general | solution.py:202
  (140 shorter events, 20.8 us)
Async XLA Ops:
  0.0 53.2 %copy-start = (bf16[1536,24]{0,1:T(8,128)(2,1)S(1)}, bf16[1536,24]{0,1:T(8,128)(2,1)}, u32[]{:S(2)}) copy-start(bf16[1536,24]{0,1:T(8,128)(2,1)} %param.21) | copy-start | bytes 221188
  6.8 8.9 %copy-start.27 = (f32[2,1792]{1,0:T(2,128)S(1)}, f32[2,1792]{1,0:T(2,128)}, u32[]{:S(2)}) copy-start(f32[2,1792]{1,0:T(2,128)} %param.23) | copy-start | bytes 43012
  6.8 9.6 %copy-start.12 = (f32[2,4,1792]{2,1,0:T(4,128)S(1)}, f32[2,4,1792]{2,1,0:T(4,128)}, u32[]{:S(2)}) copy-start(f32[2,4,1792]{2,1,0:T(4,128)} %param.22) | copy-start | bytes 172036
  6.8 10.3 %copy-start.31 = (f32[2,24]{1,0:T(2,128)S(1)}, f32[2,24]{1,0:T(2,128)}, u32[]{:S(2)}) copy-start(f32[2,24]{1,0:T(2,128)} %param.24) | copy-start | bytes 580
  6.8 10.3 %copy-start.32 = (f32[2,24]{1,0:T(2,128)S(1)}, f32[2,24]{1,0:T(2,128)}, u32[]{:S(2)}) copy-start(f32[2,24]{1,0:T(2,128)} %param.25) | copy-start | bytes 580
  6.8 41.9 %copy-start.33 = (f32[1536]{0:T(1024)S(1)}, f32[1536]{0:T(1024)}, u32[]{:S(2)}) copy-start(f32[1536]{0:T(1024)} %param.18) | copy-start | bytes 18436
  6.8 41.7 %all-to-all-start = ((bf16[16,32,1664]{2,1,0:T(8,128)(2,1)}), bf16[16,32,1664]{2,1,0:T(8,128)(2,1)S(1)}, u32[]{:S(2)}, u32[]{:S(2)}) async-start(bf16[16,32,1664]{2,1,0:T(8,128)(2,1)} %bitcast.3), calls=%async_computation | async-start | bytes 3407872 | tf_op jit(solution)/shard_map/all_to_all | solution.py:37
  48.7 4.3 %copy-start.28 = (f32[1536]{0:T(1024)S(1)}, f32[1536]{0:T(1024)}, u32[]{:S(2)}) copy-start(f32[1536]{0:T(1024)} %param.19) | copy-start | bytes 18436
  52.9 2.6 %copy-start.3 = (f32[256,1536]{1,0:T(8,128)}, f32[256,1536]{1,0:T(8,128)S(1)}, u32[]{:S(2)}) copy-start(f32[256,1536]{1,0:T(8,128)S(1)} %get-tuple-element.65) | copy-start | bytes 4718596
  56.1 16.9 %slice-start = ((s8[10223616]{0:T(1024)(128)(4,1)}), s8[4194304]{0:T(1024)(128)(4,1)S(1)}, s32[]{:S(2)}) async-start(s8[10223616]{0:T(1024)(128)(4,1)} %bitcast.148), calls=%async_computation.1 | async-start | bytes 8388608
  56.1 16.9 %slice-start.1 = ((s8[10223616]{0:T(1024)(128)(4,1)}), s8[4194304]{0:T(1024)(128)(4,1)S(1)}, s32[]{:S(2)}) async-start(s8[10223616]{0:T(1024)(128)(4,1)} %bitcast.148), calls=%async_computation.2 | async-start | bytes 8388608
  60.4 12.6 %slice-start.2 = ((s8[10223616]{0:T(1024)(128)(4,1)}), s8[1835008]{0:T(1024)(128)(4,1)S(1)}, s32[]{:S(2)}) async-start(s8[10223616]{0:T(1024)(128)(4,1)} %bitcast.148), calls=%async_computation.3 | async-start | bytes 3670016
  65.5 5.0 %collective-permute-start = (bf16[3,1536]{1,0:T(4,128)(2,1)S(1)}, bf16[3,1536]{1,0:T(4,128)(2,1)S(1)}, u32[]{:S(2)}, u32[]{:S(2)}) collective-permute-start(bf16[3,1536]{1,0:T(4,128)(2,1)S(1)} %get-tuple-element.44), channel_id=1, source_target_pairs={{0,1},{1,2},{2,3},{3,4},{4,5},{5,6},{6,7},{7,8},{8,9},{9,10},{10,1... | collective-permute-start | bytes 27656 | tf_op jit(solution)/shard_map/ppermute | solution.py:50
  68.4 4.6 %collective-permute-start.1 = (bf16[3,1536]{1,0:T(4,128)(2,1)S(1)}, bf16[3,1536]{1,0:T(4,128)(2,1)S(1)}, u32[]{:S(2)}, u32[]{:S(2)}) collective-permute-start(bf16[3,1536]{1,0:T(4,128)(2,1)S(1)} %get-tuple-element.45), channel_id=1, source_target_pairs={{1,0},{2,1},{3,2},{4,3},{5,4},{6,5},{7,6},{8,7},{9,8},{10,9},{11,1... | collective-permute-start | bytes 27656 | tf_op jit(solution)/shard_map/ppermute | solution.py:51
  86.7 4.2 %copy-start.30 = (f32[24]{0:T(128)S(1)}, f32[24]{0:T(128)}, u32[]{:S(2)}) copy-start(f32[24]{0:T(128)} %get-tuple-element.28) | copy-start | bytes 292
  86.7 4.2 %copy-start.29 = (f32[24]{0:T(128)S(1)}, f32[24]{0:T(128)}, u32[]{:S(2)}) copy-start(f32[24]{0:T(128)} %broadcast_select_fusion.1) | copy-start | bytes 292
  86.8 4.1 %collective-permute-start.2 = (bf16[25,64,128]{2,1,0:T(8,128)(2,1)S(1)}, bf16[25,64,128]{2,1,0:T(8,128)(2,1)S(1)}, u32[]{:S(2)}, u32[]{:S(2)}) collective-permute-start(bf16[25,64,128]{2,1,0:T(8,128)(2,1)S(1)} %pad_maximum_fusion), channel_id=1, source_target_pairs={{0,1},{1,0},{2,3},{3,2},{4,5},{5,4},{6,7},{7,6},{8,9},{9,8},{10,11... | collective-permute-start | bytes 1228808 | tf_op jit(solution)/shard_map/ppermute | solution.py:99
  91.2 12.6 %collective-permute-start.3 = (bf16[25,64,128]{2,1,0:T(8,128)(2,1)S(1)}, bf16[25,64,128]{2,1,0:T(8,128)(2,1)S(1)}, u32[]{:S(2)}, u32[]{:S(2)}) collective-permute-start(bf16[25,64,128]{2,1,0:T(8,128)(2,1)S(1)} %pad_maximum_fusion.1), channel_id=1, source_target_pairs={{1,3},{3,5},{5,7},{7,9},{9,11},{11,13},{13,15},{2,0},{4,2},{6,4},{... | collective-permute-start | bytes 1228808 | tf_op jit(solution)/shard_map/ppermute | solution.py:99
  103.7 2.0 %copy-start.6 = (f32[24,256]{1,0:T(8,128)S(1)}, f32[24,256]{1,0:T(8,128)}, u32[]{:S(2)}) copy-start(f32[24,256]{1,0:T(8,128)} %copy-done.5) | copy-start | bytes 73732
  103.7 2.0 %copy-start.10 = (pred[256,256]{1,0:T(8,128)(4,1)S(1)}, pred[256,256]{1,0:T(8,128)(4,1)}, u32[]{:S(2)}) copy-start(pred[256,256]{1,0:T(8,128)(4,1)} %iota_compare_fusion.7) | copy-start | bytes 196612
  103.8 2.0 %copy-start.14 = (f32[24,256]{1,0:T(8,128)S(1)}, f32[24,256]{1,0:T(8,128)}, u32[]{:S(2)}) copy-start(f32[24,256]{1,0:T(8,128)} %copy-done.13) | copy-start | bytes 73732
  104.2 14.7 %collective-permute-start.4 = (bf16[25,64,128]{2,1,0:T(8,128)(2,1)S(1)}, bf16[25,64,128]{2,1,0:T(8,128)(2,1)S(1)}, u32[]{:S(2)}, u32[]{:S(2)}) collective-permute-start(bf16[25,64,128]{2,1,0:T(8,128)(2,1)S(1)} %pad_maximum_fusion.2), channel_id=1, source_target_pairs={{1,5},{3,7},{5,9},{7,11},{9,13},{11,15},{4,0},{6,2},{8,4},{10,6},{... | collective-permute-start | bytes 1228808 | tf_op jit(solution)/shard_map/ppermute | solution.py:99
  119.2 15.1 %collective-permute-start.5 = (bf16[25,64,128]{2,1,0:T(8,128)(2,1)S(1)}, bf16[25,64,128]{2,1,0:T(8,128)(2,1)S(1)}, u32[]{:S(2)}, u32[]{:S(2)}) collective-permute-start(bf16[25,64,128]{2,1,0:T(8,128)(2,1)S(1)} %pad_maximum_fusion.3), channel_id=1, source_target_pairs={{1,9},{3,11},{5,13},{7,15},{8,0},{10,2},{12,4},{14,6},{17,25},{19,... | collective-permute-start | bytes 1228808 | tf_op jit(solution)/shard_map/ppermute | solution.py:99
  134.7 1.9 %collective-permute-start.6 = (bf16[24,64,128]{2,1,0:T(8,128)(2,1)S(1)}, bf16[24,64,128]{2,1,0:T(8,128)(2,1)S(1)}, u32[]{:S(2)}, u32[]{:S(2)}) collective-permute-start(bf16[24,64,128]{2,1,0:T(8,128)(2,1)S(1)} %fusion.89), channel_id=1, source_target_pairs={{0,1},{1,0},{2,3},{3,2},{4,5},{5,4},{6,7},{7,6},{8,9},{9,8},{10,11... | collective-permute-start | bytes 1179656 | tf_op jit(solution)/shard_map/ppermute | solution.py:129
  (22 other events, 29.0 us)

commit v10 on v9

--- a/solution.py
+++ b/solution.py
@@ -97,9 +97,9 @@
     extra = jnp.pad(extra, ((0, state.shape[1] - 2), (0, state.shape[2] - decay.shape[0])))
     payload = jnp.concatenate([state.astype(jnp.bfloat16), extra[None]], axis=0)
     got = lax.ppermute(payload, "seq", pairs)
-    heads = decay.shape[0]
-    got_decay = got[heads, 0, :heads].astype(jnp.float32) + got[heads, 1, :heads].astype(jnp.float32)
-    return got_decay, got[:heads].astype(jnp.float32)
+    heads, slab = decay.shape[0], state.shape[0]
+    got_decay = got[slab, 0, :heads].astype(jnp.float32) + got[slab, 1, :heads].astype(jnp.float32)
+    return got_decay, got[:slab].astype(jnp.float32)
 
 
 def exchange(forward, backward, ties):
@@ -120,7 +120,18 @@
         pairs = [(2 * k + 1, 2 * (k + shift) + 1) for k in range(chips - shift)]
         pairs += [(2 * (k + shift), 2 * k) for k in range(chips - shift)]
         valid = jnp.where(is_one, chip >= shift, chip + shift < chips)
-        got_decay, got_state = transfer(run, pairs)
+        if 2 * shift >= chips and chips - shift == shift:
+            half = run[1].shape[0] // 2
+            hand = [(2 * k + 1, 2 * k) for k in range(shift)]
+            hand += [(2 * k, 2 * k + 1) for k in range(shift, chips)]
+            handed = lax.ppermute(run[1][half:].astype(jnp.bfloat16), "seq", hand)
+            got_decay, got_low = transfer((run[0], run[1][:half]), pairs)
+            relay = [(2 * k, 2 * (k + shift) + 1) for k in range(shift)]
+            relay += [(2 * (k + shift) + 1, 2 * k) for k in range(shift)]
+            got_high = lax.ppermute(handed, "seq", relay).astype(jnp.float32)
+            got_state = jnp.concatenate([got_low, got_high], axis=0)
+        else:
+            got_decay, got_state = transfer(run, pairs)
         got = (jnp.where(valid, got_decay, 1.0), got_state)
         done = combine(got, done)
         if 2 * shift < chips:

time: 146 us -> 147 us (level)
  starting transfers between devices: 18.6 us -> 23.6 us
  waiting for transfers between devices: 64.3 us -> 60.6 us
    ppermute x4, waiting for transfers between devices: 30.4 us -> 24.8 us  [transfer(): got = lax.ppermute(payload, 'seq', pairs)]
    ppermute x0 -> x2, starting transfers between devices: none -> 4.99 us  [the longest x1 3.69 us: exchange(): got_high = lax.ppermute(handed, 'seq', relay).astype(jnp.float32)]
    ppermute x0 -> x2, waiting for transfers between devices: none -> 1.9 us  [the longest x1 1.21 us: exchange(): got_high = lax.ppermute(handed, 'seq', relay).astype(jnp.float32)]
  transfers between devices with their start and end apart: 8 -> 10, of which waited for: 5 -> 7; matrix products, arithmetic and copies ran while one was open for 10% -> 10% of each run, Pallas kernels for 0% -> 0%
where the time goes in v10:
time: 147 us
  waiting for transfers between devices  60.6 us (41%)
  matrix products  39.6 us (27%)
  starting transfers between devices  23.6 us (16%)
  other arithmetic  11.9 us (8%)
  local copies, waits for them, and re-layouts  9.33 us (6%)
  between operations  1.52 us (1%)
    all_to_all x1, waiting for transfers between devices, route_tiles(): lax.all_to_all(send, 'seq', 0, 0, tiled=True)  31.4 us
    ppermute x4, waiting for transfers between devices, transfer(): got = lax.ppermute(payload, 'seq', pairs)  24.8 us
    dot_general x2, matrix products, local_terms(): lax.dot_general(signal, mixing, (((2,), (2,)), ((0,), (0,))), precision=f...  7.78 us
    all_to_all x1, starting transfers between devices, route_tiles(): lax.all_to_all(send, 'seq', 0, 0, tiled=True)  7.56 us
    ppermute x4, starting transfers between devices, transfer(): got = lax.ppermute(payload, 'seq', pairs)  6.6 us
    dot_general x1, matrix products, per_device(): lax.dot_general(in_weight[:, :E], normed, turned, preferred_element_type=...  5.1 us
    slice x4, local copies, waits for them, and re-layouts, local_terms(): signal = activated[:E].reshape(HEADS, HEAD_DIM, rows)  5.09 us
    dot_general x1, matrix products, per_device(): lax.dot_general(mixed, out_weight, (((0,), (0,)), ((), ())), preferred_el...  4.65 us
  transfers between devices with their start and end apart: 10, of which 7 were waited for; matrix products, arithmetic and copies ran while one was open for 10% of the time, Pallas kernels for 0%

profile of v10, /device:TPU:0, one launch (start us, length us, event | category | flops | bytes accessed | tf_op | source)
XLA Modules:
  0.0 146.6 jit_solution(841447755940842463)
XLA Ops:
  3.1 3.8 %convolution_convert_fusion = bf16[512,1664]{1,0:T(8,128)(2,1)} fusion(bf16[512,1]{1,0:T(8,128)(2,1)S(1)} %broadcast_in_dim.48, bf16[512,1536]{1,0:T(8,128)(2,1)} %param.14, s32[512]{0:T(512)S(1)} %add_select_fusion.2), kind=kOutput, calls=%fused_computation.32 | convolution fusion | flops 878641152 | bytes 3279872 | tf_op jit(solution)/shard_map/dot_general | solution.py:35
  6.8 7.6 %all-to-all-start = ((bf16[16,32,1664]{2,1,0:T(8,128)(2,1)}), bf16[16,32,1664]{2,1,0:T(8,128)(2,1)S(1)}, u32[]{:S(2)}, u32[]{:S(2)}) async-start(bf16[16,32,1664]{2,1,0:T(8,128)(2,1)} %bitcast.3), calls=%async_computation | async-start | bytes 3407872 | tf_op jit(solution)/shard_map/all_to_all | solution.py:37
  17.2 31.4 %all-to-all-done = bf16[16,32,1664]{2,1,0:T(8,128)(2,1)S(1)} async-done(((bf16[16,32,1664]{2,1,0:T(8,128)(2,1)}), bf16[16,32,1664]{2,1,0:T(8,128)(2,1)S(1)}, u32[]{:S(2)}, u32[]{:S(2)}) %all-to-all-start) | async-done | bytes 1703968 | tf_op jit(solution)/shard_map/all_to_all | solution.py:37
  48.7 4.2 %multiply_reduce_fusion.1 = (f32[256]{0:T(256)S(1)}, f32[256,1536]{1,0:T(8,128)S(1)}) fusion(f32[1536]{0:T(1024)S(1)} %copy-done.33, bf16[1536,1536]{1,0:T(8,128)(2,1)} %param.17, bf16[512,1664]{1,0:T(8,128)(2,1)S(1)} %bitcast.151, s32[512]{0:T(512)S(1)} %add_reduce_fusion), kind=kOutput, calls=%fused_computation.76 | convolution fusion | flops 1613102848 | bytes 7875584 | tf_op jit(solution)/shard_map/dot_general | solution.py:165
  56.1 4.3 %fusion.46 = bf16[1792,256]{0,1:T(8,128)(2,1)S(1)} fusion(bf16[256,1536]{1,0:T(8,128)(2,1)S(1)} %multiply_convert_fusion.1, bf16[1536,3328]{1,0:T(8,128)(2,1)} %param.20), kind=kOutput, calls=%fused_computation.43 | convolution fusion | flops 1409744896 | bytes 7208960 | tf_op jit(solution)/shard_map/dot_general | solution.py:169
  60.4 5.1 %divide_multiply_fusion.2 = f32[1536,256]{0,1:T(8,128)} fusion(bf16[256,1536]{1,0:T(8,128)(2,1)S(1)} %multiply_convert_fusion.1, bf16[1536,3328]{1,0:T(8,128)(2,1)} %param.20), kind=kOutput, calls=%fused_computation.70 | convolution fusion | flops 1210318848 | bytes 7077888 | tf_op jit(solution)/shard_map/dot_general | solution.py:173
  65.5 2.9 %collective-permute-start = (bf16[3,1536]{1,0:T(4,128)(2,1)S(1)}, bf16[3,1536]{1,0:T(4,128)(2,1)S(1)}, u32[]{:S(2)}, u32[]{:S(2)}) collective-permute-start(bf16[3,1536]{1,0:T(4,128)(2,1)S(1)} %get-tuple-element.44), channel_id=1, source_target_pairs={{0,1},{1,2},{2,3},{3,4},{4,5},{5,6},{6,7},{7,8},{8,9},{9,10},{10,1... | collective-permute-start | bytes 27656 | tf_op jit(solution)/shard_map/ppermute | solution.py:50
  70.5 2.5 %collective-permute-done.1 = bf16[3,1536]{1,0:T(4,128)(2,1)S(1)} collective-permute-done((bf16[3,1536]{1,0:T(4,128)(2,1)S(1)}, bf16[3,1536]{1,0:T(4,128)(2,1)S(1)}, u32[]{:S(2)}, u32[]{:S(2)}) %collective-permute-start.1) | collective-permute-done | bytes 9248 | tf_op jit(solution)/shard_map/ppermute | solution.py:51
  74.7 2.3 %divide_multiply_fusion = (f32[1792,256]{0,1:T(8,128)S(1)}, f32[1792,256]{0,1:T(8,128)S(1)}) fusion(f32[1792,262]{0,1:T(8,128)S(1)} %maximum_convert_fusion, f32[1792]{0:T(1024)S(1)} %copy-done.25, f32[1792]{0:T(1024)S(1)} %copy-done.26, f32[1792]{0:T(1024)S(1)} %copy-done.20, f32[1792]{0:T(1024)S(1)} %copy-done.19, f32[1792]{0:T(1024)S(1)} %copy-done.17, ...), kind=kLoop, calls=%fused_computation.60 | loop fusion | flops 11010048 | bytes 16586752 | tf_op jit(solution)/shard_map/jit(silu)/mul | solution.py:187
  78.4 1.7 %copy.36 = f32[1536,256]{1,0:T(8,128)} copy(f32[1536,256]{0,1:T(8,128)S(1)} %slice.221) | data formatting | bytes 3145728 | tf_op jit(solution)/shard_map/slice | solution.py:60
  81.4 1.9 %copy.38 = f32[1536,256]{1,0:T(8,128)S(1)} copy(f32[1536,256]{0,1:T(8,128)} %slice.226) | data formatting | bytes 3145728 | tf_op jit(solution)/shard_map/slice | solution.py:60
  83.3 1.6 %fusion.71 = f32[24,64,128]{2,1,0:T(8,128)S(1)} fusion(f32[24,64,256]{2,1,0:T(8,128)S(1)} %bitcast.143, f32[24,256]{1,0:T(8,128)} %get-tuple-element.52, f32[1792,256]{0,1:T(8,128)S(1)} %get-tuple-element.42), kind=kOutput, calls=%fused_computation.71 | convolution fusion | flops 302383104 | bytes 2514944 | tf_op jit(solution)/shard_map/dot_general | solution.py:82
  85.0 1.7 %select_convert_fusion = (bf16[24,64,128]{2,1,0:T(8,128)(2,1)S(1)}, f32[24,64,128]{2,1,0:T(8,128)S(1)}) fusion(f32[24,64,128]{2,1,0:T(8,128)S(1)} %fusion.71, pred[]{:T(512)S(6)} %eq.69, f32[1792,256]{0,1:T(8,128)} %copy-done.1, f32[24,64,256]{2,1,0:T(8,128)S(1)} %bitcast.145, f32[24,256]{1,0:T(8,128)S(1)} %get-tuple-element.53), kind=kOutput, calls=%fused_computation.94 | convolution fusion | flops 302579712 | bytes 3694593 | tf_op jit(solution)/shard_map/dot_general | solution.py:82
  86.8 2.5 %collective-permute-start.2 = (bf16[25,64,128]{2,1,0:T(8,128)(2,1)S(1)}, bf16[25,64,128]{2,1,0:T(8,128)(2,1)S(1)}, u32[]{:S(2)}, u32[]{:S(2)}) collective-permute-start(bf16[25,64,128]{2,1,0:T(8,128)(2,1)S(1)} %pad_maximum_fusion), channel_id=1, source_target_pairs={{0,1},{1,0},{2,3},{3,2},{4,5},{5,4},{6,7},{7,6},{8,9},{9,8},{10,11... | collective-permute-start | bytes 1228808 | tf_op jit(solution)/shard_map/ppermute | solution.py:99
  92.5 3.9 %fusion.6 = f32[24,64,256]{2,1,0:T(8,128)S(1)} fusion(f32[24,64,256]{2,1,0:T(8,128)S(1)} %bitcast.144, f32[24,256]{1,0:T(8,128)S(1)} %copy-done.8, f32[24,256]{1,0:T(8,128)S(1)} %copy-done.16, f32[256,256]{1,0:T(8,128)S(1)} %fusion.105, pred[256,256]{1,0:T(8,128)(4,1)S(1)} %copy-done.11), kind=kOutput, calls=%fused_computation.6 | convolution fusion | flops 610271232 | bytes 3522560 | tf_op jit(solution)/shard_map/dot_general | solution.py:80
  96.4 7.4 %collective-permute-done.3 = bf16[25,64,128]{2,1,0:T(8,128)(2,1)S(1)} collective-permute-done((bf16[25,64,128]{2,1,0:T(8,128)(2,1)S(1)}, bf16[25,64,128]{2,1,0:T(8,128)(2,1)S(1)}, u32[]{:S(2)}, u32[]{:S(2)}) %collective-permute-start.3) | collective-permute-done | bytes 409632 | tf_op jit(solution)/shard_map/ppermute | solution.py:99
  105.8 3.9 %fusion = f32[24,64,256]{2,1,0:T(8,128)S(1)} fusion(f32[24,64,256]{2,1,0:T(8,128)S(1)} %bitcast.146, f32[24,256]{1,0:T(8,128)S(1)} %copy-done.6, f32[24,256]{1,0:T(8,128)S(1)} %copy-done.14, f32[256,256]{1,0:T(8,128)S(1)} %fusion.108, pred[256,256]{1,0:T(8,128)(4,1)S(1)} %copy-done.10), kind=kOutput, calls=%fused_computation | convolution fusion | flops 610271232 | bytes 3522560 | tf_op jit(solution)/shard_map/dot_general | solution.py:80
  109.7 9.3 %collective-permute-done.4 = bf16[25,64,128]{2,1,0:T(8,128)(2,1)S(1)} collective-permute-done((bf16[25,64,128]{2,1,0:T(8,128)(2,1)S(1)}, bf16[25,64,128]{2,1,0:T(8,128)(2,1)S(1)}, u32[]{:S(2)}, u32[]{:S(2)}) %collective-permute-start.4) | collective-permute-done | bytes 409632 | tf_op jit(solution)/shard_map/ppermute | solution.py:99
  122.5 3.7 %collective-permute-start.7 = (bf16[12,64,128]{2,1,0:T(8,128)(2,1)S(1)}, bf16[12,64,128]{2,1,0:T(8,128)(2,1)S(1)}, u32[]{:S(2)}, u32[]{:S(2)}) collective-permute-start(bf16[12,64,128]{2,1,0:T(8,128)(2,1)S(1)} %collective-permute-done.6), channel_id=1, source_target_pairs={{0,9},{2,11},{4,13},{6,15},{9,0},{11,2},{13,4},{15,6},{16,25},{18,... | collective-permute-start | bytes 589832 | tf_op jit(solution)/shard_map/ppermute | solution.py:131
  126.2 8.2 %collective-permute-done.5 = bf16[13,64,128]{2,1,0:T(8,128)(2,1)S(1)} collective-permute-done((bf16[13,64,128]{2,1,0:T(8,128)(2,1)S(1)}, bf16[13,64,128]{2,1,0:T(8,128)(2,1)S(1)}, u32[]{:S(2)}, u32[]{:S(2)}) %collective-permute-start.5) | collective-permute-done | bytes 213024 | tf_op jit(solution)/shard_map/ppermute | solution.py:99
  136.1 1.8 %fusion.79 = f32[24,64,256]{2,1,0:T(8,128)S(1)} fusion(f32[24]{0:T(128)S(1)} %get-tuple-element.39, f32[24]{0:T(128)S(1)} %mul.372, f32[24]{0:T(128)S(1)} %bitcast.153, bf16[25,64,128]{2,1,0:T(8,128)(2,1)S(1)} %collective-permute-done.2, bf16[25,64,128]{2,1,0:T(8,128)(2,1)S(1)} %collective-permute-done.4, ...), kind=kOutput, calls=%fused_computation.87 | convolution fusion | flops 304185344 | bytes 3409409 | tf_op jit(solution)/shard_map/dot_general | solution.py:206
  137.9 1.6 %multiply_add_fusion = f32[24,64,256]{2,1,0:T(8,128)S(1)} fusion(f32[24,64,256]{2,1,0:T(8,128)S(1)} %fusion.79, f32[24,64,256]{2,1,0:T(8,128)S(1)} %fusion.6, f32[24,64,256]{2,1,0:T(8,128)S(1)} %fusion, bf16[24,64,128]{2,1,0:T(8,128)(2,1)S(1)} %collective-permute-done.8, f32[24,256]{1,0:T(8,128)S(1)} %get-tuple-element.49, ...), kind=kOutput, calls=%fused_computation.69 | convolution fusion | flops 303988736 | bytes 6995969 | tf_op jit(solution)/shard_map/dot_general | solution.py:206
  140.0 1.9 %multiply_reduce_fusion = (f32[256]{0:T(256)S(1)}, f32[1536,256]{0,1:T(8,128)S(1)}) fusion(f32[1536,256]{0,1:T(8,128)S(1)} %copy.42, f32[1536,256]{0,1:T(8,128)} %divide_multiply_fusion.2), kind=kLoop, calls=%fused_computation.68 | loop fusion | flops 1179392 | bytes 4719616 | tf_op jit(solution)/shard_map/reduce_sum | solution.py:211
  141.9 4.7 %fusion.33 = bf16[256,1536]{1,0:T(8,128)(2,1)} fusion(f32[256,1536]{1,0:T(8,128)S(1)} %copy-done.4, bf16[1536,1536]{1,0:T(8,128)(2,1)} %param.27, f32[1536,256]{0,1:T(8,128)S(1)} %get-tuple-element.34, f32[1536]{0:T(1024)S(1)} %copy-done.34, f32[256]{0:T(256)S(1)} %add_rsqrt_fusion), kind=kOutput, calls=%fused_computation.37 | convolution fusion | flops 1209925632 | bytes 8657920 | tf_op jit(solution)/shard_map/dot_general | solution.py:213
  (146 shorter events, 25.5 us)
Async XLA Ops:
  0.0 53.2 %copy-start = (bf16[1536,24]{0,1:T(8,128)(2,1)S(1)}, bf16[1536,24]{0,1:T(8,128)(2,1)}, u32[]{:S(2)}) copy-start(bf16[1536,24]{0,1:T(8,128)(2,1)} %param.21) | copy-start | bytes 221188
  6.8 8.9 %copy-start.27 = (f32[2,1792]{1,0:T(2,128)S(1)}, f32[2,1792]{1,0:T(2,128)}, u32[]{:S(2)}) copy-start(f32[2,1792]{1,0:T(2,128)} %param.23) | copy-start | bytes 43012
  6.8 9.6 %copy-start.12 = (f32[2,4,1792]{2,1,0:T(4,128)S(1)}, f32[2,4,1792]{2,1,0:T(4,128)}, u32[]{:S(2)}) copy-start(f32[2,4,1792]{2,1,0:T(4,128)} %param.22) | copy-start | bytes 172036
  6.8 10.3 %copy-start.31 = (f32[2,24]{1,0:T(2,128)S(1)}, f32[2,24]{1,0:T(2,128)}, u32[]{:S(2)}) copy-start(f32[2,24]{1,0:T(2,128)} %param.24) | copy-start | bytes 580
  6.8 10.3 %copy-start.32 = (f32[2,24]{1,0:T(2,128)S(1)}, f32[2,24]{1,0:T(2,128)}, u32[]{:S(2)}) copy-start(f32[2,24]{1,0:T(2,128)} %param.25) | copy-start | bytes 580
  6.8 41.9 %copy-start.33 = (f32[1536]{0:T(1024)S(1)}, f32[1536]{0:T(1024)}, u32[]{:S(2)}) copy-start(f32[1536]{0:T(1024)} %param.18) | copy-start | bytes 18436
  6.8 41.7 %all-to-all-start = ((bf16[16,32,1664]{2,1,0:T(8,128)(2,1)}), bf16[16,32,1664]{2,1,0:T(8,128)(2,1)S(1)}, u32[]{:S(2)}, u32[]{:S(2)}) async-start(bf16[16,32,1664]{2,1,0:T(8,128)(2,1)} %bitcast.3), calls=%async_computation | async-start | bytes 3407872 | tf_op jit(solution)/shard_map/all_to_all | solution.py:37
  48.7 4.3 %copy-start.28 = (f32[1536]{0:T(1024)S(1)}, f32[1536]{0:T(1024)}, u32[]{:S(2)}) copy-start(f32[1536]{0:T(1024)} %param.19) | copy-start | bytes 18436
  52.9 2.6 %copy-start.3 = (f32[256,1536]{1,0:T(8,128)}, f32[256,1536]{1,0:T(8,128)S(1)}, u32[]{:S(2)}) copy-start(f32[256,1536]{1,0:T(8,128)S(1)} %get-tuple-element.67) | copy-start | bytes 4718596
  56.1 16.9 %slice-start = ((s8[10223616]{0:T(1024)(128)(4,1)}), s8[4194304]{0:T(1024)(128)(4,1)S(1)}, s32[]{:S(2)}) async-start(s8[10223616]{0:T(1024)(128)(4,1)} %bitcast.148), calls=%async_computation.1 | async-start | bytes 8388608
  56.1 16.9 %slice-start.1 = ((s8[10223616]{0:T(1024)(128)(4,1)}), s8[4194304]{0:T(1024)(128)(4,1)S(1)}, s32[]{:S(2)}) async-start(s8[10223616]{0:T(1024)(128)(4,1)} %bitcast.148), calls=%async_computation.2 | async-start | bytes 8388608
  60.4 12.6 %slice-start.2 = ((s8[10223616]{0:T(1024)(128)(4,1)}), s8[1835008]{0:T(1024)(128)(4,1)S(1)}, s32[]{:S(2)}) async-start(s8[10223616]{0:T(1024)(128)(4,1)} %bitcast.148), calls=%async_computation.3 | async-start | bytes 3670016
  65.5 5.0 %collective-permute-start = (bf16[3,1536]{1,0:T(4,128)(2,1)S(1)}, bf16[3,1536]{1,0:T(4,128)(2,1)S(1)}, u32[]{:S(2)}, u32[]{:S(2)}) collective-permute-start(bf16[3,1536]{1,0:T(4,128)(2,1)S(1)} %get-tuple-element.44), channel_id=1, source_target_pairs={{0,1},{1,2},{2,3},{3,4},{4,5},{5,6},{6,7},{7,8},{8,9},{9,10},{10,1... | collective-permute-start | bytes 27656 | tf_op jit(solution)/shard_map/ppermute | solution.py:50
  68.4 4.6 %collective-permute-start.1 = (bf16[3,1536]{1,0:T(4,128)(2,1)S(1)}, bf16[3,1536]{1,0:T(4,128)(2,1)S(1)}, u32[]{:S(2)}, u32[]{:S(2)}) collective-permute-start(bf16[3,1536]{1,0:T(4,128)(2,1)S(1)} %get-tuple-element.45), channel_id=1, source_target_pairs={{1,0},{2,1},{3,2},{4,3},{5,4},{6,5},{7,6},{8,7},{9,8},{10,9},{11,1... | collective-permute-start | bytes 27656 | tf_op jit(solution)/shard_map/ppermute | solution.py:51
  86.7 4.2 %copy-start.30 = (f32[24]{0:T(128)S(1)}, f32[24]{0:T(128)}, u32[]{:S(2)}) copy-start(f32[24]{0:T(128)} %get-tuple-element.28) | copy-start | bytes 292
  86.7 4.2 %copy-start.29 = (f32[24]{0:T(128)S(1)}, f32[24]{0:T(128)}, u32[]{:S(2)}) copy-start(f32[24]{0:T(128)} %broadcast_select_fusion.1) | copy-start | bytes 292
  86.8 4.1 %collective-permute-start.2 = (bf16[25,64,128]{2,1,0:T(8,128)(2,1)S(1)}, bf16[25,64,128]{2,1,0:T(8,128)(2,1)S(1)}, u32[]{:S(2)}, u32[]{:S(2)}) collective-permute-start(bf16[25,64,128]{2,1,0:T(8,128)(2,1)S(1)} %pad_maximum_fusion), channel_id=1, source_target_pairs={{0,1},{1,0},{2,3},{3,2},{4,5},{5,4},{6,7},{7,6},{8,9},{9,8},{10,11... | collective-permute-start | bytes 1228808 | tf_op jit(solution)/shard_map/ppermute | solution.py:99
  91.2 12.6 %collective-permute-start.3 = (bf16[25,64,128]{2,1,0:T(8,128)(2,1)S(1)}, bf16[25,64,128]{2,1,0:T(8,128)(2,1)S(1)}, u32[]{:S(2)}, u32[]{:S(2)}) collective-permute-start(bf16[25,64,128]{2,1,0:T(8,128)(2,1)S(1)} %pad_maximum_fusion.1), channel_id=1, source_target_pairs={{1,3},{3,5},{5,7},{7,9},{9,11},{11,13},{13,15},{2,0},{4,2},{6,4},{... | collective-permute-start | bytes 1228808 | tf_op jit(solution)/shard_map/ppermute | solution.py:99
  103.8 2.0 %copy-start.10 = (pred[256,256]{1,0:T(8,128)(4,1)S(1)}, pred[256,256]{1,0:T(8,128)(4,1)}, u32[]{:S(2)}) copy-start(pred[256,256]{1,0:T(8,128)(4,1)} %iota_compare_fusion.7) | copy-start | bytes 196612
  104.2 14.7 %collective-permute-start.4 = (bf16[25,64,128]{2,1,0:T(8,128)(2,1)S(1)}, bf16[25,64,128]{2,1,0:T(8,128)(2,1)S(1)}, u32[]{:S(2)}, u32[]{:S(2)}) collective-permute-start(bf16[25,64,128]{2,1,0:T(8,128)(2,1)S(1)} %pad_maximum_fusion.2), channel_id=1, source_target_pairs={{1,5},{3,7},{5,9},{7,11},{9,13},{11,15},{4,0},{6,2},{8,4},{10,6},{... | collective-permute-start | bytes 1228808 | tf_op jit(solution)/shard_map/ppermute | solution.py:99
  119.2 3.3 %collective-permute-start.6 = (bf16[12,64,128]{2,1,0:T(8,128)(2,1)S(1)}, bf16[12,64,128]{2,1,0:T(8,128)(2,1)S(1)}, u32[]{:S(2)}, u32[]{:S(2)}) collective-permute-start(bf16[12,64,128]{2,1,0:T(8,128)(2,1)S(1)} %get-tuple-element.47), channel_id=1, source_target_pairs={{1,0},{3,2},{5,4},{7,6},{8,9},{10,11},{12,13},{14,15},{17,16},{19,... | collective-permute-start | bytes 589832 | tf_op jit(solution)/shard_map/ppermute | solution.py:127
  120.5 13.9 %collective-permute-start.5 = (bf16[13,64,128]{2,1,0:T(8,128)(2,1)S(1)}, bf16[13,64,128]{2,1,0:T(8,128)(2,1)S(1)}, u32[]{:S(2)}, u32[]{:S(2)}) collective-permute-start(bf16[13,64,128]{2,1,0:T(8,128)(2,1)S(1)} %pad_maximum_fusion.5), channel_id=1, source_target_pairs={{1,9},{3,11},{5,13},{7,15},{8,0},{10,2},{12,4},{14,6},{17,25},{19,... | collective-permute-start | bytes 638984 | tf_op jit(solution)/shard_map/ppermute | solution.py:99
  122.5 13.1 %collective-permute-start.7 = (bf16[12,64,128]{2,1,0:T(8,128)(2,1)S(1)}, bf16[12,64,128]{2,1,0:T(8,128)(2,1)S(1)}, u32[]{:S(2)}, u32[]{:S(2)}) collective-permute-start(bf16[12,64,128]{2,1,0:T(8,128)(2,1)S(1)} %collective-permute-done.6), channel_id=1, source_target_pairs={{0,9},{2,11},{4,13},{6,15},{9,0},{11,2},{13,4},{15,6},{16,25},{18,... | collective-permute-start | bytes 589832 | tf_op jit(solution)/shard_map/ppermute | solution.py:131
  136.0 1.9 %collective-permute-start.8 = (bf16[24,64,128]{2,1,0:T(8,128)(2,1)S(1)}, bf16[24,64,128]{2,1,0:T(8,128)(2,1)S(1)}, u32[]{:S(2)}, u32[]{:S(2)}) collective-permute-start(bf16[24,64,128]{2,1,0:T(8,128)(2,1)S(1)} %fusion.89), channel_id=1, source_target_pairs={{0,1},{1,0},{2,3},{3,2},{4,5},{5,4},{6,7},{7,6},{8,9},{9,8},{10,11... | collective-permute-start | bytes 1179656 | tf_op jit(solution)/shard_map/ppermute | solution.py:140
  (24 other events, 32.8 us)

commit v11 on v9

--- a/solution.py
+++ b/solution.py
@@ -24,8 +24,11 @@
     capacity = slots // devices
     is_live = jnp.arange(slots, dtype=jnp.int32) < tile_count[0]
     owners = jnp.where(is_live, tile_pos // rows, devices)
-    one_hot = (owners[:, None] == jnp.arange(devices, dtype=jnp.int32)[None, :]).astype(jnp.int32)
-    ranking = jnp.sum(jnp.cumsum(one_hot, axis=0) * one_hot, axis=1) - 1
+    one_hot = (owners[:, None] == jnp.arange(devices, dtype=jnp.int32)[None, :]).astype(jnp.bfloat16)
+    slot_ids = jnp.arange(slots, dtype=jnp.int32)
+    before = (slot_ids[None, :] <= slot_ids[:, None]).astype(jnp.bfloat16)
+    counts = jnp.dot(before, one_hot, preferred_element_type=jnp.float32)
+    ranking = jnp.sum(counts * one_hot.astype(jnp.float32), axis=1).astype(jnp.int32) - 1
     target = jnp.where(is_live, owners * capacity + ranking, -1)
     match = target[None, :] == jnp.arange(devices * capacity, dtype=jnp.int32)[:, None]
     row_column = (tile_pos % rows + 1).astype(jnp.bfloat16)[:, None]

time: 146 us -> 145 us (level)
  no operation moved by 1% of the time
where the time goes in v11:
time: 145 us; the launch traced here: 144 us
  waiting for transfers between devices  64.3 us (44%)
  matrix products  39.9 us (28%)
  starting transfers between devices  18.6 us (13%)
  other arithmetic  10.6 us (7%)
  local copies, waits for them, and re-layouts  9.09 us (6%)
  between operations  1.48 us (1%)
    all_to_all x1, waiting for transfers between devices, route_tiles(): lax.all_to_all(send, 'seq', 0, 0, tiled=True)  31.4 us
    ppermute x4, waiting for transfers between devices, transfer(): got = lax.ppermute(payload, 'seq', pairs)  30.5 us
    dot_general x2, matrix products, local_terms(): lax.dot_general(signal, mixing, (((2,), (2,)), ((0,), (0,))), precision=f...  7.78 us
    all_to_all x1, starting transfers between devices, route_tiles(): lax.all_to_all(send, 'seq', 0, 0, tiled=True)  7.56 us
    ppermute x4, starting transfers between devices, transfer(): got = lax.ppermute(payload, 'seq', pairs)  6.59 us
    dot_general x1, matrix products, per_device(): lax.dot_general(in_weight[:, :E], normed, turned, preferred_element_type=...  5.12 us
    slice x4, local copies, waits for them, and re-layouts, local_terms(): signal = activated[:E].reshape(HEADS, HEAD_DIM, rows)  5.1 us
    dot_general x1, matrix products, per_device(): lax.dot_general(mixed, out_weight, (((0,), (0,)), ((), ())), preferred_el...  4.66 us
  transfers between devices with their start and end apart: 8, of which 5 were waited for; matrix products, arithmetic and copies ran while one was open for 10% of the time, Pallas kernels for 0%

profile of v11, /device:TPU:0, one launch (start us, length us, event | category | flops | bytes accessed | tf_op | source)
XLA Modules:
  0.0 143.9 jit_solution(4154773336145964560)
XLA Ops:
  1.8 3.7 %convolution_convert_fusion = bf16[512,1664]{1,0:T(8,128)(2,1)} fusion(bf16[512,1]{1,0:T(8,128)(2,1)S(1)} %broadcast_in_dim.47, bf16[512,1536]{1,0:T(8,128)(2,1)} %param.14, s32[512]{0:T(512)S(1)} %add_select_fusion.2), kind=kOutput, calls=%fused_computation.32 | convolution fusion | flops 878641152 | bytes 3279872 | tf_op jit(solution)/shard_map/dot_general | solution.py:38
  5.6 7.6 %all-to-all-start = ((bf16[16,32,1664]{2,1,0:T(8,128)(2,1)}), bf16[16,32,1664]{2,1,0:T(8,128)(2,1)S(1)}, u32[]{:S(2)}, u32[]{:S(2)}) async-start(bf16[16,32,1664]{2,1,0:T(8,128)(2,1)} %bitcast.1), calls=%async_computation | async-start | bytes 3407872 | tf_op jit(solution)/shard_map/all_to_all | solution.py:40
  15.9 31.4 %all-to-all-done = bf16[16,32,1664]{2,1,0:T(8,128)(2,1)S(1)} async-done(((bf16[16,32,1664]{2,1,0:T(8,128)(2,1)}), bf16[16,32,1664]{2,1,0:T(8,128)(2,1)S(1)}, u32[]{:S(2)}, u32[]{:S(2)}) %all-to-all-start) | async-done | bytes 1703968 | tf_op jit(solution)/shard_map/all_to_all | solution.py:40
  47.4 4.2 %multiply_reduce_fusion.1 = (f32[256]{0:T(256)S(1)}, f32[256,1536]{1,0:T(8,128)S(1)}) fusion(f32[1536]{0:T(1024)S(1)} %copy-done.33, bf16[1536,1536]{1,0:T(8,128)(2,1)} %param.17, bf16[512,1664]{1,0:T(8,128)(2,1)S(1)} %bitcast.135, s32[512]{0:T(512)S(1)} %add_reduce_fusion), kind=kOutput, calls=%fused_computation.76 | convolution fusion | flops 1613102848 | bytes 7875584 | tf_op jit(solution)/shard_map/dot_general | solution.py:157
  54.7 4.3 %fusion.46 = bf16[1792,256]{0,1:T(8,128)(2,1)S(1)} fusion(bf16[256,1536]{1,0:T(8,128)(2,1)S(1)} %multiply_convert_fusion.1, bf16[1536,3328]{1,0:T(8,128)(2,1)} %param.20), kind=kOutput, calls=%fused_computation.43 | convolution fusion | flops 1409744896 | bytes 7208960 | tf_op jit(solution)/shard_map/dot_general | solution.py:161
  59.1 5.1 %divide_multiply_fusion.2 = f32[1536,256]{0,1:T(8,128)} fusion(bf16[256,1536]{1,0:T(8,128)(2,1)S(1)} %multiply_convert_fusion.1, bf16[1536,3328]{1,0:T(8,128)(2,1)} %param.20), kind=kOutput, calls=%fused_computation.70 | convolution fusion | flops 1210318848 | bytes 7077888 | tf_op jit(solution)/shard_map/dot_general | solution.py:165
  64.2 2.9 %collective-permute-start = (bf16[3,1536]{1,0:T(4,128)(2,1)S(1)}, bf16[3,1536]{1,0:T(4,128)(2,1)S(1)}, u32[]{:S(2)}, u32[]{:S(2)}) collective-permute-start(bf16[3,1536]{1,0:T(4,128)(2,1)S(1)} %get-tuple-element.44), channel_id=1, source_target_pairs={{0,1},{1,2},{2,3},{3,4},{4,5},{5,6},{6,7},{7,8},{8,9},{9,10},{10,1... | collective-permute-start | bytes 27656 | tf_op jit(solution)/shard_map/ppermute | solution.py:53
  69.1 2.5 %collective-permute-done.1 = bf16[3,1536]{1,0:T(4,128)(2,1)S(1)} collective-permute-done((bf16[3,1536]{1,0:T(4,128)(2,1)S(1)}, bf16[3,1536]{1,0:T(4,128)(2,1)S(1)}, u32[]{:S(2)}, u32[]{:S(2)}) %collective-permute-start.1) | collective-permute-done | bytes 9248 | tf_op jit(solution)/shard_map/ppermute | solution.py:54
  73.3 2.3 %divide_multiply_fusion = (f32[1792,256]{0,1:T(8,128)S(1)}, f32[1792,256]{0,1:T(8,128)S(1)}) fusion(f32[1792,262]{0,1:T(8,128)S(1)} %maximum_convert_fusion, f32[1792]{0:T(1024)S(1)} %copy-done.25, f32[1792]{0:T(1024)S(1)} %copy-done.26, f32[1792]{0:T(1024)S(1)} %copy-done.20, f32[1792]{0:T(1024)S(1)} %copy-done.19, f32[1792]{0:T(1024)S(1)} %copy-done.17, ...), kind=kLoop, calls=%fused_computation.60 | loop fusion | flops 11010048 | bytes 16586752 | tf_op jit(solution)/shard_map/jit(silu)/mul | solution.py:179
  77.1 1.7 %copy.34 = f32[1536,256]{1,0:T(8,128)} copy(f32[1536,256]{0,1:T(8,128)S(1)} %slice.202) | data formatting | bytes 3145728 | tf_op jit(solution)/shard_map/slice | solution.py:63
  80.1 1.9 %copy.36 = f32[1536,256]{1,0:T(8,128)S(1)} copy(f32[1536,256]{0,1:T(8,128)} %slice.207) | data formatting | bytes 3145728 | tf_op jit(solution)/shard_map/slice | solution.py:63
  82.0 1.6 %fusion.71 = f32[24,64,128]{2,1,0:T(8,128)S(1)} fusion(f32[24,64,256]{2,1,0:T(8,128)S(1)} %bitcast.127, f32[24,256]{1,0:T(8,128)} %get-tuple-element.50, f32[1792,256]{0,1:T(8,128)S(1)} %get-tuple-element.42), kind=kOutput, calls=%fused_computation.71 | convolution fusion | flops 302383104 | bytes 2514944 | tf_op jit(solution)/shard_map/dot_general | solution.py:85
  83.7 1.7 %select_convert_fusion = (bf16[24,64,128]{2,1,0:T(8,128)(2,1)S(1)}, f32[24,64,128]{2,1,0:T(8,128)S(1)}) fusion(f32[24,64,128]{2,1,0:T(8,128)S(1)} %fusion.71, pred[]{:T(512)S(6)} %eq.52, f32[1792,256]{0,1:T(8,128)} %copy-done.1, f32[24,64,256]{2,1,0:T(8,128)S(1)} %bitcast.129, f32[24,256]{1,0:T(8,128)S(1)} %get-tuple-element.51), kind=kOutput, calls=%fused_computation.97 | convolution fusion | flops 302579712 | bytes 3694593 | tf_op jit(solution)/shard_map/dot_general | solution.py:85
  85.5 2.5 %collective-permute-start.2 = (bf16[25,64,128]{2,1,0:T(8,128)(2,1)S(1)}, bf16[25,64,128]{2,1,0:T(8,128)(2,1)S(1)}, u32[]{:S(2)}, u32[]{:S(2)}) collective-permute-start(bf16[25,64,128]{2,1,0:T(8,128)(2,1)S(1)} %pad_maximum_fusion), channel_id=1, source_target_pairs={{0,1},{1,0},{2,3},{3,2},{4,5},{5,4},{6,7},{7,6},{8,9},{9,8},{10,11... | collective-permute-start | bytes 1228808 | tf_op jit(solution)/shard_map/ppermute | solution.py:102
  91.2 3.9 %fusion.6 = f32[24,64,256]{2,1,0:T(8,128)S(1)} fusion(f32[24,64,256]{2,1,0:T(8,128)S(1)} %bitcast.128, f32[24,256]{1,0:T(8,128)S(1)} %copy-done.8, f32[24,256]{1,0:T(8,128)S(1)} %copy-done.16, f32[256,256]{1,0:T(8,128)S(1)} %fusion.107, pred[256,256]{1,0:T(8,128)(4,1)S(1)} %copy-done.11), kind=kOutput, calls=%fused_computation.6 | convolution fusion | flops 610271232 | bytes 3522560 | tf_op jit(solution)/shard_map/dot_general | solution.py:83
  95.1 7.4 %collective-permute-done.3 = bf16[25,64,128]{2,1,0:T(8,128)(2,1)S(1)} collective-permute-done((bf16[25,64,128]{2,1,0:T(8,128)(2,1)S(1)}, bf16[25,64,128]{2,1,0:T(8,128)(2,1)S(1)}, u32[]{:S(2)}, u32[]{:S(2)}) %collective-permute-start.3) | collective-permute-done | bytes 409632 | tf_op jit(solution)/shard_map/ppermute | solution.py:102
  102.9 1.5 %collective-permute-start.4 = (bf16[25,64,128]{2,1,0:T(8,128)(2,1)S(1)}, bf16[25,64,128]{2,1,0:T(8,128)(2,1)S(1)}, u32[]{:S(2)}, u32[]{:S(2)}) collective-permute-start(bf16[25,64,128]{2,1,0:T(8,128)(2,1)S(1)} %pad_maximum_fusion.2), channel_id=1, source_target_pairs={{1,5},{3,7},{5,9},{7,11},{9,13},{11,15},{4,0},{6,2},{8,4},{10,6},{... | collective-permute-start | bytes 1228808 | tf_op jit(solution)/shard_map/ppermute | solution.py:102
  104.5 3.9 %fusion = f32[24,64,256]{2,1,0:T(8,128)S(1)} fusion(f32[24,64,256]{2,1,0:T(8,128)S(1)} %bitcast.130, f32[24,256]{1,0:T(8,128)S(1)} %copy-done.6, f32[24,256]{1,0:T(8,128)S(1)} %copy-done.14, f32[256,256]{1,0:T(8,128)S(1)} %fusion.110, pred[256,256]{1,0:T(8,128)(4,1)S(1)} %copy-done.10), kind=kOutput, calls=%fused_computation | convolution fusion | flops 610271232 | bytes 3522560 | tf_op jit(solution)/shard_map/dot_general | solution.py:83
  108.3 9.3 %collective-permute-done.4 = bf16[25,64,128]{2,1,0:T(8,128)(2,1)S(1)} collective-permute-done((bf16[25,64,128]{2,1,0:T(8,128)(2,1)S(1)}, bf16[25,64,128]{2,1,0:T(8,128)(2,1)S(1)}, u32[]{:S(2)}, u32[]{:S(2)}) %collective-permute-start.4) | collective-permute-done | bytes 409632 | tf_op jit(solution)/shard_map/ppermute | solution.py:102
  119.2 13.8 %collective-permute-done.5 = bf16[25,64,128]{2,1,0:T(8,128)(2,1)S(1)} collective-permute-done((bf16[25,64,128]{2,1,0:T(8,128)(2,1)S(1)}, bf16[25,64,128]{2,1,0:T(8,128)(2,1)S(1)}, u32[]{:S(2)}, u32[]{:S(2)}) %collective-permute-start.5) | collective-permute-done | bytes 409632 | tf_op jit(solution)/shard_map/ppermute | solution.py:102
  133.5 1.8 %fusion.80 = f32[24,64,256]{2,1,0:T(8,128)S(1)} fusion(f32[24]{0:T(128)S(1)} %get-tuple-element.39, f32[24]{0:T(128)S(1)} %mul.372, f32[24]{0:T(128)S(1)} %bitcast.136, bf16[25,64,128]{2,1,0:T(8,128)(2,1)S(1)} %collective-permute-done.5, bf16[25,64,128]{2,1,0:T(8,128)(2,1)S(1)} %collective-permute-done.2, ...), kind=kOutput, calls=%fused_computation.90 | convolution fusion | flops 303988736 | bytes 3409409 | tf_op jit(solution)/shard_map/dot_general | solution.py:198
  135.3 1.6 %multiply_add_fusion = f32[24,64,256]{2,1,0:T(8,128)S(1)} fusion(f32[24,64,256]{2,1,0:T(8,128)S(1)} %fusion.80, f32[24,64,256]{2,1,0:T(8,128)S(1)} %fusion.6, f32[24,64,256]{2,1,0:T(8,128)S(1)} %fusion, bf16[24,64,128]{2,1,0:T(8,128)(2,1)S(1)} %collective-permute-done.6, f32[24,256]{1,0:T(8,128)S(1)} %get-tuple-element.47, ...), kind=kOutput, calls=%fused_computation.69 | convolution fusion | flops 303988736 | bytes 6995969 | tf_op jit(solution)/shard_map/dot_general | solution.py:198
  137.4 1.9 %multiply_reduce_fusion = (f32[256]{0:T(256)S(1)}, f32[1536,256]{0,1:T(8,128)S(1)}) fusion(f32[1536,256]{0,1:T(8,128)S(1)} %copy.40, f32[1536,256]{0,1:T(8,128)} %divide_multiply_fusion.2), kind=kLoop, calls=%fused_computation.68 | loop fusion | flops 1179392 | bytes 4719616 | tf_op jit(solution)/shard_map/reduce_sum | solution.py:203
  139.3 4.7 %fusion.33 = bf16[256,1536]{1,0:T(8,128)(2,1)} fusion(f32[256,1536]{1,0:T(8,128)S(1)} %copy-done.4, bf16[1536,1536]{1,0:T(8,128)(2,1)} %param.27, f32[1536,256]{0,1:T(8,128)S(1)} %get-tuple-element.34, f32[1536]{0:T(1024)S(1)} %copy-done.34, f32[256]{0:T(256)S(1)} %add_rsqrt_fusion), kind=kOutput, calls=%fused_computation.37 | convolution fusion | flops 1209925632 | bytes 8657920 | tf_op jit(solution)/shard_map/dot_general | solution.py:205
  (135 shorter events, 19.4 us)
Async XLA Ops:
  0.0 51.9 %copy-start = (bf16[1536,24]{0,1:T(8,128)(2,1)S(1)}, bf16[1536,24]{0,1:T(8,128)(2,1)}, u32[]{:S(2)}) copy-start(bf16[1536,24]{0,1:T(8,128)(2,1)} %param.21) | copy-start | bytes 221188
  5.6 8.9 %copy-start.27 = (f32[2,1792]{1,0:T(2,128)S(1)}, f32[2,1792]{1,0:T(2,128)}, u32[]{:S(2)}) copy-start(f32[2,1792]{1,0:T(2,128)} %param.23) | copy-start | bytes 43012
  5.6 9.6 %copy-start.12 = (f32[2,4,1792]{2,1,0:T(4,128)S(1)}, f32[2,4,1792]{2,1,0:T(4,128)}, u32[]{:S(2)}) copy-start(f32[2,4,1792]{2,1,0:T(4,128)} %param.22) | copy-start | bytes 172036
  5.6 10.3 %copy-start.31 = (f32[2,24]{1,0:T(2,128)S(1)}, f32[2,24]{1,0:T(2,128)}, u32[]{:S(2)}) copy-start(f32[2,24]{1,0:T(2,128)} %param.24) | copy-start | bytes 580
  5.6 10.3 %copy-start.32 = (f32[2,24]{1,0:T(2,128)S(1)}, f32[2,24]{1,0:T(2,128)}, u32[]{:S(2)}) copy-start(f32[2,24]{1,0:T(2,128)} %param.25) | copy-start | bytes 580
  5.6 41.9 %copy-start.33 = (f32[1536]{0:T(1024)S(1)}, f32[1536]{0:T(1024)}, u32[]{:S(2)}) copy-start(f32[1536]{0:T(1024)} %param.18) | copy-start | bytes 18436
  5.6 41.7 %all-to-all-start = ((bf16[16,32,1664]{2,1,0:T(8,128)(2,1)}), bf16[16,32,1664]{2,1,0:T(8,128)(2,1)S(1)}, u32[]{:S(2)}, u32[]{:S(2)}) async-start(bf16[16,32,1664]{2,1,0:T(8,128)(2,1)} %bitcast.1), calls=%async_computation | async-start | bytes 3407872 | tf_op jit(solution)/shard_map/all_to_all | solution.py:40
  47.4 4.3 %copy-start.28 = (f32[1536]{0:T(1024)S(1)}, f32[1536]{0:T(1024)}, u32[]{:S(2)}) copy-start(f32[1536]{0:T(1024)} %param.19) | copy-start | bytes 18436
  51.7 2.5 %copy-start.3 = (f32[256,1536]{1,0:T(8,128)}, f32[256,1536]{1,0:T(8,128)S(1)}, u32[]{:S(2)}) copy-start(f32[256,1536]{1,0:T(8,128)S(1)} %get-tuple-element.65) | copy-start | bytes 4718596
  54.7 16.9 %slice-start = ((s8[10223616]{0:T(1024)(128)(4,1)}), s8[4194304]{0:T(1024)(128)(4,1)S(1)}, s32[]{:S(2)}) async-start(s8[10223616]{0:T(1024)(128)(4,1)} %bitcast.132), calls=%async_computation.1 | async-start | bytes 8388608
  54.7 16.9 %slice-start.1 = ((s8[10223616]{0:T(1024)(128)(4,1)}), s8[4194304]{0:T(1024)(128)(4,1)S(1)}, s32[]{:S(2)}) async-start(s8[10223616]{0:T(1024)(128)(4,1)} %bitcast.132), calls=%async_computation.2 | async-start | bytes 8388608
  59.0 12.6 %slice-start.2 = ((s8[10223616]{0:T(1024)(128)(4,1)}), s8[1835008]{0:T(1024)(128)(4,1)S(1)}, s32[]{:S(2)}) async-start(s8[10223616]{0:T(1024)(128)(4,1)} %bitcast.132), calls=%async_computation.3 | async-start | bytes 3670016
  64.2 5.0 %collective-permute-start = (bf16[3,1536]{1,0:T(4,128)(2,1)S(1)}, bf16[3,1536]{1,0:T(4,128)(2,1)S(1)}, u32[]{:S(2)}, u32[]{:S(2)}) collective-permute-start(bf16[3,1536]{1,0:T(4,128)(2,1)S(1)} %get-tuple-element.44), channel_id=1, source_target_pairs={{0,1},{1,2},{2,3},{3,4},{4,5},{5,6},{6,7},{7,8},{8,9},{9,10},{10,1... | collective-permute-start | bytes 27656 | tf_op jit(solution)/shard_map/ppermute | solution.py:53
  67.0 4.6 %collective-permute-start.1 = (bf16[3,1536]{1,0:T(4,128)(2,1)S(1)}, bf16[3,1536]{1,0:T(4,128)(2,1)S(1)}, u32[]{:S(2)}, u32[]{:S(2)}) collective-permute-start(bf16[3,1536]{1,0:T(4,128)(2,1)S(1)} %get-tuple-element.45), channel_id=1, source_target_pairs={{1,0},{2,1},{3,2},{4,3},{5,4},{6,5},{7,6},{8,7},{9,8},{10,9},{11,1... | collective-permute-start | bytes 27656 | tf_op jit(solution)/shard_map/ppermute | solution.py:54
  85.4 4.2 %copy-start.30 = (f32[24]{0:T(128)S(1)}, f32[24]{0:T(128)}, u32[]{:S(2)}) copy-start(f32[24]{0:T(128)} %get-tuple-element.28) | copy-start | bytes 292
  85.4 4.2 %copy-start.29 = (f32[24]{0:T(128)S(1)}, f32[24]{0:T(128)}, u32[]{:S(2)}) copy-start(f32[24]{0:T(128)} %broadcast_select_fusion.1) | copy-start | bytes 292
  85.5 4.1 %collective-permute-start.2 = (bf16[25,64,128]{2,1,0:T(8,128)(2,1)S(1)}, bf16[25,64,128]{2,1,0:T(8,128)(2,1)S(1)}, u32[]{:S(2)}, u32[]{:S(2)}) collective-permute-start(bf16[25,64,128]{2,1,0:T(8,128)(2,1)S(1)} %pad_maximum_fusion), channel_id=1, source_target_pairs={{0,1},{1,0},{2,3},{3,2},{4,5},{5,4},{6,7},{7,6},{8,9},{9,8},{10,11... | collective-permute-start | bytes 1228808 | tf_op jit(solution)/shard_map/ppermute | solution.py:102
  89.9 12.6 %collective-permute-start.3 = (bf16[25,64,128]{2,1,0:T(8,128)(2,1)S(1)}, bf16[25,64,128]{2,1,0:T(8,128)(2,1)S(1)}, u32[]{:S(2)}, u32[]{:S(2)}) collective-permute-start(bf16[25,64,128]{2,1,0:T(8,128)(2,1)S(1)} %pad_maximum_fusion.1), channel_id=1, source_target_pairs={{1,3},{3,5},{5,7},{7,9},{9,11},{11,13},{13,15},{2,0},{4,2},{6,4},{... | collective-permute-start | bytes 1228808 | tf_op jit(solution)/shard_map/ppermute | solution.py:102
  102.4 2.0 %copy-start.6 = (f32[24,256]{1,0:T(8,128)S(1)}, f32[24,256]{1,0:T(8,128)}, u32[]{:S(2)}) copy-start(f32[24,256]{1,0:T(8,128)} %copy-done.5) | copy-start | bytes 73732
  102.5 2.0 %copy-start.10 = (pred[256,256]{1,0:T(8,128)(4,1)S(1)}, pred[256,256]{1,0:T(8,128)(4,1)}, u32[]{:S(2)}) copy-start(pred[256,256]{1,0:T(8,128)(4,1)} %iota_compare_fusion.9) | copy-start | bytes 196612
  102.5 2.0 %copy-start.14 = (f32[24,256]{1,0:T(8,128)S(1)}, f32[24,256]{1,0:T(8,128)}, u32[]{:S(2)}) copy-start(f32[24,256]{1,0:T(8,128)} %copy-done.13) | copy-start | bytes 73732
  102.9 14.7 %collective-permute-start.4 = (bf16[25,64,128]{2,1,0:T(8,128)(2,1)S(1)}, bf16[25,64,128]{2,1,0:T(8,128)(2,1)S(1)}, u32[]{:S(2)}, u32[]{:S(2)}) collective-permute-start(bf16[25,64,128]{2,1,0:T(8,128)(2,1)S(1)} %pad_maximum_fusion.2), channel_id=1, source_target_pairs={{1,5},{3,7},{5,9},{7,11},{9,13},{11,15},{4,0},{6,2},{8,4},{10,6},{... | collective-permute-start | bytes 1228808 | tf_op jit(solution)/shard_map/ppermute | solution.py:102
  117.9 15.1 %collective-permute-start.5 = (bf16[25,64,128]{2,1,0:T(8,128)(2,1)S(1)}, bf16[25,64,128]{2,1,0:T(8,128)(2,1)S(1)}, u32[]{:S(2)}, u32[]{:S(2)}) collective-permute-start(bf16[25,64,128]{2,1,0:T(8,128)(2,1)S(1)} %pad_maximum_fusion.3), channel_id=1, source_target_pairs={{1,9},{3,11},{5,13},{7,15},{8,0},{10,2},{12,4},{14,6},{17,25},{19,... | collective-permute-start | bytes 1228808 | tf_op jit(solution)/shard_map/ppermute | solution.py:102
  133.4 1.9 %collective-permute-start.6 = (bf16[24,64,128]{2,1,0:T(8,128)(2,1)S(1)}, bf16[24,64,128]{2,1,0:T(8,128)(2,1)S(1)}, u32[]{:S(2)}, u32[]{:S(2)}) collective-permute-start(bf16[24,64,128]{2,1,0:T(8,128)(2,1)S(1)} %fusion.90), channel_id=1, source_target_pairs={{0,1},{1,0},{2,3},{3,2},{4,5},{5,4},{6,7},{7,6},{8,9},{9,8},{10,11... | collective-permute-start | bytes 1179656 | tf_op jit(solution)/shard_map/ppermute | solution.py:132
  (22 other events, 28.7 us)

commit v12 on v11

--- a/solution.py
+++ b/solution.py
@@ -35,7 +35,8 @@
     source = jnp.concatenate(
         [tile_embeds, jnp.pad(row_column, ((0, 0), (0, 127)))], axis=1
     )
-    send = jnp.dot(match.astype(jnp.bfloat16), source, preferred_element_type=jnp.float32)
+    picker, source = lax.optimization_barrier((match.astype(jnp.bfloat16), source))
+    send = jnp.dot(picker, source, preferred_element_type=jnp.float32)
     send = send.astype(jnp.bfloat16).reshape(devices, capacity, width + 128)
     arrived = lax.all_to_all(send, "seq", 0, 0, tiled=True).reshape(devices * capacity, width + 128)
     arrived_rows = arrived[:, width].astype(jnp.float32).astype(jnp.int32) - 1

time: 145 us -> 145 us (level)
  other arithmetic: 10.6 us -> 12.2 us
    concatenate x0 -> x1, other arithmetic: none -> 1.53 us  [route_tiles(): jnp.concatenate([tile_embeds, jnp.pad(row_column, ((0, 0), (0, 127)))], a...]
where the time goes in v12:
time: 145 us; the launch traced here: 144 us
  waiting for transfers between devices  64.3 us (44%)
  matrix products  38.5 us (27%)
  starting transfers between devices  18.6 us (13%)
  other arithmetic  12.2 us (8%)
  local copies, waits for them, and re-layouts  9.09 us (6%)
  between operations  1.48 us (1%)
    all_to_all x1, waiting for transfers between devices, route_tiles(): lax.all_to_all(send, 'seq', 0, 0, tiled=True)  31.4 us
    ppermute x4, waiting for transfers between devices, transfer(): got = lax.ppermute(payload, 'seq', pairs)  30.4 us
    dot_general x2, matrix products, local_terms(): lax.dot_general(signal, mixing, (((2,), (2,)), ((0,), (0,))), precision=f...  7.78 us
    all_to_all x1, starting transfers between devices, route_tiles(): lax.all_to_all(send, 'seq', 0, 0, tiled=True)  7.56 us
    ppermute x4, starting transfers between devices, transfer(): got = lax.ppermute(payload, 'seq', pairs)  6.6 us
    dot_general x1, matrix products, per_device(): lax.dot_general(in_weight[:, :E], normed, turned, preferred_element_type=...  5.12 us
    slice x4, local copies, waits for them, and re-layouts, local_terms(): signal = activated[:E].reshape(HEADS, HEAD_DIM, rows)  5.1 us
    dot_general x1, matrix products, per_device(): lax.dot_general(mixed, out_weight, (((0,), (0,)), ((), ())), preferred_el...  4.66 us
  transfers between devices with their start and end apart: 8, of which 5 were waited for; matrix products, arithmetic and copies ran while one was open for 10% of the time, Pallas kernels for 0%

profile of v12, /device:TPU:0, one launch (start us, length us, event | category | flops | bytes accessed | tf_op | source)
XLA Modules:
  0.0 144.2 jit_solution(16363618624387885410)
XLA Ops:
  1.9 1.5 %fusion.63 = bf16[512,1664]{1,0:T(8,128)(2,1)S(1)} fusion(bf16[512,1]{1,0:T(8,128)(2,1)S(1)} %broadcast_in_dim.47, bf16[512,1536]{1,0:T(8,128)(2,1)} %param.14), kind=kLoop, calls=%fused_computation.62 | loop fusion | flops 5111808 | bytes 3277824 | tf_op jit(solution)/shard_map/concatenate | solution.py:35
  3.5 2.3 %convolution_convert_fusion = bf16[512,1664]{1,0:T(8,128)(2,1)} fusion(bf16[512,512]{1,0:T(8,128)(2,1)S(1)} %fusion.72, bf16[512,1664]{1,0:T(8,128)(2,1)S(1)} %fusion.63), kind=kOutput, calls=%fused_computation.32 | convolution fusion | flops 873267200 | bytes 3932160 | tf_op jit(solution)/shard_map/dot_general | solution.py:39
  5.8 7.6 %all-to-all-start = ((bf16[16,32,1664]{2,1,0:T(8,128)(2,1)}), bf16[16,32,1664]{2,1,0:T(8,128)(2,1)S(1)}, u32[]{:S(2)}, u32[]{:S(2)}) async-start(bf16[16,32,1664]{2,1,0:T(8,128)(2,1)} %bitcast.1), calls=%async_computation | async-start | bytes 3407872 | tf_op jit(solution)/shard_map/all_to_all | solution.py:41
  16.1 31.4 %all-to-all-done = bf16[16,32,1664]{2,1,0:T(8,128)(2,1)S(1)} async-done(((bf16[16,32,1664]{2,1,0:T(8,128)(2,1)}), bf16[16,32,1664]{2,1,0:T(8,128)(2,1)S(1)}, u32[]{:S(2)}, u32[]{:S(2)}) %all-to-all-start) | async-done | bytes 1703968 | tf_op jit(solution)/shard_map/all_to_all | solution.py:41
  47.7 4.2 %multiply_reduce_fusion.1 = (f32[256]{0:T(256)S(1)}, f32[256,1536]{1,0:T(8,128)S(1)}) fusion(f32[1536]{0:T(1024)S(1)} %copy-done.33, bf16[1536,1536]{1,0:T(8,128)(2,1)} %param.17, bf16[512,1664]{1,0:T(8,128)(2,1)S(1)} %bitcast.137, s32[512]{0:T(512)S(1)} %add_reduce_fusion), kind=kOutput, calls=%fused_computation.73 | convolution fusion | flops 1613102848 | bytes 7875584 | tf_op jit(solution)/shard_map/dot_general | solution.py:158
  55.0 4.3 %fusion.46 = bf16[1792,256]{0,1:T(8,128)(2,1)S(1)} fusion(bf16[256,1536]{1,0:T(8,128)(2,1)S(1)} %multiply_convert_fusion.1, bf16[1536,3328]{1,0:T(8,128)(2,1)} %param.20), kind=kOutput, calls=%fused_computation.43 | convolution fusion | flops 1409744896 | bytes 7208960 | tf_op jit(solution)/shard_map/dot_general | solution.py:162
  59.3 5.1 %divide_multiply_fusion.2 = f32[1536,256]{0,1:T(8,128)} fusion(bf16[256,1536]{1,0:T(8,128)(2,1)S(1)} %multiply_convert_fusion.1, bf16[1536,3328]{1,0:T(8,128)(2,1)} %param.20), kind=kOutput, calls=%fused_computation.67 | convolution fusion | flops 1210318848 | bytes 7077888 | tf_op jit(solution)/shard_map/dot_general | solution.py:166
  64.4 2.9 %collective-permute-start = (bf16[3,1536]{1,0:T(4,128)(2,1)S(1)}, bf16[3,1536]{1,0:T(4,128)(2,1)S(1)}, u32[]{:S(2)}, u32[]{:S(2)}) collective-permute-start(bf16[3,1536]{1,0:T(4,128)(2,1)S(1)} %get-tuple-element.48), channel_id=1, source_target_pairs={{0,1},{1,2},{2,3},{3,4},{4,5},{5,6},{6,7},{7,8},{8,9},{9,10},{10,1... | collective-permute-start | bytes 27656 | tf_op jit(solution)/shard_map/ppermute | solution.py:54
  69.4 2.5 %collective-permute-done.1 = bf16[3,1536]{1,0:T(4,128)(2,1)S(1)} collective-permute-done((bf16[3,1536]{1,0:T(4,128)(2,1)S(1)}, bf16[3,1536]{1,0:T(4,128)(2,1)S(1)}, u32[]{:S(2)}, u32[]{:S(2)}) %collective-permute-start.1) | collective-permute-done | bytes 9248 | tf_op jit(solution)/shard_map/ppermute | solution.py:55
  73.6 2.3 %divide_multiply_fusion = (f32[1792,256]{0,1:T(8,128)S(1)}, f32[1792,256]{0,1:T(8,128)S(1)}) fusion(f32[1792,262]{0,1:T(8,128)S(1)} %maximum_convert_fusion, f32[1792]{0:T(1024)S(1)} %copy-done.25, f32[1792]{0:T(1024)S(1)} %copy-done.26, f32[1792]{0:T(1024)S(1)} %copy-done.20, f32[1792]{0:T(1024)S(1)} %copy-done.19, f32[1792]{0:T(1024)S(1)} %copy-done.17, ...), kind=kLoop, calls=%fused_computation.60 | loop fusion | flops 11010048 | bytes 16586752 | tf_op jit(solution)/shard_map/jit(silu)/mul | solution.py:180
  77.3 1.7 %copy.34 = f32[1536,256]{1,0:T(8,128)} copy(f32[1536,256]{0,1:T(8,128)S(1)} %slice.202) | data formatting | bytes 3145728 | tf_op jit(solution)/shard_map/slice | solution.py:64
  80.4 1.9 %copy.36 = f32[1536,256]{1,0:T(8,128)S(1)} copy(f32[1536,256]{0,1:T(8,128)} %slice.207) | data formatting | bytes 3145728 | tf_op jit(solution)/shard_map/slice | solution.py:64
  82.3 1.6 %fusion.67 = f32[24,64,128]{2,1,0:T(8,128)S(1)} fusion(f32[24,64,256]{2,1,0:T(8,128)S(1)} %bitcast.129, f32[24,256]{1,0:T(8,128)} %get-tuple-element.54, f32[1792,256]{0,1:T(8,128)S(1)} %get-tuple-element.46), kind=kOutput, calls=%fused_computation.68 | convolution fusion | flops 302383104 | bytes 2514944 | tf_op jit(solution)/shard_map/dot_general | solution.py:86
  83.9 1.7 %select_convert_fusion = (bf16[24,64,128]{2,1,0:T(8,128)(2,1)S(1)}, f32[24,64,128]{2,1,0:T(8,128)S(1)}) fusion(f32[24,64,128]{2,1,0:T(8,128)S(1)} %fusion.67, pred[]{:T(512)S(6)} %eq.52, f32[1792,256]{0,1:T(8,128)} %copy-done.1, f32[24,64,256]{2,1,0:T(8,128)S(1)} %bitcast.131, f32[24,256]{1,0:T(8,128)S(1)} %get-tuple-element.55), kind=kOutput, calls=%fused_computation.94 | convolution fusion | flops 302579712 | bytes 3694593 | tf_op jit(solution)/shard_map/dot_general | solution.py:86
  85.7 2.5 %collective-permute-start.2 = (bf16[25,64,128]{2,1,0:T(8,128)(2,1)S(1)}, bf16[25,64,128]{2,1,0:T(8,128)(2,1)S(1)}, u32[]{:S(2)}, u32[]{:S(2)}) collective-permute-start(bf16[25,64,128]{2,1,0:T(8,128)(2,1)S(1)} %pad_maximum_fusion), channel_id=1, source_target_pairs={{0,1},{1,0},{2,3},{3,2},{4,5},{5,4},{6,7},{7,6},{8,9},{9,8},{10,11... | collective-permute-start | bytes 1228808 | tf_op jit(solution)/shard_map/ppermute | solution.py:103
  91.4 3.9 %fusion.6 = f32[24,64,256]{2,1,0:T(8,128)S(1)} fusion(f32[24,64,256]{2,1,0:T(8,128)S(1)} %bitcast.130, f32[24,256]{1,0:T(8,128)S(1)} %copy-done.8, f32[24,256]{1,0:T(8,128)S(1)} %copy-done.16, f32[256,256]{1,0:T(8,128)S(1)} %fusion.102, pred[256,256]{1,0:T(8,128)(4,1)S(1)} %copy-done.11), kind=kOutput, calls=%fused_computation.6 | convolution fusion | flops 610271232 | bytes 3522560 | tf_op jit(solution)/shard_map/dot_general | solution.py:84
  95.3 7.4 %collective-permute-done.3 = bf16[25,64,128]{2,1,0:T(8,128)(2,1)S(1)} collective-permute-done((bf16[25,64,128]{2,1,0:T(8,128)(2,1)S(1)}, bf16[25,64,128]{2,1,0:T(8,128)(2,1)S(1)}, u32[]{:S(2)}, u32[]{:S(2)}) %collective-permute-start.3) | collective-permute-done | bytes 409632 | tf_op jit(solution)/shard_map/ppermute | solution.py:103
  104.7 3.9 %fusion = f32[24,64,256]{2,1,0:T(8,128)S(1)} fusion(f32[24,64,256]{2,1,0:T(8,128)S(1)} %bitcast.132, f32[24,256]{1,0:T(8,128)S(1)} %copy-done.6, f32[24,256]{1,0:T(8,128)S(1)} %copy-done.14, f32[256,256]{1,0:T(8,128)S(1)} %fusion.105, pred[256,256]{1,0:T(8,128)(4,1)S(1)} %copy-done.10), kind=kOutput, calls=%fused_computation | convolution fusion | flops 610271232 | bytes 3522560 | tf_op jit(solution)/shard_map/dot_general | solution.py:84
  108.6 9.3 %collective-permute-done.4 = bf16[25,64,128]{2,1,0:T(8,128)(2,1)S(1)} collective-permute-done((bf16[25,64,128]{2,1,0:T(8,128)(2,1)S(1)}, bf16[25,64,128]{2,1,0:T(8,128)(2,1)S(1)}, u32[]{:S(2)}, u32[]{:S(2)}) %collective-permute-start.4) | collective-permute-done | bytes 409632 | tf_op jit(solution)/shard_map/ppermute | solution.py:103
  119.4 13.8 %collective-permute-done.5 = bf16[25,64,128]{2,1,0:T(8,128)(2,1)S(1)} collective-permute-done((bf16[25,64,128]{2,1,0:T(8,128)(2,1)S(1)}, bf16[25,64,128]{2,1,0:T(8,128)(2,1)S(1)}, u32[]{:S(2)}, u32[]{:S(2)}) %collective-permute-start.5) | collective-permute-done | bytes 409632 | tf_op jit(solution)/shard_map/ppermute | solution.py:103
  133.7 1.8 %fusion.76 = f32[24,64,256]{2,1,0:T(8,128)S(1)} fusion(f32[24]{0:T(128)S(1)} %get-tuple-element.43, f32[24]{0:T(128)S(1)} %mul.372, f32[24]{0:T(128)S(1)} %bitcast.138, bf16[25,64,128]{2,1,0:T(8,128)(2,1)S(1)} %collective-permute-done.5, bf16[25,64,128]{2,1,0:T(8,128)(2,1)S(1)} %collective-permute-done.2, ...), kind=kOutput, calls=%fused_computation.87 | convolution fusion | flops 303988736 | bytes 3409409 | tf_op jit(solution)/shard_map/dot_general | solution.py:199
  135.5 1.6 %multiply_add_fusion = f32[24,64,256]{2,1,0:T(8,128)S(1)} fusion(f32[24,64,256]{2,1,0:T(8,128)S(1)} %fusion.76, f32[24,64,256]{2,1,0:T(8,128)S(1)} %fusion.6, f32[24,64,256]{2,1,0:T(8,128)S(1)} %fusion, bf16[24,64,128]{2,1,0:T(8,128)(2,1)S(1)} %collective-permute-done.6, f32[24,256]{1,0:T(8,128)S(1)} %get-tuple-element.51, ...), kind=kOutput, calls=%fused_computation.66 | convolution fusion | flops 303988736 | bytes 6995969 | tf_op jit(solution)/shard_map/dot_general | solution.py:199
  137.6 1.9 %multiply_reduce_fusion = (f32[256]{0:T(256)S(1)}, f32[1536,256]{0,1:T(8,128)S(1)}) fusion(f32[1536,256]{0,1:T(8,128)S(1)} %copy.40, f32[1536,256]{0,1:T(8,128)} %divide_multiply_fusion.2), kind=kLoop, calls=%fused_computation.65 | loop fusion | flops 1179392 | bytes 4719616 | tf_op jit(solution)/shard_map/reduce_sum | solution.py:204
  139.5 4.7 %fusion.33 = bf16[256,1536]{1,0:T(8,128)(2,1)} fusion(f32[256,1536]{1,0:T(8,128)S(1)} %copy-done.4, bf16[1536,1536]{1,0:T(8,128)(2,1)} %param.27, f32[1536,256]{0,1:T(8,128)S(1)} %get-tuple-element.38, f32[1536]{0:T(1024)S(1)} %copy-done.34, f32[256]{0:T(256)S(1)} %add_rsqrt_fusion), kind=kOutput, calls=%fused_computation.37 | convolution fusion | flops 1209925632 | bytes 8657920 | tf_op jit(solution)/shard_map/dot_general | solution.py:206
  (137 shorter events, 21.1 us)
Async XLA Ops:
  0.0 52.2 %copy-start = (bf16[1536,24]{0,1:T(8,128)(2,1)S(1)}, bf16[1536,24]{0,1:T(8,128)(2,1)}, u32[]{:S(2)}) copy-start(bf16[1536,24]{0,1:T(8,128)(2,1)} %param.21) | copy-start | bytes 221188
  5.8 8.9 %copy-start.27 = (f32[2,1792]{1,0:T(2,128)S(1)}, f32[2,1792]{1,0:T(2,128)}, u32[]{:S(2)}) copy-start(f32[2,1792]{1,0:T(2,128)} %param.23) | copy-start | bytes 43012
  5.8 9.6 %copy-start.12 = (f32[2,4,1792]{2,1,0:T(4,128)S(1)}, f32[2,4,1792]{2,1,0:T(4,128)}, u32[]{:S(2)}) copy-start(f32[2,4,1792]{2,1,0:T(4,128)} %param.22) | copy-start | bytes 172036
  5.8 10.3 %copy-start.31 = (f32[2,24]{1,0:T(2,128)S(1)}, f32[2,24]{1,0:T(2,128)}, u32[]{:S(2)}) copy-start(f32[2,24]{1,0:T(2,128)} %param.24) | copy-start | bytes 580
  5.8 10.3 %copy-start.32 = (f32[2,24]{1,0:T(2,128)S(1)}, f32[2,24]{1,0:T(2,128)}, u32[]{:S(2)}) copy-start(f32[2,24]{1,0:T(2,128)} %param.25) | copy-start | bytes 580
  5.8 41.9 %copy-start.33 = (f32[1536]{0:T(1024)S(1)}, f32[1536]{0:T(1024)}, u32[]{:S(2)}) copy-start(f32[1536]{0:T(1024)} %param.18) | copy-start | bytes 18436
  5.8 41.7 %all-to-all-start = ((bf16[16,32,1664]{2,1,0:T(8,128)(2,1)}), bf16[16,32,1664]{2,1,0:T(8,128)(2,1)S(1)}, u32[]{:S(2)}, u32[]{:S(2)}) async-start(bf16[16,32,1664]{2,1,0:T(8,128)(2,1)} %bitcast.1), calls=%async_computation | async-start | bytes 3407872 | tf_op jit(solution)/shard_map/all_to_all | solution.py:41
  47.7 4.3 %copy-start.28 = (f32[1536]{0:T(1024)S(1)}, f32[1536]{0:T(1024)}, u32[]{:S(2)}) copy-start(f32[1536]{0:T(1024)} %param.19) | copy-start | bytes 18436
  51.9 2.5 %copy-start.3 = (f32[256,1536]{1,0:T(8,128)}, f32[256,1536]{1,0:T(8,128)S(1)}, u32[]{:S(2)}) copy-start(f32[256,1536]{1,0:T(8,128)S(1)} %get-tuple-element.69) | copy-start | bytes 4718596
  55.0 16.9 %slice-start = ((s8[10223616]{0:T(1024)(128)(4,1)}), s8[4194304]{0:T(1024)(128)(4,1)S(1)}, s32[]{:S(2)}) async-start(s8[10223616]{0:T(1024)(128)(4,1)} %bitcast.134), calls=%async_computation.1 | async-start | bytes 8388608
  55.0 16.9 %slice-start.1 = ((s8[10223616]{0:T(1024)(128)(4,1)}), s8[4194304]{0:T(1024)(128)(4,1)S(1)}, s32[]{:S(2)}) async-start(s8[10223616]{0:T(1024)(128)(4,1)} %bitcast.134), calls=%async_computation.2 | async-start | bytes 8388608
  59.3 12.6 %slice-start.2 = ((s8[10223616]{0:T(1024)(128)(4,1)}), s8[1835008]{0:T(1024)(128)(4,1)S(1)}, s32[]{:S(2)}) async-start(s8[10223616]{0:T(1024)(128)(4,1)} %bitcast.134), calls=%async_computation.3 | async-start | bytes 3670016
  64.4 5.0 %collective-permute-start = (bf16[3,1536]{1,0:T(4,128)(2,1)S(1)}, bf16[3,1536]{1,0:T(4,128)(2,1)S(1)}, u32[]{:S(2)}, u32[]{:S(2)}) collective-permute-start(bf16[3,1536]{1,0:T(4,128)(2,1)S(1)} %get-tuple-element.48), channel_id=1, source_target_pairs={{0,1},{1,2},{2,3},{3,4},{4,5},{5,6},{6,7},{7,8},{8,9},{9,10},{10,1... | collective-permute-start | bytes 27656 | tf_op jit(solution)/shard_map/ppermute | solution.py:54
  67.3 4.6 %collective-permute-start.1 = (bf16[3,1536]{1,0:T(4,128)(2,1)S(1)}, bf16[3,1536]{1,0:T(4,128)(2,1)S(1)}, u32[]{:S(2)}, u32[]{:S(2)}) collective-permute-start(bf16[3,1536]{1,0:T(4,128)(2,1)S(1)} %get-tuple-element.49), channel_id=1, source_target_pairs={{1,0},{2,1},{3,2},{4,3},{5,4},{6,5},{7,6},{8,7},{9,8},{10,9},{11,1... | collective-permute-start | bytes 27656 | tf_op jit(solution)/shard_map/ppermute | solution.py:55
  85.6 4.2 %copy-start.30 = (f32[24]{0:T(128)S(1)}, f32[24]{0:T(128)}, u32[]{:S(2)}) copy-start(f32[24]{0:T(128)} %get-tuple-element.32) | copy-start | bytes 292
  85.6 4.2 %copy-start.29 = (f32[24]{0:T(128)S(1)}, f32[24]{0:T(128)}, u32[]{:S(2)}) copy-start(f32[24]{0:T(128)} %broadcast_select_fusion.1) | copy-start | bytes 292
  85.7 4.1 %collective-permute-start.2 = (bf16[25,64,128]{2,1,0:T(8,128)(2,1)S(1)}, bf16[25,64,128]{2,1,0:T(8,128)(2,1)S(1)}, u32[]{:S(2)}, u32[]{:S(2)}) collective-permute-start(bf16[25,64,128]{2,1,0:T(8,128)(2,1)S(1)} %pad_maximum_fusion), channel_id=1, source_target_pairs={{0,1},{1,0},{2,3},{3,2},{4,5},{5,4},{6,7},{7,6},{8,9},{9,8},{10,11... | collective-permute-start | bytes 1228808 | tf_op jit(solution)/shard_map/ppermute | solution.py:103
  90.1 12.6 %collective-permute-start.3 = (bf16[25,64,128]{2,1,0:T(8,128)(2,1)S(1)}, bf16[25,64,128]{2,1,0:T(8,128)(2,1)S(1)}, u32[]{:S(2)}, u32[]{:S(2)}) collective-permute-start(bf16[25,64,128]{2,1,0:T(8,128)(2,1)S(1)} %pad_maximum_fusion.1), channel_id=1, source_target_pairs={{1,3},{3,5},{5,7},{7,9},{9,11},{11,13},{13,15},{2,0},{4,2},{6,4},{... | collective-permute-start | bytes 1228808 | tf_op jit(solution)/shard_map/ppermute | solution.py:103
  102.7 2.0 %copy-start.6 = (f32[24,256]{1,0:T(8,128)S(1)}, f32[24,256]{1,0:T(8,128)}, u32[]{:S(2)}) copy-start(f32[24,256]{1,0:T(8,128)} %copy-done.5) | copy-start | bytes 73732
  102.7 2.0 %copy-start.10 = (pred[256,256]{1,0:T(8,128)(4,1)S(1)}, pred[256,256]{1,0:T(8,128)(4,1)}, u32[]{:S(2)}) copy-start(pred[256,256]{1,0:T(8,128)(4,1)} %iota_compare_fusion.8) | copy-start | bytes 196612
  102.7 2.0 %copy-start.14 = (f32[24,256]{1,0:T(8,128)S(1)}, f32[24,256]{1,0:T(8,128)}, u32[]{:S(2)}) copy-start(f32[24,256]{1,0:T(8,128)} %copy-done.13) | copy-start | bytes 73732
  103.1 14.7 %collective-permute-start.4 = (bf16[25,64,128]{2,1,0:T(8,128)(2,1)S(1)}, bf16[25,64,128]{2,1,0:T(8,128)(2,1)S(1)}, u32[]{:S(2)}, u32[]{:S(2)}) collective-permute-start(bf16[25,64,128]{2,1,0:T(8,128)(2,1)S(1)} %pad_maximum_fusion.2), channel_id=1, source_target_pairs={{1,5},{3,7},{5,9},{7,11},{9,13},{11,15},{4,0},{6,2},{8,4},{10,6},{... | collective-permute-start | bytes 1228808 | tf_op jit(solution)/shard_map/ppermute | solution.py:103
  118.1 15.1 %collective-permute-start.5 = (bf16[25,64,128]{2,1,0:T(8,128)(2,1)S(1)}, bf16[25,64,128]{2,1,0:T(8,128)(2,1)S(1)}, u32[]{:S(2)}, u32[]{:S(2)}) collective-permute-start(bf16[25,64,128]{2,1,0:T(8,128)(2,1)S(1)} %pad_maximum_fusion.3), channel_id=1, source_target_pairs={{1,9},{3,11},{5,13},{7,15},{8,0},{10,2},{12,4},{14,6},{17,25},{19,... | collective-permute-start | bytes 1228808 | tf_op jit(solution)/shard_map/ppermute | solution.py:103
  133.6 1.9 %collective-permute-start.6 = (bf16[24,64,128]{2,1,0:T(8,128)(2,1)S(1)}, bf16[24,64,128]{2,1,0:T(8,128)(2,1)S(1)}, u32[]{:S(2)}, u32[]{:S(2)}) collective-permute-start(bf16[24,64,128]{2,1,0:T(8,128)(2,1)S(1)} %fusion.85), channel_id=1, source_target_pairs={{0,1},{1,0},{2,3},{3,2},{4,5},{5,4},{6,7},{7,6},{8,9},{9,8},{10,11... | collective-permute-start | bytes 1179656 | tf_op jit(solution)/shard_map/ppermute | solution.py:133
  (22 other events, 28.7 us)
